TPU v7x, 32 devices: a whole 2x2x4 slice. The times are simulated.
32 devices in a mesh: dp: 8 (over y, x, core), expert: 4 (over z).
Axes of the slice: x: 2, y: 2, z: 4, core: 2. Of those that a mesh axis runs over, the one named last changes fastest.
Arguments:
- hidden: bfloat16 [2, 512, 2880], P(None, ('dp', 'expert')), may hold values from -1.5 to 1.5
- norm_gain: float32 [2880], replicated, may hold values from 0.1 to 1.9
- router: bfloat16 [2880, 64], replicated, may hold values from -0.078125 to 0.078125
- routes: int32 [2, 512, 4], P(None, ('dp', 'expert')), may hold values from 0 to 63, all different within a row; in each aligned block of 16 rows (0 to 15, 16 to 31, ..., all dimensions but the last counted through in order) at most 2 rows name the same one
- w_gate: bfloat16 [64, 2880, 2048], P('expert', None, 'dp'), may hold values from -0.109375 to 0.109375
- w_up: bfloat16 [64, 2880, 2048], P('expert', None, 'dp'), may hold values from -0.109375 to 0.109375
- w_down: bfloat16 [64, 2048, 2880], P('expert', 'dp'), may hold values from -0.125 to 0.125
- queries: bfloat16 [2, 512, 4096], P(None, ('dp', 'expert')), may hold values from -5.5 to 5.5
- new_key: bfloat16 [2, 512, 512], P(None, ('dp', 'expert')), may hold values from -8 to 8
- new_value: bfloat16 [2, 512, 512], P(None, ('dp', 'expert')), may hold values from -6 to 6
- key_pages: bfloat16 [256, 4, 16, 512], P(('dp', 'expert')), may hold values from -6 to 6
- value_pages: bfloat16 [256, 4, 16, 512], P(('dp', 'expert')), may hold values from -6 to 6
- page_counts: int32 [32, 16], P(('dp', 'expert')), may hold values from 1 to 10, 32 in all within a row
- page_order: int32 [32, 32], P(('dp', 'expert')), may hold values from 0 to 31, each once within a row
Outputs:
- context: bfloat16 [2, 512, 4096], P(None, ('dp', 'expert'))
- layer_out: bfloat16 [2, 512, 2880], P(None, ('dp', 'expert'))
Inputs may be any that keep to these rules, and one draw needn't show every extreme that they name: `routes`: in each step, the 16 rows of one aligned block name each expert at most 2 times, and some block names some expert exactly 2 times. `page_counts`: each block's counts sum to 32, and the largest count of a block is exactly 10. Each row of page_order is a permutation of 0 to 31.
All inputs are finite; a program needn't handle non-finite values.
Results may differ from a plain program's by a relative error of at most 0.0095.
Values may be sent and summed in bfloat16 or wider, within the bound.
No kernel may reach another device: no remote copies, remote signals or barrier semaphores. Data moves between devices by JAX's collectives and lax.ppermute only.
A program may use at most 192 MiB of HBM per device.

v0:
```python
import jax
import jax.numpy as jnp
from jax import lax
from jax.sharding import PartitionSpec as P

HEADS = 64
KV_HEADS = 8
HEAD_DIM = 64
EXPERTS = 64
MOST = 2
STEPS = 2
BLOCK = 16


def page_layout(counts, page_perm, most_pages):
    starts = jnp.cumsum(counts) - counts
    offsets = jnp.arange(most_pages, dtype=jnp.int32)
    places = starts[:, None] + offsets[None, :]
    places = jnp.where(offsets[None, :] < counts[:, None], places, 0)
    return jnp.take(page_perm, places, axis=0)


def attention(query_rows, fresh_keys, fresh_values, space_keys, space_values, counts, page_perm):
    group_size = HEADS // KV_HEADS
    most_pages = page_perm.shape[0] // 3
    row_count = counts.shape[0]
    cache_span = most_pages * BLOCK
    slot_ids = page_layout(counts, page_perm, most_pages).reshape(-1)
    cache_keys = jnp.take(space_keys, slot_ids, axis=0).reshape(
        row_count, cache_span, KV_HEADS, HEAD_DIM
    )
    cache_values = jnp.take(space_values, slot_ids, axis=0).reshape(
        row_count, cache_span, KV_HEADS, HEAD_DIM
    )
    live_mask = jnp.arange(cache_span)[None, :] < (counts * BLOCK)[:, None]
    query_heads = query_rows.reshape(STEPS, row_count, KV_HEADS, group_size, HEAD_DIM)
    new_keys = fresh_keys.reshape(STEPS, row_count, KV_HEADS, HEAD_DIM)
    new_values = fresh_values.reshape(STEPS, row_count, KV_HEADS, HEAD_DIM)
    score_scale = HEAD_DIM ** (-0.5)
    old_scores = (
        jnp.einsum("trkgh,rlkh->trkgl", query_heads, cache_keys, preferred_element_type=jnp.float32)
        * score_scale
    )
    old_scores = jnp.where(live_mask[None, :, None, None, :], old_scores, -jnp.inf)
    new_scores = (
        jnp.einsum("trkgh,urkh->trkgu", query_heads, new_keys, preferred_element_type=jnp.float32)
        * score_scale
    )
    causal = jnp.arange(STEPS)[None, :] <= jnp.arange(STEPS)[:, None]
    new_scores = jnp.where(causal[:, None, None, None, :], new_scores, -jnp.inf)
    row_max = jnp.maximum(jnp.max(old_scores, axis=-1), jnp.max(new_scores, axis=-1))
    old_probs = jnp.exp(old_scores - row_max[..., None])
    new_probs = jnp.exp(new_scores - row_max[..., None])
    denominator = jnp.sum(old_probs, axis=-1) + jnp.sum(new_probs, axis=-1)
    numerator = jnp.einsum(
        "trkgl,rlkh->trkgh",
        old_probs.astype(jnp.bfloat16),
        cache_values,
        preferred_element_type=jnp.float32,
    )
    numerator = numerator + jnp.einsum(
        "trkgu,urkh->trkgh",
        new_probs.astype(jnp.bfloat16),
        new_values,
        preferred_element_type=jnp.float32,
    )
    result = numerator / denominator[..., None]
    return result.reshape(STEPS, row_count, HEADS * HEAD_DIM).astype(jnp.bfloat16)


def route_tables(expert_ids, gate_vals):
    numbers = jnp.arange(EXPERTS, dtype=jnp.int32)
    picked = (expert_ids[..., None] == numbers).astype(jnp.int32)
    per_row = jnp.sum(picked, axis=2)
    earlier = jnp.cumsum(per_row, axis=1) - per_row
    rank_vals = jnp.sum(picked * earlier[:, :, None, :], axis=3)
    targets = expert_ids * MOST + rank_vals
    places = jnp.arange(EXPERTS * MOST, dtype=jnp.int32)
    matches = targets[..., None] == places
    sender = jnp.any(matches, axis=2).astype(jnp.bfloat16)
    weights = jnp.sum(
        jnp.where(matches, gate_vals[..., None].astype(jnp.float32), 0.0), axis=2
    ).astype(jnp.bfloat16)
    return (sender, weights)


def expert_block(slot_rows, w_gate, w_up, w_down):
    gate_part = jnp.einsum(
        "pkxmd,xdf->pkxmf", slot_rows, w_gate, preferred_element_type=jnp.float32
    )
    up_part = jnp.einsum("pkxmd,xdf->pkxmf", slot_rows, w_up, preferred_element_type=jnp.float32)
    hidden_act = ((up_part + 1.0) * gate_part * jax.nn.sigmoid(1.702 * gate_part)).astype(
        jnp.bfloat16
    )
    return jnp.einsum(
        "pkxmf,xfd->pkxmd", hidden_act, w_down, preferred_element_type=jnp.float32
    ).astype(jnp.bfloat16)


def moe_step(hidden_rows, norm_gain, router, expert_ids, w_gate, w_up, w_down):
    residual = hidden_rows.astype(jnp.float32)
    scale_rows = lax.rsqrt(jnp.mean(residual * residual, axis=1, keepdims=True) + 1e-05)
    normed = (residual * scale_rows * norm_gain).astype(jnp.bfloat16)
    logit_rows = jnp.dot(normed, router, preferred_element_type=jnp.float32)
    numbers = jnp.arange(EXPERTS, dtype=jnp.int32)
    chosen = jnp.sum(
        jnp.where(expert_ids[..., None] == numbers, logit_rows[:, None, :], 0.0), axis=-1
    )
    spreads = chosen[:, None, :] - chosen[:, :, None]
    gate_vals = (1.0 / jnp.sum(jnp.exp(spreads), axis=2)).astype(jnp.bfloat16)
    model_width = residual.shape[1]
    columns = lax.axis_size("expert")
    local_experts = w_gate.shape[0]
    group_rows, group_ids, group_gates = (
        lax.all_gather(normed[None], "dp", axis=0, tiled=True),
        lax.all_gather(expert_ids.astype(jnp.bfloat16)[None], "dp", axis=0, tiled=True),
        lax.all_gather(gate_vals[None], "dp", axis=0, tiled=True),
    )
    sender, weights = route_tables(group_ids.astype(jnp.int32), group_gates)
    packed = jnp.einsum(
        "prs,prd->psd", sender, group_rows, preferred_element_type=jnp.float32
    ).astype(jnp.bfloat16)
    packed = packed.reshape(packed.shape[0], columns, local_experts, MOST, model_width)
    partial_out = expert_block(
        lax.all_to_all(packed, "expert", split_axis=1, concat_axis=1, tiled=True),
        w_gate,
        w_up,
        w_down,
    )
    returned = lax.all_to_all(partial_out, "expert", split_axis=1, concat_axis=1, tiled=True)
    returned = returned.reshape(returned.shape[0], EXPERTS * MOST, model_width)
    row_terms = jnp.einsum("prs,psd->prd", weights, returned, preferred_element_type=jnp.float32)
    branch_out = lax.psum_scatter(row_terms, "dp", scatter_dimension=0, tiled=True)[0]
    return (residual + branch_out).astype(jnp.bfloat16)


def body(
    hidden,
    norm_gain,
    router,
    routes,
    w_gate,
    w_up,
    w_down,
    queries,
    new_key,
    new_value,
    key_pages,
    value_pages,
    page_counts,
    page_order,
):
    host_keys, host_values = (
        lax.all_to_all(key_pages, "dp", split_axis=0, concat_axis=0, tiled=True),
        lax.all_to_all(value_pages, "dp", split_axis=0, concat_axis=0, tiled=True),
    )
    kv_width = KV_HEADS * HEAD_DIM
    space_keys = host_keys.reshape(-1, BLOCK, kv_width)
    space_values = host_values.reshape(-1, BLOCK, kv_width)
    context = attention(
        queries, new_key, new_value, space_keys, space_values, page_counts[0], page_order[0]
    )
    outputs = []
    for step_index in range(STEPS):
        outputs.append(
            moe_step(
                hidden[step_index], norm_gain, router, routes[step_index], w_gate, w_up, w_down
            )
        )
    return (context, jnp.stack(outputs))


def solution(mesh):
    return jax.shard_map(
        body,
        mesh=mesh,
        in_specs=(
            P(None, ("dp", "expert"), None),
            P(),
            P(),
            P(None, ("dp", "expert"), None),
            P("expert", None, "dp"),
            P("expert", None, "dp"),
            P("expert", "dp", None),
            P(None, ("dp", "expert"), None),
            P(None, ("dp", "expert"), None),
            P(None, ("dp", "expert"), None),
            P(("dp", "expert"), None, None, None),
            P(("dp", "expert"), None, None, None),
            P(("dp", "expert"), None),
            P(("dp", "expert"), None),
        ),
        out_specs=(P(None, ("dp", "expert"), None), P(None, ("dp", "expert"), None)),
        check_vma=False,
    )
```

profile of v0, /device:TPU:0, one launch (start us, length us, event | category | flops | bytes accessed | tf_op | source)
XLA Modules:
  0.0 657.5 jit_solution(8892093810396671834)
XLA Ops:
  13.2 12.1 %all_gather.18 = bf16[8,16,4]{1,2,0:T(4,128)(2,1)S(1)} all-gather(bf16[1,16,4]{1,2,0:T(4,128)(2,1)S(1)} %get-tuple-element.14), channel_id=1, replica_groups=mesh['dp'=8,'expert'=4] {'dp'}, dimensions={0}, use_global_device_ids=true | all-gather | bytes 1152 | tf_op jit(solution)/shard_map/all_gather | solution.py:116
  28.4 9.4 %all_gather.20 = bf16[8,16,2880]{2,1,0:T(8,128)(2,1)S(1)} all-gather(bf16[1,16,2880]{2,1,0:T(8,128)(2,1)S(1)} %get-tuple-element.7), channel_id=1, replica_groups=mesh['dp'=8,'expert'=4] {'dp'}, dimensions={0}, use_global_device_ids=true | all-gather | bytes 829440 | tf_op jit(solution)/shard_map/all_gather | solution.py:115
  45.5 8.8 %copy.98 = bf16[8,128,2880]{2,0,1:T(8,128)(2,1)} copy(bf16[8,128,2880]{1,2,0:T(8,128)(2,1)} %convolution_convert_fusion.1) | data formatting | bytes 11796480 | tf_op jit(solution)/shard_map/convert_element_type | solution.py:122
  59.5 9.3 %all_gather.21 = bf16[8,16,4]{1,2,0:T(4,128)(2,1)S(1)} all-gather(bf16[1,16,4]{1,2,0:T(4,128)(2,1)S(1)} %get-tuple-element.13), channel_id=1, replica_groups=mesh['dp'=8,'expert'=4] {'dp'}, dimensions={0}, use_global_device_ids=true | all-gather | bytes 1152 | tf_op jit(solution)/shard_map/all_gather | solution.py:116
  69.9 10.4 %all_gather.23 = bf16[8,16,2880]{2,1,0:T(8,128)(2,1)S(1)} all-gather(bf16[1,16,2880]{2,1,0:T(8,128)(2,1)S(1)} %get-tuple-element.8), channel_id=1, replica_groups=mesh['dp'=8,'expert'=4] {'dp'}, dimensions={0}, use_global_device_ids=true | all-gather | bytes 829440 | tf_op jit(solution)/shard_map/all_gather | solution.py:115
  84.2 8.8 %copy.106 = bf16[8,128,2880]{2,0,1:T(8,128)(2,1)} copy(bf16[8,128,2880]{1,2,0:T(8,128)(2,1)} %convolution_convert_fusion) | data formatting | bytes 11796480 | tf_op jit(solution)/shard_map/convert_element_type | solution.py:122
  93.1 99.8 %all-to-all-done.2 = bf16[8,4,16,2,2880]{4,0,3,2,1:T(8,128)(2,1)} async-done(((bf16[8,4,16,2,2880]{4,0,3,2,1:T(8,128)(2,1)}), bf16[8,4,16,2,2880]{4,0,3,2,1:T(8,128)(2,1)}, u32[]{:S(2)}, u32[]{:S(2)}) %all-to-all-start.2) | async-done | bytes 5898272 | tf_op jit(solution)/shard_map/all_to_all | solution.py:125
  192.9 5.7 all-to-all-start.4
  198.6 13.3 %fusion.6 = f32[16,8,4,2,256]{4,1,3,2,0:T(8,128)S(1)} fusion(bf16[16,2880,256]{2,1,0:T(8,128)(2,1)} %param.20, bf16[8,4,16,2,2880]{4,0,3,2,1:T(8,128)(2,1)} %all-to-all-done.2), kind=kOutput, calls=%fused_computation.9 | convolution fusion | flops 1509949440 | bytes 30539776 | tf_op jit(solution)/shard_map/pkxmd,xdf->pkxmf/dot_general | solution.py:88
  211.9 13.3 %fusion.77 = bf16[8,4,16,2,256]{4,0,3,1,2:T(8,128)(2,1)S(1)} fusion(f32[16,8,4,2,256]{4,1,3,2,0:T(8,128)S(1)} %fusion.6, bf16[16,2880,256]{2,1,0:T(8,128)(2,1)} %param.21, bf16[8,4,16,2,2880]{4,0,3,2,1:T(8,128)(2,1)} %all-to-all-done.2), kind=kOutput, calls=%fused_computation.52 | convolution fusion | flops 1512046592 | bytes 31064064 | tf_op jit(solution)/shard_map/pkxmd,xdf->pkxmf/dot_general | solution.py:91
  225.2 12.9 %convert_bitcast_fusion.1 = bf16[8,4,16,2,2880]{4,0,3,1,2:T(8,128)(2,1)} fusion(bf16[8,4,16,2,256]{4,0,3,1,2:T(8,128)(2,1)S(1)} %fusion.77, bf16[16,256,2880]{1,2,0:T(8,128)(2,1)} %param.22), kind=kOutput, calls=%fused_computation.20 | convolution fusion | flops 1512898560 | bytes 30015488 | tf_op jit(solution)/shard_map/pkxmf,xfd->pkxmd/dot_general | solution.py:95
  238.1 5.7 copy.101
  243.8 87.4 %all-to-all-done.4 = bf16[8,4,16,2,2880]{4,0,3,2,1:T(8,128)(2,1)} async-done(((bf16[8,4,16,2,2880]{4,0,3,2,1:T(8,128)(2,1)}), bf16[8,4,16,2,2880]{4,0,3,2,1:T(8,128)(2,1)}, u32[]{:S(2)}, u32[]{:S(2)}) %all-to-all-start.4) | async-done | bytes 5898272 | tf_op jit(solution)/shard_map/all_to_all | solution.py:125
  336.7 13.3 %fusion.4 = f32[16,8,4,2,256]{4,1,3,2,0:T(8,128)S(1)} fusion(bf16[16,2880,256]{2,1,0:T(8,128)(2,1)} %param.20, bf16[8,4,16,2,2880]{4,0,3,2,1:T(8,128)(2,1)} %all-to-all-done.4), kind=kOutput, calls=%fused_computation.7 | convolution fusion | flops 1509949440 | bytes 30539776 | tf_op jit(solution)/shard_map/pkxmd,xdf->pkxmf/dot_general | solution.py:88
  350.0 13.3 %fusion.82 = bf16[8,4,16,2,256]{4,0,3,1,2:T(8,128)(2,1)S(1)} fusion(f32[16,8,4,2,256]{4,1,3,2,0:T(8,128)S(1)} %fusion.4, bf16[16,2880,256]{2,1,0:T(8,128)(2,1)} %param.21, bf16[8,4,16,2,2880]{4,0,3,2,1:T(8,128)(2,1)} %all-to-all-done.4), kind=kOutput, calls=%fused_computation.53 | convolution fusion | flops 1512046592 | bytes 31064064 | tf_op jit(solution)/shard_map/pkxmd,xdf->pkxmf/dot_general | solution.py:91
  363.2 12.9 %convert_bitcast_fusion = bf16[8,4,16,2,2880]{4,0,3,1,2:T(8,128)(2,1)} fusion(bf16[8,4,16,2,256]{4,0,3,1,2:T(8,128)(2,1)S(1)} %fusion.82, bf16[16,256,2880]{1,2,0:T(8,128)(2,1)} %param.22), kind=kOutput, calls=%fused_computation.19 | convolution fusion | flops 1512898560 | bytes 30015488 | tf_op jit(solution)/shard_map/pkxmf,xfd->pkxmd/dot_general | solution.py:95
  376.1 5.7 copy.109
  381.8 86.9 %all-to-all-done.3 = bf16[8,4,16,2,2880]{4,0,3,2,1:T(8,128)(2,1)} async-done(((bf16[8,4,16,2,2880]{4,0,3,2,1:T(8,128)(2,1)}), bf16[8,4,16,2,2880]{4,0,3,2,1:T(8,128)(2,1)}, u32[]{:S(2)}, u32[]{:S(2)}) %all-to-all-start.3) | async-done | bytes 5898272 | tf_op jit(solution)/shard_map/all_to_all | solution.py:130
  474.8 8.7 %all-gather.2 = bf16[8,16,4]{1,2,0:T(4,128)(2,1)S(1)} all-gather(bf16[1,16,4]{1,2,0:T(4,128)(2,1)S(1)} %fusion.134), channel_id=2, replica_groups=mesh['dp'=8,'expert'=4] {'dp'}, dimensions={0}, use_global_device_ids=true | all-gather | bytes 1152 | tf_op jit(solution)/shard_map/all_gather | solution.py:117
  489.4 9.1 %all-gather.3 = bf16[8,16,4]{1,2,0:T(4,128)(2,1)S(1)} all-gather(bf16[1,16,4]{1,2,0:T(4,128)(2,1)S(1)} %fusion.135), channel_id=3, replica_groups=mesh['dp'=8,'expert'=4] {'dp'}, dimensions={0}, use_global_device_ids=true | all-gather | bytes 1152 | tf_op jit(solution)/shard_map/all_gather | solution.py:117
  510.1 95.9 %all-to-all-done.5 = bf16[8,4,16,2,2880]{4,0,3,2,1:T(8,128)(2,1)} async-done(((bf16[8,4,16,2,2880]{4,0,3,2,1:T(8,128)(2,1)}), bf16[8,4,16,2,2880]{4,0,3,2,1:T(8,128)(2,1)}, u32[]{:S(2)}, u32[]{:S(2)}) %all-to-all-start.5) | async-done | bytes 5898272 | tf_op jit(solution)/shard_map/all_to_all | solution.py:130
  615.5 7.7 %reshape.331 = bf16[16,160,8,64]{3,2,1,0:T(8,128)(2,1)} reshape(bf16[160,16,512]{2,1,0:T(8,128)(2,1)} %get-tuple-element.17) | data formatting | bytes 5242880 | tf_op jit(solution)/shard_map/reshape | solution.py:29
  628.1 5.7 bitcast_reduce_fusion
  639.0 9.7 %reduce-scatter.5.cloned.1.call-done = f32[1,16,2880]{2,1,0:T(8,128)} async-done(((f32[8,16,2880]{2,1,0:T(8,128)}), f32[1,16,2880]{2,1,0:T(8,128)}) %reduce-scatter.5.cloned.1.call-update) | async-done | bytes 184336 | tf_op jit(solution)/shard_map/reduce_scatter | solution.py:133
  (108 shorter events, 77.1 us)
Async XLA Ops:
  7.2 466.9 %copy-start = (bf16[2880,64]{0,1:T(8,128)(2,1)S(1)}, bf16[2880,64]{0,1:T(8,128)(2,1)}, u32[]{:S(2)}) copy-start(bf16[2880,64]{0,1:T(8,128)(2,1)} %param.18) | copy-start | bytes 1105924
  7.2 30.6 %all-to-all-start = ((bf16[8,4,16,512]{3,2,1,0:T(8,128)(2,1)}), bf16[8,4,16,512]{3,2,1,0:T(8,128)(2,1)S(1)}, u32[]{:S(2)}, u32[]{:S(2)}) async-start(bf16[8,4,16,512]{3,2,1,0:T(8,128)(2,1)} %param.27), calls=%async_computation | async-start | bytes 1048576 | tf_op jit(solution)/shard_map/all_to_all | solution.py:155
  37.8 16.4 %all-to-all-start.1 = ((bf16[8,4,16,512]{3,2,1,0:T(8,128)(2,1)}), bf16[8,4,16,512]{3,2,1,0:T(8,128)(2,1)S(1)}, u32[]{:S(2)}, u32[]{:S(2)}) async-start(bf16[8,4,16,512]{3,2,1,0:T(8,128)(2,1)} %param.26), calls=%async_computation.1 | async-start | bytes 1048576 | tf_op jit(solution)/shard_map/all_to_all | solution.py:154
  54.3 138.6 %all-to-all-start.2 = ((bf16[8,4,16,2,2880]{4,0,3,2,1:T(8,128)(2,1)}), bf16[8,4,16,2,2880]{4,0,3,2,1:T(8,128)(2,1)}, u32[]{:S(2)}, u32[]{:S(2)}) async-start(bf16[8,4,16,2,2880]{4,0,3,2,1:T(8,128)(2,1)} %bitcast.145), calls=%async_computation.2 | async-start | bytes 12058624 | tf_op jit(solution)/shard_map/all_to_all | solution.py:125
  192.9 138.3 %all-to-all-start.4 = ((bf16[8,4,16,2,2880]{4,0,3,2,1:T(8,128)(2,1)}), bf16[8,4,16,2,2880]{4,0,3,2,1:T(8,128)(2,1)}, u32[]{:S(2)}, u32[]{:S(2)}) async-start(bf16[8,4,16,2,2880]{4,0,3,2,1:T(8,128)(2,1)} %bitcast.146), calls=%async_computation.5 | async-start | bytes 12058624 | tf_op jit(solution)/shard_map/all_to_all | solution.py:125
  331.2 137.5 %all-to-all-start.3 = ((bf16[8,4,16,2,2880]{4,0,3,2,1:T(8,128)(2,1)}), bf16[8,4,16,2,2880]{4,0,3,2,1:T(8,128)(2,1)}, u32[]{:S(2)}, u32[]{:S(2)}) async-start(bf16[8,4,16,2,2880]{4,0,3,2,1:T(8,128)(2,1)} %copy.101), calls=%async_computation.3 | async-start | bytes 12058624 | tf_op jit(solution)/shard_map/all_to_all | solution.py:130
  381.8 92.2 %copy-start.5 = (bf16[2,16,2880]{2,1,0:T(8,128)(2,1)S(1)}, bf16[2,16,2880]{2,1,0:T(8,128)(2,1)}, u32[]{:S(2)}) copy-start(bf16[2,16,2880]{2,1,0:T(8,128)(2,1)} %param.16) | copy-start | bytes 552964
  381.8 92.2 %copy-start.9 = (f32[2880]{0:T(1024)S(1)}, f32[2880]{0:T(1024)}, u32[]{:S(2)}) copy-start(f32[2880]{0:T(1024)} %param.17) | copy-start | bytes 34564
  468.7 137.2 %all-to-all-start.5 = ((bf16[8,4,16,2,2880]{4,0,3,2,1:T(8,128)(2,1)}), bf16[8,4,16,2,2880]{4,0,3,2,1:T(8,128)(2,1)}, u32[]{:S(2)}, u32[]{:S(2)}) async-start(bf16[8,4,16,2,2880]{4,0,3,2,1:T(8,128)(2,1)} %copy.109), calls=%async_computation.6 | async-start | bytes 12058624 | tf_op jit(solution)/shard_map/all_to_all | solution.py:130
  473.9 24.5 %copy-start.12 = (s32[1,16]{1,0:T(1,128)S(1)}, s32[1,16]{1,0:T(1,128)}, u32[]{:S(2)}) copy-start(s32[1,16]{1,0:T(1,128)} %param.28) | copy-start | bytes 196
  473.9 25.4 %copy-start.7 = (bf16[2,16,4096]{2,1,0:T(8,128)(2,1)S(1)}, bf16[2,16,4096]{2,1,0:T(8,128)(2,1)}, u32[]{:S(2)}) copy-start(bf16[2,16,4096]{2,1,0:T(8,128)(2,1)} %param.23) | copy-start | bytes 786436
  473.9 25.9 %copy-start.10 = (bf16[2,16,512]{2,1,0:T(8,128)(2,1)S(1)}, bf16[2,16,512]{2,1,0:T(8,128)(2,1)}, u32[]{:S(2)}) copy-start(bf16[2,16,512]{2,1,0:T(8,128)(2,1)} %param.24) | copy-start | bytes 98308
  473.9 26.0 %copy-start.11 = (bf16[2,16,512]{2,1,0:T(8,128)(2,1)S(1)}, bf16[2,16,512]{2,1,0:T(8,128)(2,1)}, u32[]{:S(2)}) copy-start(bf16[2,16,512]{2,1,0:T(8,128)(2,1)} %param.25) | copy-start | bytes 98308
  474.0 26.1 %copy-start.1 = (s32[1,32]{1,0:T(1,128)S(1)}, s32[1,32]{1,0:T(1,128)}, u32[]{:S(2)}) copy-start(s32[1,32]{1,0:T(1,128)} %param.29) | copy-start | bytes 388
  474.0 165.0 %reduce-scatter.3.cloned.1.call-start = ((), (), s32[]{:S(2)}) async-start(), calls=%async_computation.8 | async-start | bytes 1695744 | tf_op jit(solution)/shard_map/reduce_scatter | solution.py:133
  489.3 159.4 %reduce-scatter.5.cloned.1.call-start = ((), (), s32[]{:S(2)}) async-start(), calls=%async_computation.9 | async-start | bytes 1695744 | tf_op jit(solution)/shard_map/reduce_scatter | solution.py:133
  499.8 7.7 %copy-start.6 = (bf16[2,16,8,8,64]{4,3,2,1,0:T(8,128)(2,1)}, bf16[2,16,8,8,64]{4,3,2,1,0:T(8,128)(2,1)S(1)}, u32[]{:S(2)}) copy-start(bf16[2,16,8,8,64]{4,3,2,1,0:T(8,128)(2,1)S(1)} %reshape.332) | copy-start | bytes 786436
  510.1 101.4 %copy-start.2 = (bf16[160,16,512]{2,1,0:T(8,128)(2,1)S(1)}, bf16[160,16,512]{2,1,0:T(8,128)(2,1)}, u32[]{:S(2)}) copy-start(bf16[160,16,512]{2,1,0:T(8,128)(2,1)} %gather_fusion.1) | copy-start | bytes 7864324
  615.5 7.7 %copy-start.3 = (bf16[160,16,512]{2,1,0:T(8,128)(2,1)S(1)}, bf16[160,16,512]{2,1,0:T(8,128)(2,1)}, u32[]{:S(2)}) copy-start(bf16[160,16,512]{2,1,0:T(8,128)(2,1)} %get-tuple-element.18) | copy-start | bytes 7864324
  628.1 5.8 copy-start.8
  628.1 7.5 %copy-start.4 = (bf16[16,160,8,64]{3,2,1,0:T(8,128)(2,1)S(1)}, bf16[16,160,8,64]{3,2,1,0:T(8,128)(2,1)}, u32[]{:S(2)}) copy-start(bf16[16,160,8,64]{3,2,1,0:T(8,128)(2,1)} %reshape.329) | copy-start | bytes 7864324
Sparse Core Ops, SparseCore 0:
  489.4 38.6 reduce-scatter.2
  611.5 37.0 reduce-scatter.4
where the time goes:
time: 665 us; the launch traced here: 658 us
  waiting for transfers between devices  380 us (57%)
  matrix products  109 us (16%)
  blocking collectives  58.9 us (9%)
  local copies, waits for them, and re-layouts  50.8 us (8%)
  starting transfers between devices  30.5 us (5%)
  between operations  14.8 us (2%)
  other arithmetic  13.5 us (2%)
    all_to_all x2, waiting for transfers between devices, moe_step(): lax.all_to_all(packed, 'expert', split_axis=1, concat_axis=1, tiled=True)  187 us
    all_to_all x2, waiting for transfers between devices, moe_step(): lax.all_to_all(partial_out, 'expert', split_axis=1, concat_axis=1, tiled=...  183 us
    dot_general x2, matrix products, expert_block(): jnp.einsum('pkxmd,xdf->pkxmf', slot_rows, w_gate, preferred_element_type=...  26.6 us
    dot_general x2, matrix products, expert_block(): jnp.einsum('pkxmd,xdf->pkxmf', slot_rows, w_up, preferred_element_type=jn...  26.5 us
    dot_general x2, matrix products, expert_block(): jnp.einsum('pkxmf,xfd->pkxmd', hidden_act, w_down, preferred_element_type...  25.7 us
    all_gather x2, blocking collectives, moe_step(): lax.all_gather(expert_ids.astype(jnp.bfloat16)[None], 'dp', axis=0, tiled...  21.4 us
    all_gather x2, blocking collectives, moe_step(): lax.all_gather(normed[None], 'dp', axis=0, tiled=True)  19.7 us
    all_gather x2, blocking collectives, moe_step(): lax.all_gather(gate_vals[None], 'dp', axis=0, tiled=True)  17.8 us
  transfers between devices with their start and end apart: 8, of which 5 were waited for; matrix products, arithmetic and copies ran while one was open for 26% of the time, Pallas kernels for 0%

commit v1 on v0

--- a/solution.py
+++ b/solution.py
@@ -68,70 +68,81 @@
     return result.reshape(STEPS, row_count, HEADS * HEAD_DIM).astype(jnp.bfloat16)
 
 
-def route_tables(expert_ids, gate_vals):
-    numbers = jnp.arange(EXPERTS, dtype=jnp.int32)
-    picked = (expert_ids[..., None] == numbers).astype(jnp.int32)
-    per_row = jnp.sum(picked, axis=2)
-    earlier = jnp.cumsum(per_row, axis=1) - per_row
-    rank_vals = jnp.sum(picked * earlier[:, :, None, :], axis=3)
-    targets = expert_ids * MOST + rank_vals
-    places = jnp.arange(EXPERTS * MOST, dtype=jnp.int32)
-    matches = targets[..., None] == places
-    sender = jnp.any(matches, axis=2).astype(jnp.bfloat16)
-    weights = jnp.sum(
-        jnp.where(matches, gate_vals[..., None].astype(jnp.float32), 0.0), axis=2
+MOST = 2
+
+
+def moe_layer(hidden, norm_gain, router, routes, w_gate, w_up, w_down):
+    steps, rows, model_width = hidden.shape
+    topk = routes.shape[-1]
+    n_dp = lax.axis_size("dp")
+    n_ex = lax.axis_size("expert")
+    local_experts = w_gate.shape[0]
+    blocks = n_dp * n_ex
+    residual = hidden.astype(jnp.float32)
+    scale_rows = lax.rsqrt(jnp.mean(residual * residual, axis=-1, keepdims=True) + 1e-05)
+    normed = (residual * scale_rows * norm_gain).astype(jnp.bfloat16)
+    logit_rows = jnp.einsum("trd,de->tre", normed, router, preferred_element_type=jnp.float32)
+    chosen = jnp.take_along_axis(logit_rows, routes, axis=-1)
+    spreads = chosen[..., None, :] - chosen[..., :, None]
+    gate_vals = (1.0 / jnp.sum(jnp.exp(spreads), axis=-1)).astype(jnp.bfloat16)
+    lanes = -(-(model_width + 2 * topk) // 128) * 128
+    filler = jnp.zeros((steps, rows, lanes - model_width - 2 * topk), jnp.bfloat16)
+    payload = jnp.concatenate(
+        [normed, gate_vals, routes.astype(jnp.bfloat16), filler], axis=-1
+    )
+    gathered = lax.all_gather(payload, ("dp", "expert"), axis=1, tiled=False)
+    all_rows = gathered[..., :model_width]
+    all_gates = gathered[..., model_width : model_width + topk]
+    all_ids = gathered[..., model_width + topk : model_width + 2 * topk].astype(jnp.int32)
+    first = lax.axis_index("expert") * local_experts
+    numbers = first + jnp.arange(local_experts, dtype=jnp.int32)
+    matches = all_ids[..., None] == numbers
+    picked = jnp.any(matches, axis=-2).astype(jnp.int32)
+    gate_of = jnp.sum(jnp.where(matches, all_gates[..., None].astype(jnp.float32), 0.0), axis=-2)
+    earlier = jnp.cumsum(picked, axis=2) - picked
+    ranks = jnp.arange(MOST, dtype=jnp.int32)
+    sender = (picked[..., None] > 0) & (earlier[..., None] == ranks)
+    slots = jnp.einsum(
+        "tbrxm,tbrd->tbxmd",
+        sender.astype(jnp.bfloat16),
+        all_rows,
+        preferred_element_type=jnp.float32,
     ).astype(jnp.bfloat16)
-    return (sender, weights)
-
-
-def expert_block(slot_rows, w_gate, w_up, w_down):
-    gate_part = jnp.einsum(
-        "pkxmd,xdf->pkxmf", slot_rows, w_gate, preferred_element_type=jnp.float32
-    )
-    up_part = jnp.einsum("pkxmd,xdf->pkxmf", slot_rows, w_up, preferred_element_type=jnp.float32)
+    gate_part = jnp.einsum("tbxmd,xdf->tbxmf", slots, w_gate, preferred_element_type=jnp.float32)
+    up_part = jnp.einsum("tbxmd,xdf->tbxmf", slots, w_up, preferred_element_type=jnp.float32)
     hidden_act = ((up_part + 1.0) * gate_part * jax.nn.sigmoid(1.702 * gate_part)).astype(
         jnp.bfloat16
     )
-    return jnp.einsum(
-        "pkxmf,xfd->pkxmd", hidden_act, w_down, preferred_element_type=jnp.float32
+    partial = jnp.einsum(
+        "tbxmf,xfd->tbxmd", hidden_act, w_down, preferred_element_type=jnp.float32
     ).astype(jnp.bfloat16)
-
-
-def moe_step(hidden_rows, norm_gain, router, expert_ids, w_gate, w_up, w_down):
-    residual = hidden_rows.astype(jnp.float32)
-    scale_rows = lax.rsqrt(jnp.mean(residual * residual, axis=1, keepdims=True) + 1e-05)
-    normed = (residual * scale_rows * norm_gain).astype(jnp.bfloat16)
-    logit_rows = jnp.dot(normed, router, preferred_element_type=jnp.float32)
-    numbers = jnp.arange(EXPERTS, dtype=jnp.int32)
-    chosen = jnp.sum(
-        jnp.where(expert_ids[..., None] == numbers, logit_rows[:, None, :], 0.0), axis=-1
-    )
-    spreads = chosen[:, None, :] - chosen[:, :, None]
-    gate_vals = (1.0 / jnp.sum(jnp.exp(spreads), axis=2)).astype(jnp.bfloat16)
-    model_width = residual.shape[1]
-    columns = lax.axis_size("expert")
-    local_experts = w_gate.shape[0]
-    group_rows, group_ids, group_gates = (
-        lax.all_gather(normed[None], "dp", axis=0, tiled=True),
-        lax.all_gather(expert_ids.astype(jnp.bfloat16)[None], "dp", axis=0, tiled=True),
-        lax.all_gather(gate_vals[None], "dp", axis=0, tiled=True),
-    )
-    sender, weights = route_tables(group_ids.astype(jnp.int32), group_gates)
-    packed = jnp.einsum(
-        "prs,prd->psd", sender, group_rows, preferred_element_type=jnp.float32
-    ).astype(jnp.bfloat16)
-    packed = packed.reshape(packed.shape[0], columns, local_experts, MOST, model_width)
-    partial_out = expert_block(
-        lax.all_to_all(packed, "expert", split_axis=1, concat_axis=1, tiled=True),
-        w_gate,
-        w_up,
-        w_down,
-    )
-    returned = lax.all_to_all(partial_out, "expert", split_axis=1, concat_axis=1, tiled=True)
-    returned = returned.reshape(returned.shape[0], EXPERTS * MOST, model_width)
-    row_terms = jnp.einsum("prs,psd->prd", weights, returned, preferred_element_type=jnp.float32)
-    branch_out = lax.psum_scatter(row_terms, "dp", scatter_dimension=0, tiled=True)[0]
-    return (residual + branch_out).astype(jnp.bfloat16)
+    weights = jnp.where(sender, gate_of[..., None], 0.0).astype(jnp.bfloat16)
+    grid = (steps, n_dp, n_ex)
+    if local_experts * MOST < rows:
+        summed = lax.psum_scatter(
+            partial.astype(jnp.float32).reshape(grid + partial.shape[2:]),
+            "dp",
+            scatter_dimension=1,
+            tiled=True,
+        )[:, 0]
+        own = lax.axis_index("dp")
+        own_weights = lax.dynamic_index_in_dim(weights.reshape(grid + weights.shape[2:]), own, 1, False)
+        row_terms = jnp.einsum(
+            "terxm,texmd->terd",
+            own_weights.astype(jnp.float32),
+            summed,
+            precision=lax.Precision.HIGHEST,
+            preferred_element_type=jnp.float32,
+        )
+    else:
+        row_terms = jnp.einsum(
+            "tbrxm,tbxmd->tbrd", weights, partial, preferred_element_type=jnp.float32
+        )
+        row_terms = lax.psum_scatter(
+            row_terms.reshape(grid + row_terms.shape[2:]), "dp", scatter_dimension=1, tiled=True
+        )[:, 0]
+    branch_out = lax.psum_scatter(row_terms, "expert", scatter_dimension=1, tiled=True)
+    return (residual + branch_out[:, 0]).astype(jnp.bfloat16)
 
 
 def body(
@@ -160,14 +171,8 @@
     context = attention(
         queries, new_key, new_value, space_keys, space_values, page_counts[0], page_order[0]
     )
-    outputs = []
-    for step_index in range(STEPS):
-        outputs.append(
-            moe_step(
-                hidden[step_index], norm_gain, router, routes[step_index], w_gate, w_up, w_down
-            )
-        )
-    return (context, jnp.stack(outputs))
+    layer_out = moe_layer(hidden, norm_gain, router, routes, w_gate, w_up, w_down)
+    return (context, layer_out)
 
 
 def solution(mesh):

time: 665 us -> 338 us (0.51)
  waiting for transfers between devices: 380 us -> 158 us
  blocking collectives: 58.9 us -> 0 us
  starting transfers between devices: 30.5 us -> 7.14 us
  local copies, waits for them, and re-layouts: 50.8 us -> 39 us
    all_to_all x4 -> x0, waiting for transfers between devices: 370 us -> none  [the longest x2 187 us: moe_step(): lax.all_to_all(packed, 'expert', split_axis=1, concat_axis=1, tiled=True)]
    reduce_scatter x2, waiting for transfers between devices: 9.69 us -> 82.7 us  [the longest x1 82.7 us: moe_layer(): lax.psum_scatter(row_terms.reshape(grid + row_terms.shape[2:]), 'dp', sca...]
    all_gather x0 -> x1, waiting for transfers between devices: none -> 71 us  [moe_layer(): gathered = lax.all_gather(payload, ('dp', 'expert'), axis=1, tiled=False)]
    all_gather x6 -> x0, blocking collectives: 58.9 us -> none  [the longest x2 21.4 us: moe_step(): lax.all_gather(expert_ids.astype(jnp.bfloat16)[None], 'dp', axis=0, tiled...]
    convert_element_type x4, local copies, waits for them, and re-layouts: 29 us -> 0.26 us  [the longest x1 0.11 us: moe_layer(): routes.astype(jnp.bfloat16)]
    all_to_all x4 -> x0, starting transfers between devices: 21.6 us -> none  [the longest x2 10.9 us: moe_step(): lax.all_to_all(packed, 'expert', split_axis=1, concat_axis=1, tiled=True)]
    reshape x0 -> x1, local copies, waits for them, and re-layouts: none -> 10.4 us  [moe_layer(): row_terms.reshape(grid + row_terms.shape[2:])]
    dot_general x12 -> x6, matrix products: 98.3 us -> 94.1 us  [the longest x1 32.5 us: moe_layer(): jnp.einsum('tbrxm,tbxmd->tbrd', weights, partial, preferred_element_type=...]
  transfers between devices with their start and end apart: 8 -> 5, of which waited for: 5 -> 3; matrix products, arithmetic and copies ran while one was open for 26% -> 12% of each run, Pallas kernels for 0% -> 0%
where the time goes in v1:
time: 338 us; the launch traced here: 334 us
  waiting for transfers between devices  158 us (47%)
  matrix products  105 us (31%)
  local copies, waits for them, and re-layouts  39 us (12%)
  between operations  14.4 us (4%)
  other arithmetic  11.3 us (3%)
  starting transfers between devices  7.14 us (2%)
    reduce_scatter x1, waiting for transfers between devices, moe_layer(): lax.psum_scatter(row_terms.reshape(grid + row_terms.shape[2:]), 'dp', sca...  82.7 us
    all_gather x1, waiting for transfers between devices, moe_layer(): gathered = lax.all_gather(payload, ('dp', 'expert'), axis=1, tiled=False)  71 us
    dot_general x1, matrix products, moe_layer(): jnp.einsum('tbrxm,tbxmd->tbrd', weights, partial, preferred_element_type=...  32.5 us
    dot_general x1, matrix products, moe_layer(): jnp.einsum('tbxmf,xfd->tbxmd', hidden_act, w_down, preferred_element_type...  23.2 us
    dot_general x1, matrix products, moe_layer(): jnp.einsum('tbxmd,xdf->tbxmf', slots, w_gate, preferred_element_type=jnp....  13.9 us
    dot_general x1, matrix products, moe_layer(): jnp.einsum('tbxmd,xdf->tbxmf', slots, w_up, preferred_element_type=jnp.fl...  13.7 us
    dot_general x1, matrix products, moe_layer(): jnp.einsum('tbrxm,tbrd->tbxmd', sender.astype(jnp.bfloat16), all_rows, pr...  10.5 us
    reshape x1, local copies, waits for them, and re-layouts, moe_layer(): row_terms.reshape(grid + row_terms.shape[2:])  10.4 us
  transfers between devices with their start and end apart: 5, of which 3 were waited for; matrix products, arithmetic and copies ran while one was open for 12% of the time, Pallas kernels for 0%

profile of v1, /device:TPU:0, one launch (start us, length us, event | category | flops | bytes accessed | tf_op | source)
XLA Modules:
  0.0 334.4 jit_solution(11236955227884892801)
XLA Ops:
  11.5 1.5 gather_fusion.1
  14.3 71.0 %all-gather.3.cloned.1.call-done = bf16[2,512,2944]{2,1,0:T(8,128)(2,1)} async-done(((bf16[2,16,2944]{2,1,0:T(8,128)(2,1)}), bf16[2,512,2944]{2,1,0:T(8,128)(2,1)}) %all-gather.3.cloned.1.call-update) | async-done | bytes 6029328 | tf_op jit(solution)/shard_map/all_gather | solution.py:93
  85.2 1.3 fusion.68
  88.9 10.5 %convolution_convert_fusion = bf16[2,32,16,2,2880]{4,2,3,1,0:T(8,128)(2,1)} fusion(bf16[2,32,16,2944]{3,2,1,0:T(8,128)(2,1)} %bitcast.95, s32[2,32,16,16]{3,2,1,0:T(8,128)S(1)} %copy.129, pred[2,32,16,16]{3,2,1,0:T(8,128)(4,1)S(1)} %copy.128), kind=kOutput, calls=%fused_computation.15 | convolution fusion | flops 194707456 | bytes 17907712 | tf_op jit(solution)/shard_map/tbrxm,tbrd->tbxmd/dot_general | solution.py:105
  99.4 13.7 %fusion.4 = f32[16,2,32,2,256]{4,2,3,1,0:T(8,128)S(1)} fusion(bf16[16,2880,256]{2,1,0:T(8,128)(2,1)} %param.21, bf16[2,32,16,2,2880]{4,2,3,1,0:T(8,128)(2,1)} %convolution_convert_fusion), kind=kOutput, calls=%fused_computation.8 | convolution fusion | flops 3019898880 | bytes 37486592 | tf_op jit(solution)/shard_map/tbxmd,xdf->tbxmf/dot_general | solution.py:112
  113.1 13.9 %fusion.28 = bf16[2,32,16,2,256]{4,1,3,0,2:T(8,128)(2,1)S(1)} fusion(bf16[16,2880,256]{2,1,0:T(8,128)(2,1)} %param.20, bf16[2,32,16,2,2880]{4,2,3,1,0:T(8,128)(2,1)} %convolution_convert_fusion, f32[16,2,32,2,256]{4,2,3,1,0:T(8,128)S(1)} %fusion.4), kind=kOutput, calls=%fused_computation.34 | convolution fusion | flops 3024093184 | bytes 38535168 | tf_op jit(solution)/shard_map/tbxmd,xdf->tbxmf/dot_general | solution.py:111
  127.1 23.2 %convert_bitcast_fusion = bf16[2,32,16,2,2880]{4,1,3,0,2:T(8,128)(2,1)} fusion(bf16[2,32,16,2,256]{4,1,3,0,2:T(8,128)(2,1)S(1)} %fusion.28, bf16[16,256,2880]{1,2,0:T(8,128)(2,1)} %param.22), kind=kOutput, calls=%fused_computation.12 | convolution fusion | flops 3025797120 | bytes 36438016 | tf_op jit(solution)/shard_map/tbxmf,xfd->tbxmd/dot_general | solution.py:116
  150.2 32.5 %fusion.6 = f32[2,32,16,2880,1]{3,2,4,1,0:T(8,128)} fusion(bf16[2,32,16,2,2880]{4,1,3,0,2:T(8,128)(2,1)} %convert_bitcast_fusion, bf16[2,32,16,16]{3,2,1,0:T(8,128)(2,1)S(1)} %copy.132, s32[2,32,16,16]{3,2,1,0:T(8,128)S(1)} %copy.129, pred[2,32,16,16]{3,2,1,0:T(8,128)(4,1)S(1)} %copy.128), kind=kOutput, calls=%fused_computation.10 | convolution fusion | flops 188841984 | bytes 23707648 | tf_op jit(solution)/shard_map/tbrxm,tbxmd->tbrd/dot_general | solution.py:138
  182.7 10.4 %copy.137 = f32[2,8,4,16,2880]{4,3,0,2,1:T(8,128)} copy(f32[2,8,4,16,2880]{4,3,2,1,0:T(8,128)} %bitcast.93) | data formatting | bytes 23592960 | tf_op jit(solution)/shard_map/reshape | solution.py:142
  193.2 3.5 %all-to-all-start = ((bf16[8,4,16,512]{3,2,1,0:T(8,128)(2,1)}), bf16[8,4,16,512]{3,2,1,0:T(8,128)(2,1)S(1)}, u32[]{:S(2)}, u32[]{:S(2)}) async-start(bf16[8,4,16,512]{3,2,1,0:T(8,128)(2,1)} %param.27), calls=%async_computation | async-start | bytes 1048576 | tf_op jit(solution)/shard_map/all_to_all | solution.py:166
  197.6 1.6 gather_fusion
  199.2 82.7 %reduce-scatter.3.cloned.1.call-done = f32[2,1,4,16,2880]{4,3,0,2,1:T(8,128)} async-done(((f32[2,8,4,16,2880]{4,3,0,2,1:T(8,128)}), f32[2,1,4,16,2880]{4,3,0,2,1:T(8,128)}) %reduce-scatter.3.cloned.1.call-update) | async-done | bytes 1474576 | tf_op jit(solution)/shard_map/reduce_scatter | solution.py:141
  283.3 3.5 %all-to-all-start.1 = ((bf16[8,4,16,512]{3,2,1,0:T(8,128)(2,1)}), bf16[8,4,16,512]{3,2,1,0:T(8,128)(2,1)S(1)}, u32[]{:S(2)}, u32[]{:S(2)}) async-start(bf16[8,4,16,512]{3,2,1,0:T(8,128)(2,1)} %param.26), calls=%async_computation.1 | async-start | bytes 1048576 | tf_op jit(solution)/shard_map/all_to_all | solution.py:165
  286.9 3.2 fusion.69
  290.1 2.5 gather_fusion.2
  292.6 3.9 %all-to-all-done.1 = bf16[8,4,16,512]{3,2,1,0:T(8,128)(2,1)S(1)} async-done(((bf16[8,4,16,512]{3,2,1,0:T(8,128)(2,1)}), bf16[8,4,16,512]{3,2,1,0:T(8,128)(2,1)S(1)}, u32[]{:S(2)}, u32[]{:S(2)}) %all-to-all-start.1) | async-done | bytes 524320 | tf_op jit(solution)/shard_map/all_to_all | solution.py:165
  296.5 2.5 gather_fusion.3
  299.0 4.0 %broadcast_select_fusion = (bf16[160,16,512]{2,1,0:T(8,128)(2,1)}, bf16[160,16,512]{2,1,0:T(8,128)(2,1)S(1)}) fusion(bf16[160,16,512]{2,1,0:T(8,128)(2,1)} %gather_fusion.3, pred[160]{0:T(512)(128)(4,1)S(1)} %get-tuple-element.3, bf16[160,16,512]{2,1,0:T(8,128)(2,1)} %gather_fusion.2), kind=kLoop, calls=%fused_computation.21 | loop fusion | flops 2621440 | bytes 10485920 | tf_op jit(solution)/shard_map/jit(_take)/select_n | solution.py:29
  303.0 7.5 %reshape.266 = bf16[16,160,8,64]{3,2,1,0:T(8,128)(2,1)} reshape(bf16[160,16,512]{2,1,0:T(8,128)(2,1)} %get-tuple-element.9) | data formatting | bytes 5242880 | tf_op jit(solution)/shard_map/reshape | solution.py:29
  310.5 4.6 %reshape.264 = bf16[16,160,8,64]{3,2,1,0:T(8,128)(2,1)} reshape(bf16[160,16,512]{2,1,0:T(8,128)(2,1)S(1)} %get-tuple-element.10) | data formatting | bytes 5242880 | tf_op jit(solution)/shard_map/reshape | solution.py:32
  315.1 5.7 %bitcast_reduce_fusion = (f32[2,16,8,8]{3,0,2,1:T(2,128)S(1)}, f32[16,8,160,2,8]{2,4,3,1,0:T(8,128)S(1)}) fusion(pred[16,160]{1,0:T(8,128)(4,1)S(1)} %iota_compare_fusion.1, bf16[2,16,8,8,64]{4,3,2,1,0:T(8,128)(2,1)S(1)} %reshape.267, bf16[16,160,8,64,1]{3,2,1,0,4:T(8,128)(2,1)} %bitcast.101), kind=kOutput, calls=%fused_computation.24 | convolution fusion | flops 42924032 | bytes 4205056 | tf_op jit(solution)/shard_map/trkgh,rlkh->trkgl/dot_general | solution.py:41
  322.5 1.5 fusion.23
  324.8 1.2 convert_element_type.67
  326.0 1.7 fusion.56
  (93 shorter events, 12.6 us)
Async XLA Ops:
  7.2 4.1 %copy-start = (bf16[2880,64]{0,1:T(8,128)(2,1)S(1)}, bf16[2880,64]{0,1:T(8,128)(2,1)}, u32[]{:S(2)}) copy-start(bf16[2880,64]{0,1:T(8,128)(2,1)} %param.18) | copy-start | bytes 1105924
  7.2 78.0 %all-gather.3.cloned.1.call-start = ((), (), s32[]{:S(2)}) async-start(), calls=%async_computation.6 | async-start | bytes 6217728 | tf_op jit(solution)/shard_map/all_gather | solution.py:93
  14.2 267.7 %reduce-scatter.3.cloned.1.call-start = ((), (), s32[]{:S(2)}) async-start(), calls=%async_computation.4 | async-start | bytes 13565952 | tf_op jit(solution)/shard_map/reduce_scatter | solution.py:141
  193.1 3.6 %copy-start.9 = (s32[1,16]{1,0:T(1,128)S(1)}, s32[1,16]{1,0:T(1,128)}, u32[]{:S(2)}) copy-start(s32[1,16]{1,0:T(1,128)} %param.28) | copy-start | bytes 196
  193.1 4.4 %copy-start.2 = (s32[1,32]{1,0:T(1,128)S(1)}, s32[1,32]{1,0:T(1,128)}, u32[]{:S(2)}) copy-start(s32[1,32]{1,0:T(1,128)} %param.29) | copy-start | bytes 388
  193.2 90.2 %all-to-all-start = ((bf16[8,4,16,512]{3,2,1,0:T(8,128)(2,1)}), bf16[8,4,16,512]{3,2,1,0:T(8,128)(2,1)S(1)}, u32[]{:S(2)}, u32[]{:S(2)}) async-start(bf16[8,4,16,512]{3,2,1,0:T(8,128)(2,1)} %param.27), calls=%async_computation | async-start | bytes 1048576 | tf_op jit(solution)/shard_map/all_to_all | solution.py:166
  196.7 129.3 %reduce-scatter.5.cloned.1.call-start = ((), (), s32[]{:S(2)}) async-start(), calls=%async_computation.5 | async-start | bytes 1884160 | tf_op jit(solution)/shard_map/reduce_scatter | solution.py:144
  197.6 84.3 %copy-start.7 = (bf16[2,16,512]{2,1,0:T(8,128)(2,1)S(1)}, bf16[2,16,512]{2,1,0:T(8,128)(2,1)}, u32[]{:S(2)}) copy-start(bf16[2,16,512]{2,1,0:T(8,128)(2,1)} %param.24) | copy-start | bytes 98308
  197.6 84.4 %copy-start.8 = (bf16[2,16,512]{2,1,0:T(8,128)(2,1)S(1)}, bf16[2,16,512]{2,1,0:T(8,128)(2,1)}, u32[]{:S(2)}) copy-start(bf16[2,16,512]{2,1,0:T(8,128)(2,1)} %param.25) | copy-start | bytes 98308
  197.6 85.2 %copy-start.4 = (bf16[2,16,4096]{2,1,0:T(8,128)(2,1)S(1)}, bf16[2,16,4096]{2,1,0:T(8,128)(2,1)}, u32[]{:S(2)}) copy-start(bf16[2,16,4096]{2,1,0:T(8,128)(2,1)} %param.23) | copy-start | bytes 786436
  283.3 13.2 %all-to-all-start.1 = ((bf16[8,4,16,512]{3,2,1,0:T(8,128)(2,1)}), bf16[8,4,16,512]{3,2,1,0:T(8,128)(2,1)S(1)}, u32[]{:S(2)}, u32[]{:S(2)}) async-start(bf16[8,4,16,512]{3,2,1,0:T(8,128)(2,1)} %param.26), calls=%async_computation.1 | async-start | bytes 1048576 | tf_op jit(solution)/shard_map/all_to_all | solution.py:165
  315.1 7.4 %slice-start = ((s8[5242880]{0:T(1024)(128)(4,1)}), s8[4194304]{0:T(1024)(128)(4,1)S(1)}, s32[]{:S(2)}) async-start(s8[5242880]{0:T(1024)(128)(4,1)} %bitcast.98), calls=%async_computation.7 | async-start | bytes 8388608
  315.1 5.8 %copy-start.5 = (f32[2,16,8,8,2]{3,4,0,2,1:T(2,128)S(1)}, f32[2,16,8,8,2]{3,4,0,2,1:T(2,128)}, u32[]{:S(2)}) copy-start(f32[2,16,8,8,2]{3,4,0,2,1:T(2,128)} %get-tuple-element.14) | copy-start | bytes 49156
  315.1 7.4 %slice-start.1 = ((s8[5242880]{0:T(1024)(128)(4,1)}), s8[1048576]{0:T(1024)(128)(4,1)S(1)}, s32[]{:S(2)}) async-start(s8[5242880]{0:T(1024)(128)(4,1)} %bitcast.98), calls=%async_computation.8 | async-start | bytes 2097152
  322.5 1.5 copy-start.6
  324.0 2.0 copy-start.3
  324.1 3.7 %copy-start.1 = (bf16[2880,64]{0,1:T(8,128)(2,1)S(1)}, bf16[2880,64]{0,1:T(8,128)(2,1)}, u32[]{:S(2)}) copy-start(bf16[2880,64]{0,1:T(8,128)(2,1)} %param.18) | copy-start | bytes 1105924
Sparse Core Ops, SparseCore 0:
  14.3 70.8 all-gather.2
  193.3 88.5 reduce-scatter.2
  284.2 34.2 reduce-scatter.4

commit v2 on v1

--- a/solution.py
+++ b/solution.py
@@ -71,13 +71,20 @@
 MOST = 2
 
 
+def sibling(x):
+    n_dp = lax.axis_size("dp")
+    pairs = [(i, i ^ 1) for i in range(n_dp)]
+    return lax.ppermute(x, "dp", perm=pairs)
+
+
 def moe_layer(hidden, norm_gain, router, routes, w_gate, w_up, w_down):
     steps, rows, model_width = hidden.shape
     topk = routes.shape[-1]
     n_dp = lax.axis_size("dp")
     n_ex = lax.axis_size("expert")
     local_experts = w_gate.shape[0]
-    blocks = n_dp * n_ex
+    core = lax.axis_index("dp") % 2
+    same_core = [[i for i in range(n_dp) if i % 2 == c] for c in range(2)]
     residual = hidden.astype(jnp.float32)
     scale_rows = lax.rsqrt(jnp.mean(residual * residual, axis=-1, keepdims=True) + 1e-05)
     normed = (residual * scale_rows * norm_gain).astype(jnp.bfloat16)
@@ -90,7 +97,12 @@
     payload = jnp.concatenate(
         [normed, gate_vals, routes.astype(jnp.bfloat16), filler], axis=-1
     )
-    gathered = lax.all_gather(payload, ("dp", "expert"), axis=1, tiled=False)
+    mine = lax.dynamic_index_in_dim(payload, core, 0, keepdims=False)
+    theirs = sibling(lax.dynamic_index_in_dim(payload, 1 - core, 0, keepdims=False))
+    pair = jnp.where(core == 0, jnp.stack([mine, theirs]), jnp.stack([theirs, mine]))
+    pair = lax.all_gather(pair, "expert", axis=0, tiled=False)
+    gathered_mine = lax.all_gather(pair, "dp", axis=0, tiled=False, axis_index_groups=same_core)
+    gathered = jnp.stack([gathered_mine, sibling(gathered_mine)])
     all_rows = gathered[..., :model_width]
     all_gates = gathered[..., model_width : model_width + topk]
     all_ids = gathered[..., model_width + topk : model_width + 2 * topk].astype(jnp.int32)
@@ -99,50 +111,52 @@
     matches = all_ids[..., None] == numbers
     picked = jnp.any(matches, axis=-2).astype(jnp.int32)
     gate_of = jnp.sum(jnp.where(matches, all_gates[..., None].astype(jnp.float32), 0.0), axis=-2)
-    earlier = jnp.cumsum(picked, axis=2) - picked
+    earlier = jnp.cumsum(picked, axis=4) - picked
     ranks = jnp.arange(MOST, dtype=jnp.int32)
     sender = (picked[..., None] > 0) & (earlier[..., None] == ranks)
     slots = jnp.einsum(
-        "tbrxm,tbrd->tbxmd",
+        "tkecrxm,tkecrd->tkecxmd",
         sender.astype(jnp.bfloat16),
         all_rows,
         preferred_element_type=jnp.float32,
     ).astype(jnp.bfloat16)
-    gate_part = jnp.einsum("tbxmd,xdf->tbxmf", slots, w_gate, preferred_element_type=jnp.float32)
-    up_part = jnp.einsum("tbxmd,xdf->tbxmf", slots, w_up, preferred_element_type=jnp.float32)
+    gate_part = jnp.einsum("tkecxmd,xdf->tkecxmf", slots, w_gate, preferred_element_type=jnp.float32)
+    up_part = jnp.einsum("tkecxmd,xdf->tkecxmf", slots, w_up, preferred_element_type=jnp.float32)
     hidden_act = ((up_part + 1.0) * gate_part * jax.nn.sigmoid(1.702 * gate_part)).astype(
         jnp.bfloat16
     )
     partial = jnp.einsum(
-        "tbxmf,xfd->tbxmd", hidden_act, w_down, preferred_element_type=jnp.float32
+        "tkecxmf,xfd->tkecxmd", hidden_act, w_down, preferred_element_type=jnp.float32
     ).astype(jnp.bfloat16)
     weights = jnp.where(sender, gate_of[..., None], 0.0).astype(jnp.bfloat16)
-    grid = (steps, n_dp, n_ex)
     if local_experts * MOST < rows:
-        summed = lax.psum_scatter(
-            partial.astype(jnp.float32).reshape(grid + partial.shape[2:]),
-            "dp",
-            scatter_dimension=1,
-            tiled=True,
-        )[:, 0]
-        own = lax.axis_index("dp")
-        own_weights = lax.dynamic_index_in_dim(weights.reshape(grid + weights.shape[2:]), own, 1, False)
-        row_terms = jnp.einsum(
-            "terxm,texmd->terd",
+        terms = partial.astype(jnp.float32)
+        spread = "tecrxm,tecxmd->tecrd"
+    else:
+        terms = jnp.einsum(
+            "tkecrxm,tkecxmd->tkecrd", weights, partial, preferred_element_type=jnp.float32
+        )
+        spread = None
+    terms = terms[0] + sibling(terms[1])
+    terms = lax.psum_scatter(
+        terms, "dp", scatter_dimension=0, tiled=True, axis_index_groups=same_core
+    )[0]
+    terms = lax.psum_scatter(terms, "expert", scatter_dimension=0, tiled=True)[0]
+    if spread is not None:
+        chip = lax.axis_index("dp") // 2
+        own_weights = lax.dynamic_index_in_dim(weights[0], chip, 0, keepdims=False)
+        own_weights = lax.dynamic_index_in_dim(own_weights, lax.axis_index("expert"), 0, keepdims=False)
+        terms = jnp.einsum(
+            "crxm,cxmd->crd",
             own_weights.astype(jnp.float32),
-            summed,
+            terms,
             precision=lax.Precision.HIGHEST,
             preferred_element_type=jnp.float32,
         )
-    else:
-        row_terms = jnp.einsum(
-            "tbrxm,tbxmd->tbrd", weights, partial, preferred_element_type=jnp.float32
-        )
-        row_terms = lax.psum_scatter(
-            row_terms.reshape(grid + row_terms.shape[2:]), "dp", scatter_dimension=1, tiled=True
-        )[:, 0]
-    branch_out = lax.psum_scatter(row_terms, "expert", scatter_dimension=1, tiled=True)
-    return (residual + branch_out[:, 0]).astype(jnp.bfloat16)
+    own_now = lax.dynamic_index_in_dim(terms, core, 0, keepdims=False)
+    own_other = sibling(lax.dynamic_index_in_dim(terms, 1 - core, 0, keepdims=False))
+    branch_out = jnp.where(core == 0, jnp.stack([own_now, own_other]), jnp.stack([own_other, own_now]))
+    return (residual + branch_out).astype(jnp.bfloat16)
 
 
 def body(

time: 338 us -> 361 us (1.068)
  waiting for transfers between devices: 158 us -> 131 us
  blocking collectives: 0 us -> 21.2 us
  matrix products: 105 us -> 126 us
  other arithmetic: 11.3 us -> 25.7 us
  local copies, waits for them, and re-layouts: 39 us -> 30 us
    reduce_scatter x2 -> x1, waiting for transfers between devices: 82.7 us -> 0.01 us  [moe_layer(): lax.psum_scatter(terms, 'expert', scatter_dimension=0, tiled=True)[0]]
    unnamed x3 -> x4, waiting for transfers between devices: 0.05 us -> 67.7 us
    all_gather x1, waiting for transfers between devices: 71 us -> 42.9 us  [moe_layer(): lax.all_gather(pair, 'dp', axis=0, tiled=False, axis_index_groups=same_core)]
    all_gather x0 -> x1, blocking collectives: none -> 21.2 us  [moe_layer(): pair = lax.all_gather(pair, 'expert', axis=0, tiled=False)]
    dot_general x5, matrix products: 93.8 us -> 115 us  [the longest x1 35.9 us: moe_layer(): jnp.einsum('tkecxmd,xdf->tkecxmf', slots, w_up, preferred_element_type=jn...]
    ppermute x0 -> x4, waiting for transfers between devices: none -> 16.4 us  [sibling(): return lax.ppermute(x, 'dp', perm=pairs)]
    reshape x1 -> x0, local copies, waits for them, and re-layouts: 10.4 us -> none  [moe_layer(): row_terms.reshape(grid + row_terms.shape[2:])]
    add x0 -> x1, other arithmetic: none -> 6.12 us  [moe_layer(): terms = terms[0] + sibling(terms[1])]
  transfers between devices with their start and end apart: 5 -> 9, of which waited for: 3 -> 6; matrix products, arithmetic and copies ran while one was open for 12% -> 11% of each run, Pallas kernels for 0% -> 0%
where the time goes in v2:
time: 361 us; the launch traced here: 356 us
  waiting for transfers between devices  131 us (36%)
  matrix products  126 us (35%)
  local copies, waits for them, and re-layouts  30 us (8%)
  other arithmetic  25.7 us (7%)
  blocking collectives  21.2 us (6%)
  between operations  14.4 us (4%)
  starting transfers between devices  8.06 us (2%)
    unnamed x4, waiting for transfers between devices  67.7 us
    all_gather x1, waiting for transfers between devices, moe_layer(): lax.all_gather(pair, 'dp', axis=0, tiled=False, axis_index_groups=same_core)  42.9 us
    dot_general x1, matrix products, moe_layer(): jnp.einsum('tkecxmd,xdf->tkecxmf', slots, w_up, preferred_element_type=jn...  35.9 us
    dot_general x1, matrix products, moe_layer(): jnp.einsum('tkecxmd,xdf->tkecxmf', slots, w_gate, preferred_element_type=...  35.7 us
    all_gather x1, blocking collectives, moe_layer(): pair = lax.all_gather(pair, 'expert', axis=0, tiled=False)  21.2 us
    dot_general x1, matrix products, moe_layer(): jnp.einsum('tkecrxm,tkecxmd->tkecrd', weights, partial, preferred_element...  20.4 us
    ppermute x4, waiting for transfers between devices, sibling(): return lax.ppermute(x, 'dp', perm=pairs)  16.4 us
    dot_general x1, matrix products, moe_layer(): jnp.einsum('tkecxmf,xfd->tkecxmd', hidden_act, w_down, preferred_element_...  14.9 us
  transfers between devices with their start and end apart: 9, of which 6 were waited for; matrix products, arithmetic and copies ran while one was open for 11% of the time, Pallas kernels for 0%

profile of v2, /device:TPU:0, one launch (start us, length us, event | category | flops | bytes accessed | tf_op | source)
XLA Modules:
  0.0 356.3 jit_solution(14501192801052914973)
XLA Ops:
  15.0 21.2 %all_gather.10 = bf16[4,2,16,2944]{3,2,1,0:T(8,128)(2,1)} all-gather(bf16[1,2,16,2944]{3,2,1,0:T(8,128)(2,1)S(1)} %maximum_select_fusion.1), channel_id=1, replica_groups=mesh['dp'=8,'expert'=4] {'expert'}, dimensions={0}, use_global_device_ids=true | all-gather | bytes 942080 | tf_op jit(solution)/shard_map/all_gather | solution.py:103
  36.3 42.9 %all-gather.3.cloned.1.call-done = bf16[16,2,16,2944]{3,2,1,0:T(8,128)(2,1)} async-done(((bf16[4,2,16,2944]{3,2,1,0:T(8,128)(2,1)}), bf16[16,2,16,2944]{3,2,1,0:T(8,128)(2,1)}) %all-gather.3.cloned.1.call-update) | async-done | bytes 3014672 | tf_op jit(solution)/shard_map/all_gather | solution.py:104
  79.2 5.7 %collective-permute-done.1 = bf16[4,4,2,16,2944]{4,3,2,1,0:T(8,128)(2,1)S(1)} collective-permute-done((bf16[4,4,2,16,2944]{4,3,2,1,0:T(8,128)(2,1)}, bf16[4,4,2,16,2944]{4,3,2,1,0:T(8,128)(2,1)S(1)}, u32[]{:S(2)}, u32[]{:S(2)}) %collective-permute-start.1) | collective-permute-done | bytes 3014688 | tf_op jit(solution)/shard_map/ppermute | solution.py:77
  90.6 2.3 reduce_window_sum.18
  92.9 1.9 convert_subtract_fusion
  96.2 2.2 fusion.27
  98.4 7.8 %convolution_convert_fusion = bf16[2,4,4,2,16,2,2880]{6,4,5,3,2,1,0:T(8,128)(2,1)} fusion(bf16[1,4,4,2,16,2944]{5,4,3,2,1,0:T(8,128)(2,1)} %bitcast.119, bf16[1,4,4,2,16,2944]{5,4,3,2,1,0:T(8,128)(2,1)S(1)} %bitcast.117, s32[2,4,4,2,16,16]{5,4,3,2,1,0:T(8,128)} %convert_subtract_fusion, pred[2,4,4,2,16,16]{5,4,3,2,1,0:T(8,128)(4,1)S(1)} %get-tuple-element.11), kind=kOutput, calls=%fused_computation.16 | convolution fusion | flops 206503936 | bytes 17907712 | tf_op jit(solution)/shard_map/tkecrxm,tkecrd->tkecxmd/dot_general | solution.py:117
  106.2 35.9 %fusion.4 = f32[16,2,4,4,2,2,256]{6,3,5,4,2,1,0:T(4,128)} fusion(bf16[16,2880,256]{2,1,0:T(8,128)(2,1)} %param.21, bf16[2,4,4,2,16,2,2880]{6,4,5,3,2,1,0:T(8,128)(2,1)} %convolution_convert_fusion), kind=kOutput, calls=%fused_computation.8 | convolution fusion | flops 3019898880 | bytes 37486592 | tf_op jit(solution)/shard_map/tkecxmd,xdf->tkecxmf/dot_general | solution.py:124
  142.1 35.7 %fusion.45 = bf16[2,4,4,2,16,2,256]{6,2,5,3,1,0,4:T(4,128)(2,1)S(1)} fusion(bf16[16,2880,256]{2,1,0:T(8,128)(2,1)} %param.20, bf16[2,4,4,2,16,2,2880]{6,4,5,3,2,1,0:T(8,128)(2,1)} %convolution_convert_fusion, f32[16,2,4,4,2,2,256]{6,3,5,4,2,1,0:T(4,128)} %fusion.4), kind=kOutput, calls=%fused_computation.45 | convolution fusion | flops 3024093184 | bytes 38535168 | tf_op jit(solution)/shard_map/tkecxmd,xdf->tkecxmf/dot_general | solution.py:123
  177.9 14.9 %fusion.11 = bf16[2,4,4,2,16,2,2880]{6,2,5,3,1,0,4:T(4,128)(2,1)} fusion(bf16[2,4,4,2,16,2,256]{6,2,5,3,1,0,4:T(4,128)(2,1)S(1)} %fusion.45, bf16[16,256,2880]{1,2,0:T(8,128)(2,1)} %param.22), kind=kOutput, calls=%fused_computation.13 | convolution fusion | flops 3025797120 | bytes 36438016 | tf_op jit(solution)/shard_map/tkecxmf,xfd->tkecxmd/dot_general | solution.py:128
  192.8 20.4 %fusion.16 = f32[2,4,4,2,16,2880]{5,4,3,2,1,0:T(8,128)S(1)} fusion(bf16[2,4,4,2,16,2,2880]{6,2,5,3,1,0,4:T(4,128)(2,1)} %fusion.11, bf16[2,4,4,2,16,16]{5,4,3,2,1,0:T(8,128)(2,1)S(1)} %copy-done.7, s32[2,4,4,2,16,16]{5,4,3,2,1,0:T(8,128)S(1)} %copy-done.5, pred[2,4,4,2,16,16]{5,4,3,2,1,0:T(8,128)(4,1)S(1)} %get-tuple-element.11), kind=kOutput, calls=%fused_computation.17 | convolution fusion | flops 188841984 | bytes 23707648 | tf_op jit(solution)/shard_map/tkecrxm,tkecxmd->tkecrd/dot_general | solution.py:136
  213.9 9.8 %collective-permute-done.2 = f32[4,4,2,16,2880]{4,3,2,1,0:T(8,128)} collective-permute-done((f32[4,4,2,16,2880]{4,3,2,1,0:T(8,128)S(1)}, f32[4,4,2,16,2880]{4,3,2,1,0:T(8,128)}, u32[]{:S(2)}, u32[]{:S(2)}) %collective-permute-start.2) | collective-permute-done | bytes 5898272 | tf_op jit(solution)/shard_map/ppermute | solution.py:77
  223.6 6.1 %fusion.19 = f32[4,4,2,16,2880]{4,3,2,1,0:T(8,128)} fusion(f32[4,4,2,16,2880]{4,3,2,1,0:T(8,128)} %collective-permute-done.2, f32[2,4,4,2,16,2880]{5,4,3,2,1,0:T(8,128)S(1)} %fusion.16), kind=kLoop, calls=%fused_computation.20 | loop fusion | flops 1474560 | bytes 17694720 | tf_op jit(solution)/shard_map/add | solution.py:140
  229.8 3.6 %all-to-all-start = ((bf16[8,4,16,512]{3,2,1,0:T(8,128)(2,1)}), bf16[8,4,16,512]{3,2,1,0:T(8,128)(2,1)S(1)}, u32[]{:S(2)}, u32[]{:S(2)}) async-start(bf16[8,4,16,512]{3,2,1,0:T(8,128)(2,1)} %param.27), calls=%async_computation | async-start | bytes 1048576 | tf_op jit(solution)/shard_map/all_to_all | solution.py:180
  234.0 67.6 %reduce-scatter.7.cloned.1.call-done = f32[1,4,2,16,2880]{4,3,2,1,0:T(8,128)} async-done(((f32[4,4,2,16,2880]{4,3,2,1,0:T(8,128)}), f32[1,4,2,16,2880]{4,3,2,1,0:T(8,128)}) %reduce-scatter.7.cloned.1.call-update) | async-done | bytes 1474576
  305.1 3.5 all-to-all-start.1
  308.6 3.2 fusion.84
  311.8 2.5 gather_fusion.2
  314.3 3.9 %all-to-all-done.1 = bf16[8,4,16,512]{3,2,1,0:T(8,128)(2,1)S(1)} async-done(((bf16[8,4,16,512]{3,2,1,0:T(8,128)(2,1)}), bf16[8,4,16,512]{3,2,1,0:T(8,128)(2,1)S(1)}, u32[]{:S(2)}, u32[]{:S(2)}) %all-to-all-start.1) | async-done | bytes 524320 | tf_op jit(solution)/shard_map/all_to_all | solution.py:179
  318.2 2.5 gather_fusion.3
  320.7 4.0 %broadcast_select_fusion = (bf16[160,16,512]{2,1,0:T(8,128)(2,1)}, bf16[160,16,512]{2,1,0:T(8,128)(2,1)S(1)}) fusion(bf16[160,16,512]{2,1,0:T(8,128)(2,1)} %gather_fusion.3, pred[160]{0:T(512)(128)(4,1)S(1)} %get-tuple-element.3, bf16[160,16,512]{2,1,0:T(8,128)(2,1)} %gather_fusion.2), kind=kLoop, calls=%fused_computation.30 | loop fusion | flops 2621440 | bytes 10485920 | tf_op jit(solution)/shard_map/jit(_take)/select_n | solution.py:29
  324.7 7.5 %reshape.323 = bf16[16,160,8,64]{3,2,1,0:T(8,128)(2,1)} reshape(bf16[160,16,512]{2,1,0:T(8,128)(2,1)} %get-tuple-element.15) | data formatting | bytes 5242880 | tf_op jit(solution)/shard_map/reshape | solution.py:29
  332.2 4.6 %reshape.321 = bf16[16,160,8,64]{3,2,1,0:T(8,128)(2,1)} reshape(bf16[160,16,512]{2,1,0:T(8,128)(2,1)S(1)} %get-tuple-element.16) | data formatting | bytes 5242880 | tf_op jit(solution)/shard_map/reshape | solution.py:32
  336.8 5.7 %bitcast_reduce_fusion = (f32[2,16,8,8]{3,0,2,1:T(2,128)S(1)}, f32[16,8,160,2,8]{2,4,3,1,0:T(8,128)S(1)}) fusion(pred[16,160]{1,0:T(8,128)(4,1)S(1)} %iota_compare_fusion.1, bf16[2,16,8,8,64]{4,3,2,1,0:T(8,128)(2,1)S(1)} %reshape.324, bf16[16,160,8,64,1]{3,2,1,0,4:T(8,128)(2,1)} %bitcast.123), kind=kOutput, calls=%fused_computation.35 | convolution fusion | flops 42924032 | bytes 4205056 | tf_op jit(solution)/shard_map/trkgh,rlkh->trkgl/dot_general | solution.py:41
  (110 shorter events, 26.5 us)
Async XLA Ops:
  7.2 4.0 %copy-start = (bf16[2880,64]{0,1:T(8,128)(2,1)S(1)}, bf16[2880,64]{0,1:T(8,128)(2,1)}, u32[]{:S(2)}) copy-start(bf16[2880,64]{0,1:T(8,128)(2,1)} %param.18) | copy-start | bytes 1105924
  7.2 72.0 %all-gather.3.cloned.1.call-start = ((), (), s32[]{:S(2)}) async-start(), calls=%async_computation.5 | async-start | bytes 3768320 | tf_op jit(solution)/shard_map/all_gather | solution.py:104
  13.5 1.5 collective-permute-start
  36.3 265.3 %reduce-scatter.7.cloned.1.call-start = ((), (), s32[]{:S(2)}) async-start(), calls=%async_computation.6 | async-start | bytes 7536640
  79.2 5.7 %collective-permute-start.1 = (bf16[4,4,2,16,2944]{4,3,2,1,0:T(8,128)(2,1)}, bf16[4,4,2,16,2944]{4,3,2,1,0:T(8,128)(2,1)S(1)}, u32[]{:S(2)}, u32[]{:S(2)}) collective-permute-start(bf16[4,4,2,16,2944]{4,3,2,1,0:T(8,128)(2,1)} %bitcast.115), channel_id=1, source_target_pairs={{0,4},{4,0},{8,12},{12,8},{16,20},{20,16},{24,28},{28,24},{1,5},{5... | collective-permute-start | bytes 9043976 | tf_op jit(solution)/shard_map/ppermute | solution.py:77
  88.4 10.0 %copy-start.3 = (bf16[16,2,16,2944]{3,2,1,0:T(8,128)(2,1)S(1)}, bf16[16,2,16,2944]{3,2,1,0:T(8,128)(2,1)}, u32[]{:S(2)}) copy-start(bf16[16,2,16,2944]{3,2,1,0:T(8,128)(2,1)} %all-gather.3.cloned.1.call-done) | copy-start | bytes 9043972
  177.8 14.9 %copy-start.5 = (s32[2,4,4,2,16,16]{5,4,3,2,1,0:T(8,128)S(1)}, s32[2,4,4,2,16,16]{5,4,3,2,1,0:T(8,128)}, u32[]{:S(2)}) copy-start(s32[2,4,4,2,16,16]{5,4,3,2,1,0:T(8,128)} %convert_subtract_fusion) | copy-start | bytes 196612
  177.9 14.9 %copy-start.7 = (bf16[2,4,4,2,16,16]{5,4,3,2,1,0:T(8,128)(2,1)S(1)}, bf16[2,4,4,2,16,16]{5,4,3,2,1,0:T(8,128)(2,1)}, u32[]{:S(2)}) copy-start(bf16[2,4,4,2,16,16]{5,4,3,2,1,0:T(8,128)(2,1)} %fusion.27) | copy-start | bytes 98308
  213.7 10.0 %collective-permute-start.2 = (f32[4,4,2,16,2880]{4,3,2,1,0:T(8,128)S(1)}, f32[4,4,2,16,2880]{4,3,2,1,0:T(8,128)}, u32[]{:S(2)}, u32[]{:S(2)}) collective-permute-start(f32[4,4,2,16,2880]{4,3,2,1,0:T(8,128)S(1)} %slice_bitcast_fusion), channel_id=1, source_target_pairs={{0,4},{4,0},{8,12},{12,8},{16,20},{20,16},{24,28},{28,24},{1,5},{5... | collective-permute-start | bytes 17694728 | tf_op jit(solution)/shard_map/ppermute | solution.py:77
  229.8 3.8 %copy-start.13 = (s32[1,16]{1,0:T(1,128)S(1)}, s32[1,16]{1,0:T(1,128)}, u32[]{:S(2)}) copy-start(s32[1,16]{1,0:T(1,128)} %param.28) | copy-start | bytes 196
  229.8 72.3 %copy-start.8 = (bf16[2,16,4096]{2,1,0:T(8,128)(2,1)S(1)}, bf16[2,16,4096]{2,1,0:T(8,128)(2,1)}, u32[]{:S(2)}) copy-start(bf16[2,16,4096]{2,1,0:T(8,128)(2,1)} %param.23) | copy-start | bytes 786436
  229.8 72.8 %copy-start.11 = (bf16[2,16,512]{2,1,0:T(8,128)(2,1)S(1)}, bf16[2,16,512]{2,1,0:T(8,128)(2,1)}, u32[]{:S(2)}) copy-start(bf16[2,16,512]{2,1,0:T(8,128)(2,1)} %param.24) | copy-start | bytes 98308
  229.8 72.9 %copy-start.12 = (bf16[2,16,512]{2,1,0:T(8,128)(2,1)S(1)}, bf16[2,16,512]{2,1,0:T(8,128)(2,1)}, u32[]{:S(2)}) copy-start(bf16[2,16,512]{2,1,0:T(8,128)(2,1)} %param.25) | copy-start | bytes 98308
  229.8 73.6 %copy-start.2 = (s32[1,32]{1,0:T(1,128)S(1)}, s32[1,32]{1,0:T(1,128)}, u32[]{:S(2)}) copy-start(s32[1,32]{1,0:T(1,128)} %param.29) | copy-start | bytes 388
  229.8 75.2 %all-to-all-start = ((bf16[8,4,16,512]{3,2,1,0:T(8,128)(2,1)}), bf16[8,4,16,512]{3,2,1,0:T(8,128)(2,1)S(1)}, u32[]{:S(2)}, u32[]{:S(2)}) async-start(bf16[8,4,16,512]{3,2,1,0:T(8,128)(2,1)} %param.27), calls=%async_computation | async-start | bytes 1048576 | tf_op jit(solution)/shard_map/all_to_all | solution.py:180
  233.5 112.3 %reduce-scatter.5.cloned.1.call-start = ((), (), s32[]{:S(2)}) async-start(), calls=%async_computation.4 | async-start | bytes 1884160 | tf_op jit(solution)/shard_map/reduce_scatter | solution.py:144
  305.1 13.2 %all-to-all-start.1 = ((bf16[8,4,16,512]{3,2,1,0:T(8,128)(2,1)}), bf16[8,4,16,512]{3,2,1,0:T(8,128)(2,1)S(1)}, u32[]{:S(2)}, u32[]{:S(2)}) async-start(bf16[8,4,16,512]{3,2,1,0:T(8,128)(2,1)} %param.26), calls=%async_computation.1 | async-start | bytes 1048576 | tf_op jit(solution)/shard_map/all_to_all | solution.py:179
  336.8 7.4 %slice-start = ((s8[5242880]{0:T(1024)(128)(4,1)}), s8[4194304]{0:T(1024)(128)(4,1)S(1)}, s32[]{:S(2)}) async-start(s8[5242880]{0:T(1024)(128)(4,1)} %bitcast.120), calls=%async_computation.7 | async-start | bytes 8388608
  336.8 5.8 %copy-start.9 = (f32[2,16,8,8,2]{3,4,0,2,1:T(2,128)S(1)}, f32[2,16,8,8,2]{3,4,0,2,1:T(2,128)}, u32[]{:S(2)}) copy-start(f32[2,16,8,8,2]{3,4,0,2,1:T(2,128)} %get-tuple-element.20) | copy-start | bytes 49156
  336.8 7.4 %slice-start.1 = ((s8[5242880]{0:T(1024)(128)(4,1)}), s8[1048576]{0:T(1024)(128)(4,1)S(1)}, s32[]{:S(2)}) async-start(s8[5242880]{0:T(1024)(128)(4,1)} %bitcast.120), calls=%async_computation.8 | async-start | bytes 2097152
  344.2 2.7 copy-start.10
  346.8 2.0 collective-permute-start.3
  346.9 1.9 copy-start.6
  346.9 2.7 copy-start.1
  (1 other events, 1.6 us)
Sparse Core Ops, SparseCore 0:
  36.4 42.7 all-gather.2
  229.9 71.6 reduce-scatter.6
  303.9 34.2 reduce-scatter.4

commit v3 on v1

--- a/solution.py
+++ b/solution.py
@@ -91,9 +91,17 @@
         [normed, gate_vals, routes.astype(jnp.bfloat16), filler], axis=-1
     )
     gathered = lax.all_gather(payload, ("dp", "expert"), axis=1, tiled=False)
+    return gathered, residual
+
+
+def moe_finish(gathered, residual, topk, w_gate, w_up, w_down):
+    steps, rows, model_width = residual.shape
+    n_dp = lax.axis_size("dp")
+    n_ex = lax.axis_size("expert")
+    local_experts = w_gate.shape[0]
     all_rows = gathered[..., :model_width]
     all_gates = gathered[..., model_width : model_width + topk]
-    all_ids = gathered[..., model_width + topk : model_width + 2 * topk].astype(jnp.int32)
+    all_ids = jnp.round(gathered[..., model_width + topk : model_width + 2 * topk]).astype(jnp.int32)
     first = lax.axis_index("expert") * local_experts
     numbers = first + jnp.arange(local_experts, dtype=jnp.int32)
     matches = all_ids[..., None] == numbers
@@ -137,12 +145,12 @@
     else:
         row_terms = jnp.einsum(
             "tbrxm,tbxmd->tbrd", weights, partial, preferred_element_type=jnp.float32
-        )
+        ).astype(jnp.bfloat16)
         row_terms = lax.psum_scatter(
             row_terms.reshape(grid + row_terms.shape[2:]), "dp", scatter_dimension=1, tiled=True
         )[:, 0]
     branch_out = lax.psum_scatter(row_terms, "expert", scatter_dimension=1, tiled=True)
-    return (residual + branch_out[:, 0]).astype(jnp.bfloat16)
+    return (residual + branch_out[:, 0].astype(jnp.float32)).astype(jnp.bfloat16)
 
 
 def body(
@@ -168,10 +176,12 @@
     kv_width = KV_HEADS * HEAD_DIM
     space_keys = host_keys.reshape(-1, BLOCK, kv_width)
     space_values = host_values.reshape(-1, BLOCK, kv_width)
+    gathered, residual = moe_layer(hidden, norm_gain, router, routes, w_gate, w_up, w_down)
     context = attention(
         queries, new_key, new_value, space_keys, space_values, page_counts[0], page_order[0]
     )
-    layer_out = moe_layer(hidden, norm_gain, router, routes, w_gate, w_up, w_down)
+    gathered, context = lax.optimization_barrier((gathered, context))
+    layer_out = moe_finish(gathered, residual, routes.shape[-1], w_gate, w_up, w_down)
     return (context, layer_out)
 
 

time: 338 us -> 295 us (0.87)
  waiting for transfers between devices: 158 us -> 108 us
  local copies, waits for them, and re-layouts: 39 us -> 55.1 us
  matrix products: 105 us -> 91.2 us
    all_gather x1, waiting for transfers between devices: 71 us -> 12.4 us  [moe_layer(): gathered = lax.all_gather(payload, ('dp', 'expert'), axis=1, tiled=False)]
    optimization_barrier x0 -> x1, local copies, waits for them, and re-layouts: none -> 26 us  [body(): gathered, context = lax.optimization_barrier((gathered, context))]
    dot_general x5, matrix products: 93.8 us -> 79.3 us  [the longest x1 23.1 us: moe_finish(): jnp.einsum('tbxmf,xfd->tbxmd', hidden_act, w_down, preferred_element_type...]
    reshape x1, local copies, waits for them, and re-layouts: 10.4 us -> 3.05 us  [moe_finish(): row_terms.reshape(grid + row_terms.shape[2:])]
    all_to_all x1, waiting for transfers between devices: 0.01 us -> 3.86 us  [body(): lax.all_to_all(value_pages, 'dp', split_axis=0, concat_axis=0, tiled=True)]
  transfers between devices with their start and end apart: 5 -> 5, of which waited for: 3 -> 5; matrix products, arithmetic and copies ran while one was open for 12% -> 14% of each run, Pallas kernels for 0% -> 0%
where the time goes in v3:
time: 295 us; the launch traced here: 290 us
  waiting for transfers between devices  108 us (37%)
  matrix products  91.2 us (31%)
  local copies, waits for them, and re-layouts  55.1 us (19%)
  between operations  14.4 us (5%)
  other arithmetic  12.5 us (4%)
  starting transfers between devices  8.8 us (3%)
    reduce_scatter x1, waiting for transfers between devices, moe_finish(): lax.psum_scatter(row_terms.reshape(grid + row_terms.shape[2:]), 'dp', sca...  59.4 us
    optimization_barrier x1, local copies, waits for them, and re-layouts, body(): gathered, context = lax.optimization_barrier((gathered, context))  26 us
    reduce_scatter x1, waiting for transfers between devices, moe_finish(): lax.psum_scatter(row_terms, 'expert', scatter_dimension=1, tiled=True)  25.4 us
    dot_general x1, matrix products, moe_finish(): jnp.einsum('tbxmf,xfd->tbxmd', hidden_act, w_down, preferred_element_type...  23.1 us
    dot_general x1, matrix products, moe_finish(): jnp.einsum('tbrxm,tbxmd->tbrd', weights, partial, preferred_element_type=...  17.9 us
    dot_general x1, matrix products, moe_finish(): jnp.einsum('tbxmd,xdf->tbxmf', slots, w_gate, preferred_element_type=jnp....  13.9 us
    dot_general x1, matrix products, moe_finish(): jnp.einsum('tbxmd,xdf->tbxmf', slots, w_up, preferred_element_type=jnp.fl...  13.9 us
    all_gather x1, waiting for transfers between devices, moe_layer(): gathered = lax.all_gather(payload, ('dp', 'expert'), axis=1, tiled=False)  12.4 us
  transfers between devices with their start and end apart: 5, of which 5 were waited for; matrix products, arithmetic and copies ran while one was open for 14% of the time, Pallas kernels for 0%

profile of v3, /device:TPU:0, one launch (start us, length us, event | category | flops | bytes accessed | tf_op | source)
XLA Modules:
  0.0 289.6 jit_solution(8246230687556691771)
XLA Ops:
  11.4 1.5 gather_fusion.1
  14.2 5.2 %all-to-all-start.1 = ((bf16[8,4,16,512]{3,2,1,0:T(8,128)(2,1)}), bf16[8,4,16,512]{3,2,1,0:T(8,128)(2,1)S(1)}, u32[]{:S(2)}, u32[]{:S(2)}) async-start(bf16[8,4,16,512]{3,2,1,0:T(8,128)(2,1)} %param.26), calls=%async_computation.1 | async-start | bytes 1048576 | tf_op jit(solution)/shard_map/all_to_all | solution.py:173
  21.1 1.6 gather_fusion
  22.7 6.6 %all-to-all-done.1 = bf16[8,4,16,512]{3,2,1,0:T(8,128)(2,1)S(1)} async-done(((bf16[8,4,16,512]{3,2,1,0:T(8,128)(2,1)}), bf16[8,4,16,512]{3,2,1,0:T(8,128)(2,1)S(1)}, u32[]{:S(2)}, u32[]{:S(2)}) %all-to-all-start.1) | async-done | bytes 524320 | tf_op jit(solution)/shard_map/all_to_all | solution.py:173
  29.3 3.5 %all-to-all-start = ((bf16[8,4,16,512]{3,2,1,0:T(8,128)(2,1)}), bf16[8,4,16,512]{3,2,1,0:T(8,128)(2,1)S(1)}, u32[]{:S(2)}, u32[]{:S(2)}) async-start(bf16[8,4,16,512]{3,2,1,0:T(8,128)(2,1)} %param.27), calls=%async_computation | async-start | bytes 1048576 | tf_op jit(solution)/shard_map/all_to_all | solution.py:174
  32.9 3.2 %fusion.73 = (f32[2,16,8,8]{3,0,2,1:T(2,128)S(1)}, f32[2,16,8,8,2]{3,4,0,2,1:T(2,128)}) fusion(bf16[2,16,8,8,64]{4,3,2,1,0:T(8,128)(2,1)S(1)} %reshape.270, bf16[2,16,8,64,1]{3,2,1,0,4:T(8,128)(2,1)S(1)} %bitcast.105, pred[2,2]{1,0:T(4,128)(4,1)S(1)} %iota_compare_fusion.3), kind=kOutput, calls=%fused_computation.104 | convolution fusion | flops 534528 | bytes 319492 | tf_op jit(solution)/shard_map/trkgh,urkh->trkgu/dot_general | solution.py:46
  36.1 2.5 gather_fusion.3
  38.6 3.9 %all-to-all-done = bf16[8,4,16,512]{3,2,1,0:T(8,128)(2,1)S(1)} async-done(((bf16[8,4,16,512]{3,2,1,0:T(8,128)(2,1)}), bf16[8,4,16,512]{3,2,1,0:T(8,128)(2,1)S(1)}, u32[]{:S(2)}, u32[]{:S(2)}) %all-to-all-start) | async-done | bytes 524320 | tf_op jit(solution)/shard_map/all_to_all | solution.py:174
  42.4 2.5 gather_fusion.2
  44.9 4.5 %broadcast_select_fusion = (bf16[160,16,512]{2,1,0:T(8,128)(2,1)S(1)}, bf16[160,16,512]{2,1,0:T(8,128)(2,1)}) fusion(bf16[160,16,512]{2,1,0:T(8,128)(2,1)} %gather_fusion.3, pred[160]{0:T(512)(128)(4,1)S(1)} %get-tuple-element.7, bf16[160,16,512]{2,1,0:T(8,128)(2,1)} %gather_fusion.2), kind=kLoop, calls=%fused_computation.23 | loop fusion | flops 2621440 | bytes 10485920 | tf_op jit(solution)/shard_map/jit(_take)/select_n | solution.py:29
  49.4 7.5 %reshape.267 = bf16[16,160,8,64]{3,2,1,0:T(8,128)(2,1)} reshape(bf16[160,16,512]{2,1,0:T(8,128)(2,1)} %get-tuple-element.14) | data formatting | bytes 5242880 | tf_op jit(solution)/shard_map/reshape | solution.py:32
  56.9 4.6 %reshape.269 = bf16[16,160,8,64]{3,2,1,0:T(8,128)(2,1)} reshape(bf16[160,16,512]{2,1,0:T(8,128)(2,1)S(1)} %get-tuple-element.13) | data formatting | bytes 5242880 | tf_op jit(solution)/shard_map/reshape | solution.py:29
  61.5 6.3 %bitcast_reduce_fusion = (f32[2,16,8,8]{3,0,2,1:T(2,128)S(1)}, f32[16,8,160,2,8]{2,4,3,1,0:T(8,128)S(1)}) fusion(pred[16,160]{1,0:T(8,128)(4,1)S(1)} %iota_compare_fusion.1, bf16[2,16,8,8,64]{4,3,2,1,0:T(8,128)(2,1)S(1)} %reshape.270, bf16[16,160,8,64,1]{3,2,1,0,4:T(8,128)(2,1)} %bitcast.102), kind=kOutput, calls=%fused_computation.26 | convolution fusion | flops 42924032 | bytes 4205056 | tf_op jit(solution)/shard_map/trkgh,rlkh->trkgl/dot_general | solution.py:41
  73.0 12.4 %all-gather.3.cloned.1.call-done = bf16[2,512,2944]{2,1,0:T(8,128)(2,1)} async-done(((bf16[2,16,2944]{2,1,0:T(8,128)(2,1)}), bf16[2,512,2944]{2,1,0:T(8,128)(2,1)}) %all-gather.3.cloned.1.call-update) | async-done | bytes 6029328 | tf_op jit(solution)/shard_map/all_gather | solution.py:93
  85.4 26.0 %copy.125 = bf16[2,32,16,2944]{1,2,3,0:T(8,128)(2,1)} copy(bf16[2,32,16,2944]{3,2,1,0:T(8,128)(2,1)} %bitcast.94) | data formatting | bytes 12058624 | tf_op jit(solution)/shard_map/optimization_barrier | solution.py:183
  113.9 10.5 %convolution_convert_fusion = bf16[2,32,16,2,2880]{4,2,3,1,0:T(8,128)(2,1)} fusion(bf16[2,32,16,2944]{3,2,1,0:T(8,128)(2,1)} %bitcast.95, s32[2,32,16,16]{3,2,1,0:T(8,128)S(1)} %copy.129, pred[2,32,16,16]{3,2,1,0:T(8,128)(4,1)S(1)} %copy.128), kind=kOutput, calls=%fused_computation.16 | convolution fusion | flops 194707456 | bytes 17907712 | tf_op jit(solution)/shard_map/tbrxm,tbrd->tbxmd/dot_general | solution.py:113
  124.4 13.9 %fusion.4 = f32[16,2,32,2,256]{4,2,3,1,0:T(8,128)S(1)} fusion(bf16[16,2880,256]{2,1,0:T(8,128)(2,1)} %param.21, bf16[2,32,16,2,2880]{4,2,3,1,0:T(8,128)(2,1)} %convolution_convert_fusion), kind=kOutput, calls=%fused_computation.8 | convolution fusion | flops 3019898880 | bytes 37486592 | tf_op jit(solution)/shard_map/tbxmd,xdf->tbxmf/dot_general | solution.py:120
  138.3 13.9 %fusion.32 = bf16[2,32,16,2,256]{4,1,3,0,2:T(8,128)(2,1)S(1)} fusion(bf16[16,2880,256]{2,1,0:T(8,128)(2,1)} %param.20, bf16[2,32,16,2,2880]{4,2,3,1,0:T(8,128)(2,1)} %convolution_convert_fusion, f32[16,2,32,2,256]{4,2,3,1,0:T(8,128)S(1)} %fusion.4), kind=kOutput, calls=%fused_computation.36 | convolution fusion | flops 3024093184 | bytes 38535168 | tf_op jit(solution)/shard_map/tbxmd,xdf->tbxmf/dot_general | solution.py:119
  152.3 23.1 %convert_bitcast_fusion = bf16[2,32,16,2,2880]{4,1,3,0,2:T(8,128)(2,1)} fusion(bf16[2,32,16,2,256]{4,1,3,0,2:T(8,128)(2,1)S(1)} %fusion.32, bf16[16,256,2880]{1,2,0:T(8,128)(2,1)} %param.22), kind=kOutput, calls=%fused_computation.13 | convolution fusion | flops 3025797120 | bytes 36438016 | tf_op jit(solution)/shard_map/tbxmf,xfd->tbxmd/dot_general | solution.py:124
  175.3 17.9 %bitcast_convert_fusion = bf16[2,32,16,2880]{3,2,1,0:T(8,128)(2,1)S(1)} fusion(bf16[2,32,16,2,2880]{4,1,3,0,2:T(8,128)(2,1)} %convert_bitcast_fusion, bf16[2,32,16,16]{3,2,1,0:T(8,128)(2,1)S(1)} %copy.132, s32[2,32,16,16]{3,2,1,0:T(8,128)S(1)} %copy.129, pred[2,32,16,16]{3,2,1,0:T(8,128)(4,1)S(1)} %copy.128), kind=kOutput, calls=%fused_computation.10 | convolution fusion | flops 191791104 | bytes 17809408 | tf_op jit(solution)/shard_map/tbrxm,tbxmd->tbrd/dot_general | solution.py:146
  193.2 3.1 %copy.137 = bf16[2,8,4,16,2880]{4,3,0,2,1:T(8,128)(2,1)} copy(bf16[2,8,4,16,2880]{4,3,2,1,0:T(8,128)(2,1)S(1)} %bitcast.96) | data formatting | bytes 11796480 | tf_op jit(solution)/shard_map/reshape | solution.py:150
  196.4 59.4 %reduce-scatter.3.cloned.1.call-done = bf16[2,1,4,16,2880]{4,3,0,2,1:T(8,128)(2,1)} async-done(((bf16[2,8,4,16,2880]{4,3,0,2,1:T(8,128)(2,1)}), bf16[2,1,4,16,2880]{4,3,0,2,1:T(8,128)(2,1)}) %reduce-scatter.3.cloned.1.call-update) | async-done | bytes 737296 | tf_op jit(solution)/shard_map/reduce_scatter | solution.py:149
  255.8 25.4 %reduce-scatter.5.cloned.1.call-done = bf16[2,1,16,2880]{3,2,0,1:T(8,128)(2,1)} async-done(((bf16[2,4,16,2880]{3,2,0,1:T(8,128)(2,1)}), bf16[2,1,16,2880]{3,2,0,1:T(8,128)(2,1)}) %reduce-scatter.5.cloned.1.call-update) | async-done | bytes 184336 | tf_op jit(solution)/shard_map/reduce_scatter | solution.py:152
  281.2 1.6 fusion.60
  (89 shorter events, 14.8 us)
Async XLA Ops:
  7.2 4.0 %copy-start = (bf16[2880,64]{0,1:T(8,128)(2,1)S(1)}, bf16[2880,64]{0,1:T(8,128)(2,1)}, u32[]{:S(2)}) copy-start(bf16[2880,64]{0,1:T(8,128)(2,1)} %param.18) | copy-start | bytes 1105924
  7.2 78.2 %all-gather.3.cloned.1.call-start = ((), (), s32[]{:S(2)}) async-start(), calls=%async_computation.6 | async-start | bytes 6217728 | tf_op jit(solution)/shard_map/all_gather | solution.py:93
  11.4 8.0 %copy-start.8 = (s32[1,16]{1,0:T(1,128)S(1)}, s32[1,16]{1,0:T(1,128)}, u32[]{:S(2)}) copy-start(s32[1,16]{1,0:T(1,128)} %param.28) | copy-start | bytes 196
  11.4 8.9 %copy-start.4 = (bf16[2,16,4096]{2,1,0:T(8,128)(2,1)S(1)}, bf16[2,16,4096]{2,1,0:T(8,128)(2,1)}, u32[]{:S(2)}) copy-start(bf16[2,16,4096]{2,1,0:T(8,128)(2,1)} %param.23) | copy-start | bytes 786436
  12.9 7.9 %copy-start.6 = (bf16[2,16,512]{2,1,0:T(8,128)(2,1)S(1)}, bf16[2,16,512]{2,1,0:T(8,128)(2,1)}, u32[]{:S(2)}) copy-start(bf16[2,16,512]{2,1,0:T(8,128)(2,1)} %param.24) | copy-start | bytes 98308
  13.0 8.0 %copy-start.7 = (bf16[2,16,512]{2,1,0:T(8,128)(2,1)S(1)}, bf16[2,16,512]{2,1,0:T(8,128)(2,1)}, u32[]{:S(2)}) copy-start(bf16[2,16,512]{2,1,0:T(8,128)(2,1)} %param.25) | copy-start | bytes 98308
  13.0 8.1 %copy-start.2 = (s32[1,32]{1,0:T(1,128)S(1)}, s32[1,32]{1,0:T(1,128)}, u32[]{:S(2)}) copy-start(s32[1,32]{1,0:T(1,128)} %param.29) | copy-start | bytes 388
  14.2 15.0 %all-to-all-start.1 = ((bf16[8,4,16,512]{3,2,1,0:T(8,128)(2,1)}), bf16[8,4,16,512]{3,2,1,0:T(8,128)(2,1)S(1)}, u32[]{:S(2)}, u32[]{:S(2)}) async-start(bf16[8,4,16,512]{3,2,1,0:T(8,128)(2,1)} %param.26), calls=%async_computation.1 | async-start | bytes 1048576 | tf_op jit(solution)/shard_map/all_to_all | solution.py:173
  29.3 13.2 %all-to-all-start = ((bf16[8,4,16,512]{3,2,1,0:T(8,128)(2,1)}), bf16[8,4,16,512]{3,2,1,0:T(8,128)(2,1)S(1)}, u32[]{:S(2)}, u32[]{:S(2)}) async-start(bf16[8,4,16,512]{3,2,1,0:T(8,128)(2,1)} %param.27), calls=%async_computation | async-start | bytes 1048576 | tf_op jit(solution)/shard_map/all_to_all | solution.py:174
  32.8 223.0 %reduce-scatter.3.cloned.1.call-start = ((), (), s32[]{:S(2)}) async-start(), calls=%async_computation.4 | async-start | bytes 6782976 | tf_op jit(solution)/shard_map/reduce_scatter | solution.py:149
  61.5 8.0 %slice-start = ((s8[5242880]{0:T(1024)(128)(4,1)}), s8[4194304]{0:T(1024)(128)(4,1)S(1)}, s32[]{:S(2)}) async-start(s8[5242880]{0:T(1024)(128)(4,1)} %bitcast.99), calls=%async_computation.7 | async-start | bytes 8388608
  61.5 6.4 %copy-start.5 = (f32[2,16,8,8,2]{3,4,0,2,1:T(2,128)S(1)}, f32[2,16,8,8,2]{3,4,0,2,1:T(2,128)}, u32[]{:S(2)}) copy-start(f32[2,16,8,8,2]{3,4,0,2,1:T(2,128)} %get-tuple-element.18) | copy-start | bytes 49156
  61.5 8.0 %slice-start.1 = ((s8[5242880]{0:T(1024)(128)(4,1)}), s8[1048576]{0:T(1024)(128)(4,1)S(1)}, s32[]{:S(2)}) async-start(s8[5242880]{0:T(1024)(128)(4,1)} %bitcast.99), calls=%async_computation.8 | async-start | bytes 2097152
  196.3 86.5 %copy-start.1 = (bf16[2880,64]{0,1:T(8,128)(2,1)S(1)}, bf16[2880,64]{0,1:T(8,128)(2,1)}, u32[]{:S(2)}) copy-start(bf16[2880,64]{0,1:T(8,128)(2,1)} %param.18) | copy-start | bytes 1105924
  196.3 84.9 %copy-start.3 = (bf16[2,16,2880]{2,1,0:T(8,128)(2,1)S(1)}, bf16[2,16,2880]{2,1,0:T(8,128)(2,1)}, u32[]{:S(2)}) copy-start(bf16[2,16,2880]{2,1,0:T(8,128)(2,1)} %param.16) | copy-start | bytes 552964
  196.3 84.8 %reduce-scatter.5.cloned.1.call-start = ((), (), s32[]{:S(2)}) async-start(), calls=%async_computation.5 | async-start | bytes 942080 | tf_op jit(solution)/shard_map/reduce_scatter | solution.py:152
Sparse Core Ops, SparseCore 0:
  14.4 70.9 all-gather.2
  196.4 59.2 reduce-scatter.2
  258.2 22.9 reduce-scatter.4

commit v4 on v3

--- a/solution.py
+++ b/solution.py
@@ -99,7 +99,8 @@
     n_dp = lax.axis_size("dp")
     n_ex = lax.axis_size("expert")
     local_experts = w_gate.shape[0]
-    all_rows = gathered[..., :model_width]
+    blocks = n_dp * n_ex
+    all_rows = gathered[..., :model_width].reshape(steps * blocks * rows, model_width)
     all_gates = gathered[..., model_width : model_width + topk]
     all_ids = jnp.round(gathered[..., model_width + topk : model_width + 2 * topk]).astype(jnp.int32)
     first = lax.axis_index("expert") * local_experts
@@ -109,48 +110,57 @@
     gate_of = jnp.sum(jnp.where(matches, all_gates[..., None].astype(jnp.float32), 0.0), axis=-2)
     earlier = jnp.cumsum(picked, axis=2) - picked
     ranks = jnp.arange(MOST, dtype=jnp.int32)
-    sender = (picked[..., None] > 0) & (earlier[..., None] == ranks)
-    slots = jnp.einsum(
-        "tbrxm,tbrd->tbxmd",
-        sender.astype(jnp.bfloat16),
-        all_rows,
-        preferred_element_type=jnp.float32,
-    ).astype(jnp.bfloat16)
-    gate_part = jnp.einsum("tbxmd,xdf->tbxmf", slots, w_gate, preferred_element_type=jnp.float32)
-    up_part = jnp.einsum("tbxmd,xdf->tbxmf", slots, w_up, preferred_element_type=jnp.float32)
+    sender = ((picked[..., None] > 0) & (earlier[..., None] == ranks)).astype(jnp.int32)
+    row_no = jnp.arange(rows, dtype=jnp.int32)[:, None, None]
+    slot_row = jnp.sum(sender * row_no, axis=2)
+    slot_gate = jnp.sum(sender.astype(jnp.float32) * gate_of[..., None], axis=2)
+    base = (jnp.arange(steps * blocks, dtype=jnp.int32) * rows).reshape(steps, blocks, 1, 1)
+    slot_src = jnp.transpose(slot_row + base, (2, 0, 1, 3)).reshape(-1)
+    slot_w = jnp.transpose(slot_gate, (2, 0, 1, 3)).reshape(-1).astype(jnp.bfloat16)
+    slots = jnp.take(all_rows, slot_src, axis=0).reshape(local_experts, -1, model_width)
+    gate_part = jnp.einsum("xsd,xdf->xsf", slots, w_gate, preferred_element_type=jnp.float32)
+    up_part = jnp.einsum("xsd,xdf->xsf", slots, w_up, preferred_element_type=jnp.float32)
     hidden_act = ((up_part + 1.0) * gate_part * jax.nn.sigmoid(1.702 * gate_part)).astype(
         jnp.bfloat16
     )
     partial = jnp.einsum(
-        "tbxmf,xfd->tbxmd", hidden_act, w_down, preferred_element_type=jnp.float32
+        "xsf,xfd->xsd", hidden_act, w_down, preferred_element_type=jnp.float32
     ).astype(jnp.bfloat16)
-    weights = jnp.where(sender, gate_of[..., None], 0.0).astype(jnp.bfloat16)
-    grid = (steps, n_dp, n_ex)
+    partial = partial.reshape(-1, model_width)
     if local_experts * MOST < rows:
-        summed = lax.psum_scatter(
-            partial.astype(jnp.float32).reshape(grid + partial.shape[2:]),
-            "dp",
-            scatter_dimension=1,
-            tiled=True,
-        )[:, 0]
+        slot_terms = partial.astype(jnp.float32).reshape(local_experts, steps, n_dp, n_ex, MOST, model_width)
+        slot_terms = lax.psum_scatter(slot_terms, "dp", scatter_dimension=2, tiled=True)[:, :, 0]
         own = lax.axis_index("dp")
-        own_weights = lax.dynamic_index_in_dim(weights.reshape(grid + weights.shape[2:]), own, 1, False)
+        own_sender = sender.reshape(steps, n_dp, n_ex, rows, local_experts, MOST)
+        own_sender = lax.dynamic_index_in_dim(own_sender, own, 1, False)
+        own_gate = lax.dynamic_index_in_dim(slot_gate.reshape(steps, n_dp, n_ex, local_experts, MOST), own, 1, False)
+        own_weights = own_sender.astype(jnp.float32) * own_gate[:, :, None]
         row_terms = jnp.einsum(
-            "terxm,texmd->terd",
-            own_weights.astype(jnp.float32),
-            summed,
+            "terxm,xtemd->terd",
+            own_weights,
+            slot_terms,
             precision=lax.Precision.HIGHEST,
             preferred_element_type=jnp.float32,
         )
+        branch_out = lax.psum_scatter(row_terms, "expert", scatter_dimension=1, tiled=True)[:, 0]
     else:
-        row_terms = jnp.einsum(
-            "tbrxm,tbxmd->tbrd", weights, partial, preferred_element_type=jnp.float32
-        ).astype(jnp.bfloat16)
-        row_terms = lax.psum_scatter(
-            row_terms.reshape(grid + row_terms.shape[2:]), "dp", scatter_dimension=1, tiled=True
-        )[:, 0]
-    branch_out = lax.psum_scatter(row_terms, "expert", scatter_dimension=1, tiled=True)
-    return (residual + branch_out[:, 0].astype(jnp.float32)).astype(jnp.bfloat16)
+        q = jnp.arange(n_dp * n_ex * steps * rows, dtype=jnp.int32).reshape(n_dp, n_ex, steps, rows)
+        q_src = (
+            jnp.arange(steps, dtype=jnp.int32)[None, None, :, None] * (blocks * rows)
+            + (jnp.arange(n_dp, dtype=jnp.int32)[:, None, None, None] * n_ex
+               + jnp.arange(n_ex, dtype=jnp.int32)[None, :, None, None]) * rows
+            + jnp.arange(rows, dtype=jnp.int32)[None, None, None, :]
+        ) + 0 * q
+        spread = jnp.where(
+            slot_src[:, None] == q_src.reshape(1, -1),
+            slot_w[:, None],
+            jnp.zeros((), jnp.bfloat16),
+        )
+        row_terms = jnp.einsum("sq,sd->qd", spread, partial, preferred_element_type=jnp.float32)
+        row_terms = row_terms.reshape(n_dp, n_ex, steps, rows, model_width)
+        row_terms = lax.psum_scatter(row_terms, "dp", scatter_dimension=0, tiled=True)[0]
+        branch_out = lax.psum_scatter(row_terms, "expert", scatter_dimension=0, tiled=True)[0]
+    return (residual + branch_out).astype(jnp.bfloat16)
 
 
 def body(

time: 295 us -> 365 us (1.24)
  local copies, waits for them, and re-layouts: 55.1 us -> 111 us
  waiting for transfers between devices: 108 us -> 147 us
  matrix products: 91.2 us -> 68.3 us
    gather x0 -> x2, local copies, waits for them, and re-layouts: none -> 40.9 us  [moe_finish(): jnp.take(all_rows, slot_src, axis=0).reshape(local_experts, -1, model_width)]
    reduce_scatter x2, waiting for transfers between devices: 84.8 us -> 125 us  [the longest x1 88.7 us: moe_finish(): lax.psum_scatter(row_terms, 'dp', scatter_dimension=0, tiled=True)[0]]
    dot_general x5 -> x3, matrix products: 79.3 us -> 56.3 us  [the longest x1 24.6 us: moe_finish(): jnp.einsum('xsf,xfd->xsd', hidden_act, w_down, preferred_element_type=jnp...]
    convert_element_type x0 -> x3, local copies, waits for them, and re-layouts: none -> 16.8 us  [the longest x1 16.2 us: moe_finish(): partial = jnp.einsum('xsf,xfd->xsd', hidden_act, w_down, preferred_elemen...]
  transfers between devices with their start and end apart: 5 -> 5, of which waited for: 5 -> 5; matrix products, arithmetic and copies ran while one was open for 14% -> 11% of each run, Pallas kernels for 0% -> 0%
where the time goes in v4:
time: 365 us; the launch traced here: 363 us
  waiting for transfers between devices  147 us (40%)
  local copies, waits for them, and re-layouts  111 us (30%)
  matrix products  68.3 us (19%)
  between operations  14.2 us (4%)
  other arithmetic  13.7 us (4%)
  starting transfers between devices  8.8 us (2%)
    reduce_scatter x1, waiting for transfers between devices, moe_finish(): lax.psum_scatter(row_terms, 'dp', scatter_dimension=0, tiled=True)[0]  88.7 us
    gather x2, local copies, waits for them, and re-layouts, moe_finish(): jnp.take(all_rows, slot_src, axis=0).reshape(local_experts, -1, model_width)  40.9 us
    reduce_scatter x1, waiting for transfers between devices, moe_finish(): lax.psum_scatter(row_terms, 'expert', scatter_dimension=0, tiled=True)[0]  36.6 us
    optimization_barrier x1, local copies, waits for them, and re-layouts, body(): gathered, context = lax.optimization_barrier((gathered, context))  26 us
    dot_general x1, matrix products, moe_finish(): jnp.einsum('xsf,xfd->xsd', hidden_act, w_down, preferred_element_type=jnp...  24.6 us
    dot_general x1, matrix products, moe_finish(): jnp.einsum('sq,sd->qd', spread, partial, preferred_element_type=jnp.float32)  17.8 us
    convert_element_type x1, local copies, waits for them, and re-layouts, moe_finish(): partial = jnp.einsum('xsf,xfd->xsd', hidden_act, w_down, preferred_elemen...  16.2 us
    dot_general x1, matrix products, moe_finish(): jnp.einsum('xsd,xdf->xsf', slots, w_gate, preferred_element_type=jnp.floa...  13.9 us
  transfers between devices with their start and end apart: 5, of which 5 were waited for; matrix products, arithmetic and copies ran while one was open for 11% of the time, Pallas kernels for 0%

profile of v4, /device:TPU:0, one launch (start us, length us, event | category | flops | bytes accessed | tf_op | source)
XLA Modules:
  0.0 362.8 jit_solution(5975666577565036751)
XLA Ops:
  11.4 1.5 gather_fusion.2
  14.2 5.2 %all-to-all-start.1 = ((bf16[8,4,16,512]{3,2,1,0:T(8,128)(2,1)}), bf16[8,4,16,512]{3,2,1,0:T(8,128)(2,1)S(1)}, u32[]{:S(2)}, u32[]{:S(2)}) async-start(bf16[8,4,16,512]{3,2,1,0:T(8,128)(2,1)} %param.26), calls=%async_computation.1 | async-start | bytes 1048576 | tf_op jit(solution)/shard_map/all_to_all | solution.py:183
  20.3 1.6 gather_fusion
  24.1 5.2 %all-to-all-done.1 = bf16[8,4,16,512]{3,2,1,0:T(8,128)(2,1)S(1)} async-done(((bf16[8,4,16,512]{3,2,1,0:T(8,128)(2,1)}), bf16[8,4,16,512]{3,2,1,0:T(8,128)(2,1)S(1)}, u32[]{:S(2)}, u32[]{:S(2)}) %all-to-all-start.1) | async-done | bytes 524320 | tf_op jit(solution)/shard_map/all_to_all | solution.py:183
  29.2 3.5 all-to-all-start
  32.8 3.2 fusion.55
  36.1 2.5 gather_fusion.4
  38.5 3.9 %all-to-all-done = bf16[8,4,16,512]{3,2,1,0:T(8,128)(2,1)S(1)} async-done(((bf16[8,4,16,512]{3,2,1,0:T(8,128)(2,1)}), bf16[8,4,16,512]{3,2,1,0:T(8,128)(2,1)S(1)}, u32[]{:S(2)}, u32[]{:S(2)}) %all-to-all-start) | async-done | bytes 524320 | tf_op jit(solution)/shard_map/all_to_all | solution.py:184
  42.4 2.5 gather_fusion.3
  44.9 4.0 %broadcast_select_fusion.3 = (bf16[160,16,512]{2,1,0:T(8,128)(2,1)S(1)}, bf16[160,16,512]{2,1,0:T(8,128)(2,1)}) fusion(bf16[160,16,512]{2,1,0:T(8,128)(2,1)} %gather_fusion.4, pred[160]{0:T(512)(128)(4,1)S(1)} %copy-done.10, bf16[160,16,512]{2,1,0:T(8,128)(2,1)} %gather_fusion.3), kind=kLoop, calls=%fused_computation.19 | loop fusion | flops 2621440 | bytes 10485920 | tf_op jit(solution)/shard_map/jit(_take)/select_n | solution.py:29
  48.9 7.5 %reshape.404 = bf16[16,160,8,64]{3,2,1,0:T(8,128)(2,1)} reshape(bf16[160,16,512]{2,1,0:T(8,128)(2,1)} %get-tuple-element.14) | data formatting | bytes 5242880 | tf_op jit(solution)/shard_map/reshape | solution.py:32
  56.4 4.6 %reshape.406 = bf16[16,160,8,64]{3,2,1,0:T(8,128)(2,1)} reshape(bf16[160,16,512]{2,1,0:T(8,128)(2,1)S(1)} %get-tuple-element.13) | data formatting | bytes 5242880 | tf_op jit(solution)/shard_map/reshape | solution.py:29
  61.0 6.4 %bitcast_reduce_fusion = (f32[2,16,8,8]{3,0,2,1:T(2,128)S(1)}, f32[16,8,160,2,8]{2,4,3,1,0:T(8,128)S(1)}) fusion(pred[16,160]{1,0:T(8,128)(4,1)S(1)} %iota_compare_fusion.1, bf16[2,16,8,8,64]{4,3,2,1,0:T(8,128)(2,1)S(1)} %reshape.407, bf16[16,160,8,64,1]{3,2,1,0,4:T(8,128)(2,1)} %bitcast.88), kind=kOutput, calls=%fused_computation.22 | convolution fusion | flops 42924032 | bytes 4205056 | tf_op jit(solution)/shard_map/trkgh,rlkh->trkgl/dot_general | solution.py:41
  72.6 12.8 %all-gather.3.cloned.1.call-done = bf16[2,512,2944]{2,1,0:T(8,128)(2,1)} async-done(((bf16[2,16,2944]{2,1,0:T(8,128)(2,1)}), bf16[2,512,2944]{2,1,0:T(8,128)(2,1)}) %all-gather.3.cloned.1.call-update) | async-done | bytes 6029328 | tf_op jit(solution)/shard_map/all_gather | solution.py:93
  85.4 26.0 %copy.128 = bf16[2,32,16,2944]{1,2,3,0:T(8,128)(2,1)} copy(bf16[2,32,16,2944]{3,2,1,0:T(8,128)(2,1)} %bitcast.81) | data formatting | bytes 12058624 | tf_op jit(solution)/shard_map/optimization_barrier | solution.py:193
  114.6 25.6 %gather_fusion.1 = bf16[2048,2880]{1,0:T(8,128)(2,1)} fusion(bf16[1024,2880]{1,0:T(8,128)(2,1)} %bitcast.82, s32[2048]{0:T(1024)S(1)} %broadcast_clamp_fusion), kind=kCustom, calls=%fused_computation.3 | custom fusion | bytes 23601152 | tf_op jit(solution)/shard_map/jit(_take)/gather | solution.py:120
  140.1 15.4 %copy.140 = bf16[16,128,2880]{1,2,0:T(8,128)(2,1)} copy(bf16[16,128,2880]{2,1,0:T(8,128)(2,1)} %bitcast.83) | data formatting | bytes 23592960 | tf_op jit(solution)/shard_map/jit(_take)/gather | solution.py:120
  155.6 13.9 %fusion = f32[16,128,256]{2,1,0:T(8,128)S(1)} fusion(bf16[16,2880,256]{2,1,0:T(8,128)(2,1)} %param.20, bf16[16,128,2880]{1,2,0:T(8,128)(2,1)} %copy.140, pred[16,128]{1,0:T(8,128)(4,1)S(1)} %copy.138), kind=kOutput, calls=%fused_computation.6 | convolution fusion | flops 3025797120 | bytes 37488640 | tf_op jit(solution)/shard_map/xsd,xdf->xsf/dot_general | solution.py:121
  169.5 24.6 %convolution_convert_fusion = bf16[16,128,2880]{1,2,0:T(8,128)(2,1)} fusion(bf16[16,256,2880]{1,2,0:T(8,128)(2,1)} %param.22, f32[16,128,256]{2,1,0:T(8,128)S(1)} %fusion, bf16[16,2880,256]{2,1,0:T(8,128)(2,1)} %param.21, bf16[16,128,2880]{1,2,0:T(8,128)(2,1)} %copy.140, pred[16,128]{1,0:T(8,128)(4,1)S(1)} %copy.138), kind=kOutput, calls=%fused_computation.9 | convolution fusion | flops 6055788544 | bytes 72878080 | tf_op jit(solution)/shard_map/xsf,xfd->xsd/dot_general | solution.py:126
  194.1 16.2 %copy.141 = bf16[16,128,2880]{2,1,0:T(8,128)(2,1)} copy(bf16[16,128,2880]{1,2,0:T(8,128)(2,1)} %convolution_convert_fusion) | data formatting | bytes 23592960 | tf_op jit(solution)/shard_map/convert_element_type | solution.py:128
  211.3 17.8 %fusion.8 = f32[8,4,2,16,2880]{4,3,2,1,0:T(8,128)} fusion(bf16[2048,2880,1,1,1]{1,0,4,3,2:T(8,128)(2,1)} %bitcast.86, s32[8,4,2,16]{3,2,1,0:T(2,128)S(1)} %iota_add_fusion, s32[2048]{0:T(1024)S(1)} %eq.55, bf16[2048]{0:T(1024)(128)(2,1)S(1)} %convert_element_type.88), kind=kOutput, calls=%fused_computation.16 | convolution fusion | flops 12083789824 | bytes 23609344 | tf_op jit(solution)/shard_map/sq,sd->qd/dot_general | solution.py:159
  229.2 88.7 %reduce-scatter.3.cloned.1.call-done = f32[1,4,2,16,2880]{4,3,2,1,0:T(8,128)} async-done(((f32[8,4,2,16,2880]{4,3,2,1,0:T(8,128)}), f32[1,4,2,16,2880]{4,3,2,1,0:T(8,128)}) %reduce-scatter.3.cloned.1.call-update) | async-done | bytes 1474576 | tf_op jit(solution)/shard_map/reduce_scatter | solution.py:161
  318.0 36.6 %reduce-scatter.5.cloned.1.call-done = f32[1,2,16,2880]{3,2,1,0:T(8,128)} async-done(((f32[4,2,16,2880]{3,2,1,0:T(8,128)}), f32[1,2,16,2880]{3,2,1,0:T(8,128)}) %reduce-scatter.5.cloned.1.call-update) | async-done | bytes 368656 | tf_op jit(solution)/shard_map/reduce_scatter | solution.py:162
  354.5 1.7 fusion.37
  (108 shorter events, 17.9 us)
Async XLA Ops:
  7.2 4.0 %copy-start = (bf16[2880,64]{0,1:T(8,128)(2,1)S(1)}, bf16[2880,64]{0,1:T(8,128)(2,1)}, u32[]{:S(2)}) copy-start(bf16[2880,64]{0,1:T(8,128)(2,1)} %param.18) | copy-start | bytes 1105924
  7.2 78.2 %all-gather.3.cloned.1.call-start = ((), (), s32[]{:S(2)}) async-start(), calls=%async_computation.6 | async-start | bytes 6217728 | tf_op jit(solution)/shard_map/all_gather | solution.py:93
  11.4 8.0 %copy-start.9 = (s32[1,16]{1,0:T(1,128)S(1)}, s32[1,16]{1,0:T(1,128)}, u32[]{:S(2)}) copy-start(s32[1,16]{1,0:T(1,128)} %param.28) | copy-start | bytes 196
  12.9 7.3 %copy-start.2 = (s32[1,32]{1,0:T(1,128)S(1)}, s32[1,32]{1,0:T(1,128)}, u32[]{:S(2)}) copy-start(s32[1,32]{1,0:T(1,128)} %param.29) | copy-start | bytes 388
  14.2 15.0 %all-to-all-start.1 = ((bf16[8,4,16,512]{3,2,1,0:T(8,128)(2,1)}), bf16[8,4,16,512]{3,2,1,0:T(8,128)(2,1)S(1)}, u32[]{:S(2)}, u32[]{:S(2)}) async-start(bf16[8,4,16,512]{3,2,1,0:T(8,128)(2,1)} %param.26), calls=%async_computation.1 | async-start | bytes 1048576 | tf_op jit(solution)/shard_map/all_to_all | solution.py:183
  20.3 2.8 copy-start.5
  20.3 3.4 copy-start.7
  20.3 3.5 copy-start.8
  29.2 13.2 %all-to-all-start = ((bf16[8,4,16,512]{3,2,1,0:T(8,128)(2,1)}), bf16[8,4,16,512]{3,2,1,0:T(8,128)(2,1)S(1)}, u32[]{:S(2)}, u32[]{:S(2)}) async-start(bf16[8,4,16,512]{3,2,1,0:T(8,128)(2,1)} %param.27), calls=%async_computation | async-start | bytes 1048576 | tf_op jit(solution)/shard_map/all_to_all | solution.py:184
  32.7 285.2 %reduce-scatter.3.cloned.1.call-start = ((), (), s32[]{:S(2)}) async-start(), calls=%async_computation.4 | async-start | bytes 13565952 | tf_op jit(solution)/shard_map/reduce_scatter | solution.py:161
  36.0 8.8 %copy-start.10 = (pred[160]{0:T(512)(128)(4,1)S(1)}, pred[160]{0:T(512)(128)(4,1)}, u32[]{:S(2)}) copy-start(pred[160]{0:T(512)(128)(4,1)} %get-tuple-element.7) | copy-start | bytes 484
  60.9 6.5 %copy-start.6 = (f32[2,16,8,8,2]{3,4,0,2,1:T(2,128)S(1)}, f32[2,16,8,8,2]{3,4,0,2,1:T(2,128)}, u32[]{:S(2)}) copy-start(f32[2,16,8,8,2]{3,4,0,2,1:T(2,128)} %get-tuple-element.18) | copy-start | bytes 49156
  61.0 8.2 %copy-start.3 = (bf16[16,160,8,64]{3,2,1,0:T(8,128)(2,1)S(1)}, bf16[16,160,8,64]{3,2,1,0:T(8,128)(2,1)}, u32[]{:S(2)}) copy-start(bf16[16,160,8,64]{3,2,1,0:T(8,128)(2,1)} %reshape.404) | copy-start | bytes 7864324
  85.4 28.2 %copy-start.11 = (s32[2,32]{1,0:T(2,128)S(1)}, s32[2,32]{1,0:T(2,128)}, u32[]{:S(2)}) copy-start(s32[2,32]{1,0:T(2,128)} %add_multiply_fusion.1) | copy-start | bytes 772
  229.2 127.1 %copy-start.1 = (bf16[2880,64]{0,1:T(8,128)(2,1)S(1)}, bf16[2880,64]{0,1:T(8,128)(2,1)}, u32[]{:S(2)}) copy-start(bf16[2880,64]{0,1:T(8,128)(2,1)} %param.18) | copy-start | bytes 1105924
  229.2 125.4 %copy-start.4 = (bf16[2,16,2880]{2,1,0:T(8,128)(2,1)S(1)}, bf16[2,16,2880]{2,1,0:T(8,128)(2,1)}, u32[]{:S(2)}) copy-start(bf16[2,16,2880]{2,1,0:T(8,128)(2,1)} %param.16) | copy-start | bytes 552964
  229.2 125.3 %reduce-scatter.5.cloned.1.call-start = ((), (), s32[]{:S(2)}) async-start(), calls=%async_computation.5 | async-start | bytes 1884160 | tf_op jit(solution)/shard_map/reduce_scatter | solution.py:162
Sparse Core Ops, SparseCore 0:
  14.3 71.0 all-gather.2
  229.3 88.5 reduce-scatter.2
  320.3 34.2 reduce-scatter.4

commit v5 on v3

--- a/solution.py
+++ b/solution.py
@@ -94,14 +94,14 @@
     return gathered, residual
 
 
-def moe_finish(gathered, residual, topk, w_gate, w_up, w_down):
+def moe_finish(gathered, meta, residual, topk, w_gate, w_up, w_down):
     steps, rows, model_width = residual.shape
     n_dp = lax.axis_size("dp")
     n_ex = lax.axis_size("expert")
     local_experts = w_gate.shape[0]
     all_rows = gathered[..., :model_width]
-    all_gates = gathered[..., model_width : model_width + topk]
-    all_ids = jnp.round(gathered[..., model_width + topk : model_width + 2 * topk]).astype(jnp.int32)
+    all_gates = meta[..., :topk]
+    all_ids = jnp.round(meta[..., topk : 2 * topk]).astype(jnp.int32)
     first = lax.axis_index("expert") * local_experts
     numbers = first + jnp.arange(local_experts, dtype=jnp.int32)
     matches = all_ids[..., None] == numbers
@@ -110,12 +110,16 @@
     earlier = jnp.cumsum(picked, axis=2) - picked
     ranks = jnp.arange(MOST, dtype=jnp.int32)
     sender = (picked[..., None] > 0) & (earlier[..., None] == ranks)
+    groups = steps * n_dp * n_ex
+    slot_count = local_experts * MOST
+    sender_t = jnp.transpose(sender.reshape(groups, rows, slot_count), (0, 2, 1))
     slots = jnp.einsum(
-        "tbrxm,tbrd->tbxmd",
-        sender.astype(jnp.bfloat16),
-        all_rows,
+        "gsr,grd->gsd",
+        sender_t.astype(jnp.bfloat16),
+        all_rows.reshape(groups, rows, model_width),
         preferred_element_type=jnp.float32,
     ).astype(jnp.bfloat16)
+    slots = slots.reshape(steps, n_dp * n_ex, local_experts, MOST, model_width)
     gate_part = jnp.einsum("tbxmd,xdf->tbxmf", slots, w_gate, preferred_element_type=jnp.float32)
     up_part = jnp.einsum("tbxmd,xdf->tbxmf", slots, w_up, preferred_element_type=jnp.float32)
     hidden_act = ((up_part + 1.0) * gate_part * jax.nn.sigmoid(1.702 * gate_part)).astype(
@@ -144,13 +148,14 @@
         )
     else:
         row_terms = jnp.einsum(
-            "tbrxm,tbxmd->tbrd", weights, partial, preferred_element_type=jnp.float32
-        ).astype(jnp.bfloat16)
+            "tbrxm,tbxmd->btrd", weights, partial, preferred_element_type=jnp.float32
+        )
         row_terms = lax.psum_scatter(
-            row_terms.reshape(grid + row_terms.shape[2:]), "dp", scatter_dimension=1, tiled=True
-        )[:, 0]
+            row_terms.reshape((n_dp, n_ex) + row_terms.shape[1:]), "dp", scatter_dimension=0, tiled=True
+        )[0]
+        row_terms = jnp.moveaxis(row_terms, 0, 1)
     branch_out = lax.psum_scatter(row_terms, "expert", scatter_dimension=1, tiled=True)
-    return (residual + branch_out[:, 0].astype(jnp.float32)).astype(jnp.bfloat16)
+    return (residual + branch_out[:, 0]).astype(jnp.bfloat16)
 
 
 def body(
@@ -180,8 +185,9 @@
     context = attention(
         queries, new_key, new_value, space_keys, space_values, page_counts[0], page_order[0]
     )
-    gathered, context = lax.optimization_barrier((gathered, context))
-    layer_out = moe_finish(gathered, residual, routes.shape[-1], w_gate, w_up, w_down)
+    meta = gathered[..., hidden.shape[-1] :]
+    gathered, meta, context = lax.optimization_barrier((gathered, meta, context))
+    layer_out = moe_finish(gathered, meta, residual, routes.shape[-1], w_gate, w_up, w_down)
     return (context, layer_out)
 
 

time: 295 us -> 336 us (1.14)
  waiting for transfers between devices: 108 us -> 148 us
    reduce_scatter x1, waiting for transfers between devices: 59.4 us -> 88.6 us  [moe_finish(): lax.psum_scatter(row_terms.reshape((n_dp, n_ex) + row_terms.shape[1:]), '...]
    optimization_barrier x1, local copies, waits for them, and re-layouts: 26 us -> 0.53 us  [body(): lax.optimization_barrier((gathered, meta, context))]
    reshape x1, local copies, waits for them, and re-layouts: 3.05 us -> 23.5 us  [moe_finish(): slots = slots.reshape(steps, n_dp * n_ex, local_experts, MOST, model_width)]
    reduce_scatter x1, waiting for transfers between devices: 25.4 us -> 36.6 us  [moe_finish(): lax.psum_scatter(row_terms, 'expert', scatter_dimension=1, tiled=True)]
  transfers between devices with their start and end apart: 5 -> 5, of which waited for: 5 -> 5; matrix products, arithmetic and copies ran while one was open for 14% -> 12% of each run, Pallas kernels for 0% -> 0%
where the time goes in v5:
time: 336 us; the launch traced here: 332 us
  waiting for transfers between devices  148 us (44%)
  matrix products  94.3 us (28%)
  local copies, waits for them, and re-layouts  53.4 us (16%)
  between operations  14.4 us (4%)
  other arithmetic  12.5 us (4%)
  starting transfers between devices  8.98 us (3%)
    reduce_scatter x1, waiting for transfers between devices, moe_finish(): lax.psum_scatter(row_terms.reshape((n_dp, n_ex) + row_terms.shape[1:]), '...  88.6 us
    reduce_scatter x1, waiting for transfers between devices, moe_finish(): lax.psum_scatter(row_terms, 'expert', scatter_dimension=1, tiled=True)  36.6 us
    reshape x1, local copies, waits for them, and re-layouts, moe_finish(): slots = slots.reshape(steps, n_dp * n_ex, local_experts, MOST, model_width)  23.5 us
    dot_general x1, matrix products, moe_finish(): jnp.einsum('tbxmf,xfd->tbxmd', hidden_act, w_down, preferred_element_type...  23.1 us
    dot_general x1, matrix products, moe_finish(): jnp.einsum('tbrxm,tbxmd->btrd', weights, partial, preferred_element_type=...  22 us
    dot_general x1, matrix products, moe_finish(): jnp.einsum('tbxmd,xdf->tbxmf', slots, w_gate, preferred_element_type=jnp....  14.7 us
    dot_general x1, matrix products, moe_finish(): jnp.einsum('tbxmd,xdf->tbxmf', slots, w_up, preferred_element_type=jnp.fl...  14.5 us
    all_gather x1, waiting for transfers between devices, moe_layer(): gathered = lax.all_gather(payload, ('dp', 'expert'), axis=1, tiled=False)  12.7 us
  transfers between devices with their start and end apart: 5, of which 5 were waited for; matrix products, arithmetic and copies ran while one was open for 12% of the time, Pallas kernels for 0%

profile of v5, /device:TPU:0, one launch (start us, length us, event | category | flops | bytes accessed | tf_op | source)
XLA Modules:
  0.0 331.7 jit_solution(5167508493009530030)
XLA Ops:
  11.5 1.5 gather_fusion.1
  14.2 5.2 %all-to-all-start = ((bf16[8,4,16,512]{3,2,1,0:T(8,128)(2,1)}), bf16[8,4,16,512]{3,2,1,0:T(8,128)(2,1)S(1)}, u32[]{:S(2)}, u32[]{:S(2)}) async-start(bf16[8,4,16,512]{3,2,1,0:T(8,128)(2,1)} %param.27), calls=%async_computation | async-start | bytes 1048576 | tf_op jit(solution)/shard_map/all_to_all | solution.py:179
  21.2 1.6 gather_fusion
  22.8 6.5 %all-to-all-done = bf16[8,4,16,512]{3,2,1,0:T(8,128)(2,1)S(1)} async-done(((bf16[8,4,16,512]{3,2,1,0:T(8,128)(2,1)}), bf16[8,4,16,512]{3,2,1,0:T(8,128)(2,1)S(1)}, u32[]{:S(2)}, u32[]{:S(2)}) %all-to-all-start) | async-done | bytes 524320 | tf_op jit(solution)/shard_map/all_to_all | solution.py:179
  29.3 3.5 %all-to-all-start.1 = ((bf16[8,4,16,512]{3,2,1,0:T(8,128)(2,1)}), bf16[8,4,16,512]{3,2,1,0:T(8,128)(2,1)S(1)}, u32[]{:S(2)}, u32[]{:S(2)}) async-start(bf16[8,4,16,512]{3,2,1,0:T(8,128)(2,1)} %param.26), calls=%async_computation.1 | async-start | bytes 1048576 | tf_op jit(solution)/shard_map/all_to_all | solution.py:178
  33.1 3.2 fusion.60
  36.3 2.5 gather_fusion.2
  38.7 3.7 %all-to-all-done.1 = bf16[8,4,16,512]{3,2,1,0:T(8,128)(2,1)S(1)} async-done(((bf16[8,4,16,512]{3,2,1,0:T(8,128)(2,1)}), bf16[8,4,16,512]{3,2,1,0:T(8,128)(2,1)S(1)}, u32[]{:S(2)}, u32[]{:S(2)}) %all-to-all-start.1) | async-done | bytes 524320 | tf_op jit(solution)/shard_map/all_to_all | solution.py:178
  42.4 2.5 gather_fusion.3
  44.9 4.0 %broadcast_select_fusion = (bf16[160,16,512]{2,1,0:T(8,128)(2,1)}, bf16[160,16,512]{2,1,0:T(8,128)(2,1)S(1)}) fusion(bf16[160,16,512]{2,1,0:T(8,128)(2,1)} %gather_fusion.3, pred[160]{0:T(512)(128)(4,1)S(1)} %get-tuple-element.9, bf16[160,16,512]{2,1,0:T(8,128)(2,1)} %gather_fusion.2), kind=kLoop, calls=%fused_computation.20 | loop fusion | flops 2621440 | bytes 10485920 | tf_op jit(solution)/shard_map/jit(_take)/select_n | solution.py:29
  48.9 7.5 %reshape.277 = bf16[16,160,8,64]{3,2,1,0:T(8,128)(2,1)} reshape(bf16[160,16,512]{2,1,0:T(8,128)(2,1)} %get-tuple-element.15) | data formatting | bytes 5242880 | tf_op jit(solution)/shard_map/reshape | solution.py:29
  56.4 4.6 %reshape.275 = bf16[16,160,8,64]{3,2,1,0:T(8,128)(2,1)} reshape(bf16[160,16,512]{2,1,0:T(8,128)(2,1)S(1)} %get-tuple-element.16) | data formatting | bytes 5242880 | tf_op jit(solution)/shard_map/reshape | solution.py:32
  61.0 6.5 %bitcast_reduce_fusion = (f32[2,16,8,8]{3,0,2,1:T(2,128)S(1)}, f32[16,8,160,2,8]{2,4,3,1,0:T(8,128)S(1)}) fusion(pred[16,160]{1,0:T(8,128)(4,1)S(1)} %iota_compare_fusion, bf16[2,16,8,8,64]{4,3,2,1,0:T(8,128)(2,1)S(1)} %reshape.278, bf16[16,160,8,64,1]{3,2,1,0,4:T(8,128)(2,1)} %bitcast.107), kind=kOutput, calls=%fused_computation.23 | convolution fusion | flops 42924032 | bytes 4205056 | tf_op jit(solution)/shard_map/trkgh,rlkh->trkgl/dot_general | solution.py:41
  69.2 1.5 fusion.28
  72.7 12.7 %all-gather.3.cloned.1.call-done = bf16[2,512,2944]{2,1,0:T(8,128)(2,1)} async-done(((bf16[2,16,2944]{2,1,0:T(8,128)(2,1)}), bf16[2,512,2944]{2,1,0:T(8,128)(2,1)}) %all-gather.3.cloned.1.call-update) | async-done | bytes 6029328 | tf_op jit(solution)/shard_map/all_gather | solution.py:93
  92.2 8.1 %convolution_convert_fusion = bf16[64,32,2880]{2,1,0:T(8,128)(2,1)} fusion(pred[64,16,32]{2,1,0:T(8,128)(4,1)S(1)} %copy.129, bf16[64,16,2880]{2,1,0:T(8,128)(2,1)} %bitcast.101), kind=kOutput, calls=%fused_computation.15 | convolution fusion | flops 194641920 | bytes 17727488 | tf_op jit(solution)/shard_map/gsr,grd->gsd/dot_general | solution.py:116
  100.3 23.5 %reshape.282 = bf16[2,32,16,2,2880]{4,3,2,1,0:T(2,128)(2,1)} reshape(bf16[64,32,2880]{2,1,0:T(8,128)(2,1)} %convolution_convert_fusion) | data formatting | bytes 23592960 | tf_op jit(solution)/shard_map/reshape | solution.py:122
  123.8 14.5 %fusion.4 = f32[16,2,32,2,256]{4,2,3,1,0:T(8,128)S(1)} fusion(bf16[16,2880,256]{2,1,0:T(8,128)(2,1)} %param.21, bf16[2,32,16,2,2880]{4,3,2,1,0:T(2,128)(2,1)} %reshape.282), kind=kOutput, calls=%fused_computation.8 | convolution fusion | flops 3019898880 | bytes 37486592 | tf_op jit(solution)/shard_map/tbxmd,xdf->tbxmf/dot_general | solution.py:124
  138.2 14.7 %fusion.23 = bf16[2,32,16,2,256]{4,1,3,0,2:T(8,128)(2,1)S(1)} fusion(bf16[16,2880,256]{2,1,0:T(8,128)(2,1)} %param.20, bf16[2,32,16,2,2880]{4,3,2,1,0:T(2,128)(2,1)} %reshape.282, f32[16,2,32,2,256]{4,2,3,1,0:T(8,128)S(1)} %fusion.4), kind=kOutput, calls=%fused_computation.29 | convolution fusion | flops 3024093184 | bytes 38535168 | tf_op jit(solution)/shard_map/tbxmd,xdf->tbxmf/dot_general | solution.py:123
  152.9 23.1 %convert_bitcast_fusion = bf16[2,32,16,2,2880]{4,1,3,0,2:T(8,128)(2,1)} fusion(bf16[2,32,16,2,256]{4,1,3,0,2:T(8,128)(2,1)S(1)} %fusion.23, bf16[16,256,2880]{1,2,0:T(8,128)(2,1)} %param.22), kind=kOutput, calls=%fused_computation.12 | convolution fusion | flops 3025797120 | bytes 36438016 | tf_op jit(solution)/shard_map/tbxmf,xfd->tbxmd/dot_general | solution.py:128
  176.0 22.0 %fusion.6 = f32[32,2,16,2880,1]{3,2,4,1,0:T(8,128)} fusion(bf16[2,32,16,16,2]{3,2,4,0,1:T(8,128)(2,1)S(1)} %copy.132, bf16[2,32,16,2,2880]{4,1,3,0,2:T(8,128)(2,1)} %convert_bitcast_fusion), kind=kOutput, calls=%fused_computation.10 | convolution fusion | flops 188743680 | bytes 23658496 | tf_op jit(solution)/shard_map/tbrxm,tbxmd->btrd/dot_general | solution.py:150
  198.0 88.6 %reduce-scatter.3.cloned.1.call-done = f32[1,4,2,16,2880]{4,3,2,1,0:T(8,128)} async-done(((f32[8,4,2,16,2880]{4,3,2,1,0:T(8,128)}), f32[1,4,2,16,2880]{4,3,2,1,0:T(8,128)}) %reduce-scatter.3.cloned.1.call-update) | async-done | bytes 1474576 | tf_op jit(solution)/shard_map/reduce_scatter | solution.py:153
  286.7 36.6 %reduce-scatter.5.cloned.1.call-done = f32[2,1,16,2880]{3,2,0,1:T(8,128)} async-done(((f32[2,4,16,2880]{3,2,0,1:T(8,128)}), f32[2,1,16,2880]{3,2,0,1:T(8,128)}) %reduce-scatter.5.cloned.1.call-update) | async-done | bytes 368656 | tf_op jit(solution)/shard_map/reduce_scatter | solution.py:157
  323.3 1.7 fusion.49
  (100 shorter events, 17.8 us)
Async XLA Ops:
  7.2 4.1 %copy-start = (bf16[2880,64]{0,1:T(8,128)(2,1)S(1)}, bf16[2880,64]{0,1:T(8,128)(2,1)}, u32[]{:S(2)}) copy-start(bf16[2880,64]{0,1:T(8,128)(2,1)} %param.18) | copy-start | bytes 1105924
  7.2 78.2 %all-gather.3.cloned.1.call-start = ((), (), s32[]{:S(2)}) async-start(), calls=%async_computation.6 | async-start | bytes 6217728 | tf_op jit(solution)/shard_map/all_gather | solution.py:93
  11.5 7.9 %copy-start.8 = (s32[1,16]{1,0:T(1,128)S(1)}, s32[1,16]{1,0:T(1,128)}, u32[]{:S(2)}) copy-start(s32[1,16]{1,0:T(1,128)} %param.28) | copy-start | bytes 196
  11.5 8.9 %copy-start.6 = (bf16[2,16,512]{2,1,0:T(8,128)(2,1)S(1)}, bf16[2,16,512]{2,1,0:T(8,128)(2,1)}, u32[]{:S(2)}) copy-start(bf16[2,16,512]{2,1,0:T(8,128)(2,1)} %param.24) | copy-start | bytes 98308
  11.5 9.0 %copy-start.7 = (bf16[2,16,512]{2,1,0:T(8,128)(2,1)S(1)}, bf16[2,16,512]{2,1,0:T(8,128)(2,1)}, u32[]{:S(2)}) copy-start(bf16[2,16,512]{2,1,0:T(8,128)(2,1)} %param.25) | copy-start | bytes 98308
  11.5 9.1 %copy-start.4 = (bf16[2,16,4096]{2,1,0:T(8,128)(2,1)S(1)}, bf16[2,16,4096]{2,1,0:T(8,128)(2,1)}, u32[]{:S(2)}) copy-start(bf16[2,16,4096]{2,1,0:T(8,128)(2,1)} %param.23) | copy-start | bytes 786436
  13.1 8.1 %copy-start.2 = (s32[1,32]{1,0:T(1,128)S(1)}, s32[1,32]{1,0:T(1,128)}, u32[]{:S(2)}) copy-start(s32[1,32]{1,0:T(1,128)} %param.29) | copy-start | bytes 388
  14.2 15.0 %all-to-all-start = ((bf16[8,4,16,512]{3,2,1,0:T(8,128)(2,1)}), bf16[8,4,16,512]{3,2,1,0:T(8,128)(2,1)S(1)}, u32[]{:S(2)}, u32[]{:S(2)}) async-start(bf16[8,4,16,512]{3,2,1,0:T(8,128)(2,1)} %param.27), calls=%async_computation | async-start | bytes 1048576 | tf_op jit(solution)/shard_map/all_to_all | solution.py:179
  29.3 13.2 %all-to-all-start.1 = ((bf16[8,4,16,512]{3,2,1,0:T(8,128)(2,1)}), bf16[8,4,16,512]{3,2,1,0:T(8,128)(2,1)S(1)}, u32[]{:S(2)}, u32[]{:S(2)}) async-start(bf16[8,4,16,512]{3,2,1,0:T(8,128)(2,1)} %param.26), calls=%async_computation.1 | async-start | bytes 1048576 | tf_op jit(solution)/shard_map/all_to_all | solution.py:178
  32.8 253.9 %reduce-scatter.3.cloned.1.call-start = ((), (), s32[]{:S(2)}) async-start(), calls=%async_computation.4 | async-start | bytes 13565952 | tf_op jit(solution)/shard_map/reduce_scatter | solution.py:153
  61.0 8.2 %slice-start = ((s8[5242880]{0:T(1024)(128)(4,1)}), s8[4194304]{0:T(1024)(128)(4,1)S(1)}, s32[]{:S(2)}) async-start(s8[5242880]{0:T(1024)(128)(4,1)} %bitcast.104), calls=%async_computation.7 | async-start | bytes 8388608
  61.0 6.6 %copy-start.5 = (f32[2,16,8,8,2]{3,4,0,2,1:T(2,128)S(1)}, f32[2,16,8,8,2]{3,4,0,2,1:T(2,128)}, u32[]{:S(2)}) copy-start(f32[2,16,8,8,2]{3,4,0,2,1:T(2,128)} %get-tuple-element.20) | copy-start | bytes 49156
  61.0 8.2 %slice-start.1 = ((s8[5242880]{0:T(1024)(128)(4,1)}), s8[1048576]{0:T(1024)(128)(4,1)S(1)}, s32[]{:S(2)}) async-start(s8[5242880]{0:T(1024)(128)(4,1)} %bitcast.104), calls=%async_computation.8 | async-start | bytes 2097152
  198.0 125.4 %copy-start.3 = (bf16[2,16,2880]{2,1,0:T(8,128)(2,1)S(1)}, bf16[2,16,2880]{2,1,0:T(8,128)(2,1)}, u32[]{:S(2)}) copy-start(bf16[2,16,2880]{2,1,0:T(8,128)(2,1)} %param.16) | copy-start | bytes 552964
  198.0 127.0 %copy-start.1 = (bf16[2880,64]{0,1:T(8,128)(2,1)S(1)}, bf16[2880,64]{0,1:T(8,128)(2,1)}, u32[]{:S(2)}) copy-start(bf16[2880,64]{0,1:T(8,128)(2,1)} %param.18) | copy-start | bytes 1105924
  198.0 125.3 %reduce-scatter.5.cloned.1.call-start = ((), (), s32[]{:S(2)}) async-start(), calls=%async_computation.5 | async-start | bytes 1884160 | tf_op jit(solution)/shard_map/reduce_scatter | solution.py:157
Sparse Core Ops, SparseCore 0:
  14.4 70.9 all-gather.2
  198.1 88.5 reduce-scatter.2
  289.0 34.2 reduce-scatter.4

commit v6 on v5

--- a/solution.py
+++ b/solution.py
@@ -110,16 +110,12 @@
     earlier = jnp.cumsum(picked, axis=2) - picked
     ranks = jnp.arange(MOST, dtype=jnp.int32)
     sender = (picked[..., None] > 0) & (earlier[..., None] == ranks)
-    groups = steps * n_dp * n_ex
-    slot_count = local_experts * MOST
-    sender_t = jnp.transpose(sender.reshape(groups, rows, slot_count), (0, 2, 1))
     slots = jnp.einsum(
-        "gsr,grd->gsd",
-        sender_t.astype(jnp.bfloat16),
-        all_rows.reshape(groups, rows, model_width),
+        "tbrxm,tbrd->tbxmd",
+        sender.astype(jnp.bfloat16),
+        all_rows,
         preferred_element_type=jnp.float32,
     ).astype(jnp.bfloat16)
-    slots = slots.reshape(steps, n_dp * n_ex, local_experts, MOST, model_width)
     gate_part = jnp.einsum("tbxmd,xdf->tbxmf", slots, w_gate, preferred_element_type=jnp.float32)
     up_part = jnp.einsum("tbxmd,xdf->tbxmf", slots, w_up, preferred_element_type=jnp.float32)
     hidden_act = ((up_part + 1.0) * gate_part * jax.nn.sigmoid(1.702 * gate_part)).astype(
@@ -149,13 +145,13 @@
     else:
         row_terms = jnp.einsum(
             "tbrxm,tbxmd->btrd", weights, partial, preferred_element_type=jnp.float32
-        )
+        ).astype(jnp.bfloat16)
         row_terms = lax.psum_scatter(
             row_terms.reshape((n_dp, n_ex) + row_terms.shape[1:]), "dp", scatter_dimension=0, tiled=True
         )[0]
         row_terms = jnp.moveaxis(row_terms, 0, 1)
     branch_out = lax.psum_scatter(row_terms, "expert", scatter_dimension=1, tiled=True)
-    return (residual + branch_out[:, 0]).astype(jnp.bfloat16)
+    return (residual + branch_out[:, 0].astype(jnp.float32)).astype(jnp.bfloat16)
 
 
 def body(

time: 336 us -> 269 us (0.80)
  waiting for transfers between devices: 148 us -> 108 us
  local copies, waits for them, and re-layouts: 53.4 us -> 27.8 us
    reduce_scatter x1, waiting for transfers between devices: 88.6 us -> 59.4 us  [moe_finish(): lax.psum_scatter(row_terms.reshape((n_dp, n_ex) + row_terms.shape[1:]), '...]
    reshape x1 -> x0, local copies, waits for them, and re-layouts: 23.5 us -> none  [moe_finish(): slots = slots.reshape(steps, n_dp * n_ex, local_experts, MOST, model_width)]
    reduce_scatter x1, waiting for transfers between devices: 36.6 us -> 25.4 us  [moe_finish(): lax.psum_scatter(row_terms, 'expert', scatter_dimension=1, tiled=True)]
  transfers between devices with their start and end apart: 5 -> 5, of which waited for: 5 -> 5; matrix products, arithmetic and copies ran while one was open for 12% -> 15% of each run, Pallas kernels for 0% -> 0%
where the time goes in v6:
time: 269 us; the launch traced here: 264 us
  waiting for transfers between devices  108 us (40%)
  matrix products  93.7 us (35%)
  local copies, waits for them, and re-layouts  27.8 us (10%)
  between operations  14.6 us (5%)
  other arithmetic  11.4 us (4%)
  starting transfers between devices  8.8 us (3%)
    reduce_scatter x1, waiting for transfers between devices, moe_finish(): lax.psum_scatter(row_terms.reshape((n_dp, n_ex) + row_terms.shape[1:]), '...  59.4 us
    reduce_scatter x1, waiting for transfers between devices, moe_finish(): lax.psum_scatter(row_terms, 'expert', scatter_dimension=1, tiled=True)  25.4 us
    dot_general x1, matrix products, moe_finish(): jnp.einsum('tbxmf,xfd->tbxmd', hidden_act, w_down, preferred_element_type...  23.1 us
    dot_general x1, matrix products, moe_finish(): jnp.einsum('tbrxm,tbxmd->btrd', weights, partial, preferred_element_type=...  20.2 us
    dot_general x1, matrix products, moe_finish(): jnp.einsum('tbxmd,xdf->tbxmf', slots, w_gate, preferred_element_type=jnp....  13.9 us
    dot_general x1, matrix products, moe_finish(): jnp.einsum('tbxmd,xdf->tbxmf', slots, w_up, preferred_element_type=jnp.fl...  13.9 us
    all_gather x1, waiting for transfers between devices, moe_layer(): gathered = lax.all_gather(payload, ('dp', 'expert'), axis=1, tiled=False)  12.6 us
    dot_general x1, matrix products, moe_finish(): jnp.einsum('tbrxm,tbrd->tbxmd', sender.astype(jnp.bfloat16), all_rows, pr...  10.5 us
  transfers between devices with their start and end apart: 5, of which 5 were waited for; matrix products, arithmetic and copies ran while one was open for 15% of the time, Pallas kernels for 0%

profile of v6, /device:TPU:0, one launch (start us, length us, event | category | flops | bytes accessed | tf_op | source)
XLA Modules:
  0.0 264.1 jit_solution(9170812825892365245)
XLA Ops:
  11.5 1.5 gather_fusion.1
  14.2 5.2 %all-to-all-start = ((bf16[8,4,16,512]{3,2,1,0:T(8,128)(2,1)}), bf16[8,4,16,512]{3,2,1,0:T(8,128)(2,1)S(1)}, u32[]{:S(2)}, u32[]{:S(2)}) async-start(bf16[8,4,16,512]{3,2,1,0:T(8,128)(2,1)} %param.27), calls=%async_computation | async-start | bytes 1048576 | tf_op jit(solution)/shard_map/all_to_all | solution.py:175
  21.1 1.6 gather_fusion
  22.7 6.6 %all-to-all-done = bf16[8,4,16,512]{3,2,1,0:T(8,128)(2,1)S(1)} async-done(((bf16[8,4,16,512]{3,2,1,0:T(8,128)(2,1)}), bf16[8,4,16,512]{3,2,1,0:T(8,128)(2,1)S(1)}, u32[]{:S(2)}, u32[]{:S(2)}) %all-to-all-start) | async-done | bytes 524320 | tf_op jit(solution)/shard_map/all_to_all | solution.py:175
  29.3 3.5 %all-to-all-start.1 = ((bf16[8,4,16,512]{3,2,1,0:T(8,128)(2,1)}), bf16[8,4,16,512]{3,2,1,0:T(8,128)(2,1)S(1)}, u32[]{:S(2)}, u32[]{:S(2)}) async-start(bf16[8,4,16,512]{3,2,1,0:T(8,128)(2,1)} %param.26), calls=%async_computation.1 | async-start | bytes 1048576 | tf_op jit(solution)/shard_map/all_to_all | solution.py:174
  32.9 3.2 %fusion.68 = (f32[2,16,8,8]{3,0,2,1:T(2,128)S(1)}, f32[2,16,8,8,2]{3,4,0,2,1:T(2,128)}) fusion(bf16[2,16,8,8,64]{4,3,2,1,0:T(8,128)(2,1)S(1)} %reshape.270, bf16[2,16,8,64,1]{3,2,1,0,4:T(8,128)(2,1)S(1)} %bitcast.107, pred[2,2]{1,0:T(4,128)(4,1)S(1)} %iota_compare_fusion.3), kind=kOutput, calls=%fused_computation.100 | convolution fusion | flops 534528 | bytes 319492 | tf_op jit(solution)/shard_map/trkgh,urkh->trkgu/dot_general | solution.py:46
  36.1 2.5 gather_fusion.2
  38.6 3.9 %all-to-all-done.1 = bf16[8,4,16,512]{3,2,1,0:T(8,128)(2,1)S(1)} async-done(((bf16[8,4,16,512]{3,2,1,0:T(8,128)(2,1)}), bf16[8,4,16,512]{3,2,1,0:T(8,128)(2,1)S(1)}, u32[]{:S(2)}, u32[]{:S(2)}) %all-to-all-start.1) | async-done | bytes 524320 | tf_op jit(solution)/shard_map/all_to_all | solution.py:174
  42.4 2.5 gather_fusion.3
  44.9 4.1 %broadcast_select_fusion = (bf16[160,16,512]{2,1,0:T(8,128)(2,1)}, bf16[160,16,512]{2,1,0:T(8,128)(2,1)S(1)}) fusion(bf16[160,16,512]{2,1,0:T(8,128)(2,1)} %gather_fusion.3, pred[160]{0:T(512)(128)(4,1)S(1)} %get-tuple-element.9, bf16[160,16,512]{2,1,0:T(8,128)(2,1)} %gather_fusion.2), kind=kLoop, calls=%fused_computation.23 | loop fusion | flops 2621440 | bytes 10485920 | tf_op jit(solution)/shard_map/jit(_take)/select_n | solution.py:29
  49.1 7.5 %reshape.269 = bf16[16,160,8,64]{3,2,1,0:T(8,128)(2,1)} reshape(bf16[160,16,512]{2,1,0:T(8,128)(2,1)} %get-tuple-element.15) | data formatting | bytes 5242880 | tf_op jit(solution)/shard_map/reshape | solution.py:29
  56.5 4.6 %reshape.267 = bf16[16,160,8,64]{3,2,1,0:T(8,128)(2,1)} reshape(bf16[160,16,512]{2,1,0:T(8,128)(2,1)S(1)} %get-tuple-element.16) | data formatting | bytes 5242880 | tf_op jit(solution)/shard_map/reshape | solution.py:32
  61.1 6.5 %bitcast_reduce_fusion = (f32[2,16,8,8]{3,0,2,1:T(2,128)S(1)}, f32[16,8,160,2,8]{2,4,3,1,0:T(8,128)S(1)}) fusion(pred[16,160]{1,0:T(8,128)(4,1)S(1)} %iota_compare_fusion.1, bf16[2,16,8,8,64]{4,3,2,1,0:T(8,128)(2,1)S(1)} %reshape.270, bf16[16,160,8,64,1]{3,2,1,0,4:T(8,128)(2,1)} %bitcast.104), kind=kOutput, calls=%fused_computation.26 | convolution fusion | flops 42924032 | bytes 4205056 | tf_op jit(solution)/shard_map/trkgh,rlkh->trkgl/dot_general | solution.py:41
  69.3 1.5 fusion.27
  71.6 1.2 convert_element_type.80
  72.8 12.6 %all-gather.3.cloned.1.call-done = bf16[2,512,2944]{2,1,0:T(8,128)(2,1)} async-done(((bf16[2,16,2944]{2,1,0:T(8,128)(2,1)}), bf16[2,512,2944]{2,1,0:T(8,128)(2,1)}) %all-gather.3.cloned.1.call-update) | async-done | bytes 6029328 | tf_op jit(solution)/shard_map/all_gather | solution.py:93
  88.9 10.5 %convolution_convert_fusion = bf16[2,32,16,2,2880]{4,2,3,1,0:T(8,128)(2,1)} fusion(bf16[2,32,16,2944]{3,2,1,0:T(8,128)(2,1)} %bitcast.98, s32[2,32,16,16]{3,2,0,1:T(8,128)S(1)} %copy.125, pred[2,32,16,16]{3,2,0,1:T(8,128)(4,1)S(1)} %copy.124), kind=kOutput, calls=%fused_computation.16 | convolution fusion | flops 194707456 | bytes 17907712 | tf_op jit(solution)/shard_map/tbrxm,tbrd->tbxmd/dot_general | solution.py:113
  99.4 13.9 %fusion.4 = f32[16,2,32,2,256]{4,2,3,1,0:T(8,128)S(1)} fusion(bf16[16,2880,256]{2,1,0:T(8,128)(2,1)} %param.21, bf16[2,32,16,2,2880]{4,2,3,1,0:T(8,128)(2,1)} %convolution_convert_fusion), kind=kOutput, calls=%fused_computation.8 | convolution fusion | flops 3019898880 | bytes 37486592 | tf_op jit(solution)/shard_map/tbxmd,xdf->tbxmf/dot_general | solution.py:120
  113.4 13.9 %fusion.32 = bf16[2,32,16,2,256]{4,1,3,0,2:T(8,128)(2,1)S(1)} fusion(bf16[16,2880,256]{2,1,0:T(8,128)(2,1)} %param.20, bf16[2,32,16,2,2880]{4,2,3,1,0:T(8,128)(2,1)} %convolution_convert_fusion, f32[16,2,32,2,256]{4,2,3,1,0:T(8,128)S(1)} %fusion.4), kind=kOutput, calls=%fused_computation.36 | convolution fusion | flops 3024093184 | bytes 38535168 | tf_op jit(solution)/shard_map/tbxmd,xdf->tbxmf/dot_general | solution.py:119
  127.3 23.1 %convert_bitcast_fusion = bf16[2,32,16,2,2880]{4,1,3,0,2:T(8,128)(2,1)} fusion(bf16[2,32,16,2,256]{4,1,3,0,2:T(8,128)(2,1)S(1)} %fusion.32, bf16[16,256,2880]{1,2,0:T(8,128)(2,1)} %param.22), kind=kOutput, calls=%fused_computation.13 | convolution fusion | flops 3025797120 | bytes 36438016 | tf_op jit(solution)/shard_map/tbxmf,xfd->tbxmd/dot_general | solution.py:124
  150.4 20.2 %bitcast_convert_fusion = bf16[32,2,16,2880]{3,2,1,0:T(8,128)(2,1)} fusion(bf16[2,32,16,2,2880]{4,1,3,0,2:T(8,128)(2,1)} %convert_bitcast_fusion, bf16[2,32,16,16]{3,2,0,1:T(8,128)(2,1)S(1)} %copy.127, s32[2,32,16,16]{3,2,0,1:T(8,128)S(1)} %copy.125, pred[2,32,16,16]{3,2,0,1:T(8,128)(4,1)S(1)} %copy.124), kind=kOutput, calls=%fused_computation.10 | convolution fusion | flops 191791104 | bytes 17809408 | tf_op jit(solution)/shard_map/tbrxm,tbxmd->btrd/dot_general | solution.py:146
  170.7 59.4 %reduce-scatter.3.cloned.1.call-done = bf16[1,4,2,16,2880]{4,3,2,1,0:T(8,128)(2,1)} async-done(((bf16[8,4,2,16,2880]{4,3,2,1,0:T(8,128)(2,1)}), bf16[1,4,2,16,2880]{4,3,2,1,0:T(8,128)(2,1)}) %reduce-scatter.3.cloned.1.call-update) | async-done | bytes 737296 | tf_op jit(solution)/shard_map/reduce_scatter | solution.py:149
  230.1 25.4 %reduce-scatter.5.cloned.1.call-done = bf16[2,1,16,2880]{3,2,0,1:T(8,128)(2,1)} async-done(((bf16[2,4,16,2880]{3,2,0,1:T(8,128)(2,1)}), bf16[2,1,16,2880]{3,2,0,1:T(8,128)(2,1)}) %reduce-scatter.5.cloned.1.call-update) | async-done | bytes 184336 | tf_op jit(solution)/shard_map/reduce_scatter | solution.py:153
  255.5 1.6 fusion.56
  (89 shorter events, 13.1 us)
Async XLA Ops:
  7.2 4.1 %copy-start = (bf16[2880,64]{0,1:T(8,128)(2,1)S(1)}, bf16[2880,64]{0,1:T(8,128)(2,1)}, u32[]{:S(2)}) copy-start(bf16[2880,64]{0,1:T(8,128)(2,1)} %param.18) | copy-start | bytes 1105924
  7.2 78.2 %all-gather.3.cloned.1.call-start = ((), (), s32[]{:S(2)}) async-start(), calls=%async_computation.6 | async-start | bytes 6217728 | tf_op jit(solution)/shard_map/all_gather | solution.py:93
  11.5 7.9 %copy-start.8 = (s32[1,16]{1,0:T(1,128)S(1)}, s32[1,16]{1,0:T(1,128)}, u32[]{:S(2)}) copy-start(s32[1,16]{1,0:T(1,128)} %param.28) | copy-start | bytes 196
  11.5 8.8 %copy-start.6 = (bf16[2,16,512]{2,1,0:T(8,128)(2,1)S(1)}, bf16[2,16,512]{2,1,0:T(8,128)(2,1)}, u32[]{:S(2)}) copy-start(bf16[2,16,512]{2,1,0:T(8,128)(2,1)} %param.24) | copy-start | bytes 98308
  11.5 8.9 %copy-start.7 = (bf16[2,16,512]{2,1,0:T(8,128)(2,1)S(1)}, bf16[2,16,512]{2,1,0:T(8,128)(2,1)}, u32[]{:S(2)}) copy-start(bf16[2,16,512]{2,1,0:T(8,128)(2,1)} %param.25) | copy-start | bytes 98308
  11.5 9.0 %copy-start.4 = (bf16[2,16,4096]{2,1,0:T(8,128)(2,1)S(1)}, bf16[2,16,4096]{2,1,0:T(8,128)(2,1)}, u32[]{:S(2)}) copy-start(bf16[2,16,4096]{2,1,0:T(8,128)(2,1)} %param.23) | copy-start | bytes 786436
  13.1 8.0 %copy-start.2 = (s32[1,32]{1,0:T(1,128)S(1)}, s32[1,32]{1,0:T(1,128)}, u32[]{:S(2)}) copy-start(s32[1,32]{1,0:T(1,128)} %param.29) | copy-start | bytes 388
  14.2 15.0 %all-to-all-start = ((bf16[8,4,16,512]{3,2,1,0:T(8,128)(2,1)}), bf16[8,4,16,512]{3,2,1,0:T(8,128)(2,1)S(1)}, u32[]{:S(2)}, u32[]{:S(2)}) async-start(bf16[8,4,16,512]{3,2,1,0:T(8,128)(2,1)} %param.27), calls=%async_computation | async-start | bytes 1048576 | tf_op jit(solution)/shard_map/all_to_all | solution.py:175
  29.3 13.2 %all-to-all-start.1 = ((bf16[8,4,16,512]{3,2,1,0:T(8,128)(2,1)}), bf16[8,4,16,512]{3,2,1,0:T(8,128)(2,1)S(1)}, u32[]{:S(2)}, u32[]{:S(2)}) async-start(bf16[8,4,16,512]{3,2,1,0:T(8,128)(2,1)} %param.26), calls=%async_computation.1 | async-start | bytes 1048576 | tf_op jit(solution)/shard_map/all_to_all | solution.py:174
  32.8 197.3 %reduce-scatter.3.cloned.1.call-start = ((), (), s32[]{:S(2)}) async-start(), calls=%async_computation.4 | async-start | bytes 6782976 | tf_op jit(solution)/shard_map/reduce_scatter | solution.py:149
  61.1 8.2 %slice-start = ((s8[5242880]{0:T(1024)(128)(4,1)}), s8[4194304]{0:T(1024)(128)(4,1)S(1)}, s32[]{:S(2)}) async-start(s8[5242880]{0:T(1024)(128)(4,1)} %bitcast.101), calls=%async_computation.7 | async-start | bytes 8388608
  61.1 6.6 %copy-start.5 = (f32[2,16,8,8,2]{3,4,0,2,1:T(2,128)S(1)}, f32[2,16,8,8,2]{3,4,0,2,1:T(2,128)}, u32[]{:S(2)}) copy-start(f32[2,16,8,8,2]{3,4,0,2,1:T(2,128)} %get-tuple-element.20) | copy-start | bytes 49156
  61.1 8.2 %slice-start.1 = ((s8[5242880]{0:T(1024)(128)(4,1)}), s8[1048576]{0:T(1024)(128)(4,1)S(1)}, s32[]{:S(2)}) async-start(s8[5242880]{0:T(1024)(128)(4,1)} %bitcast.101), calls=%async_computation.8 | async-start | bytes 2097152
  170.6 86.5 %copy-start.1 = (bf16[2880,64]{0,1:T(8,128)(2,1)S(1)}, bf16[2880,64]{0,1:T(8,128)(2,1)}, u32[]{:S(2)}) copy-start(bf16[2880,64]{0,1:T(8,128)(2,1)} %param.18) | copy-start | bytes 1105924
  170.6 84.9 %copy-start.3 = (bf16[2,16,2880]{2,1,0:T(8,128)(2,1)S(1)}, bf16[2,16,2880]{2,1,0:T(8,128)(2,1)}, u32[]{:S(2)}) copy-start(bf16[2,16,2880]{2,1,0:T(8,128)(2,1)} %param.16) | copy-start | bytes 552964
  170.7 84.8 %reduce-scatter.5.cloned.1.call-start = ((), (), s32[]{:S(2)}) async-start(), calls=%async_computation.5 | async-start | bytes 942080 | tf_op jit(solution)/shard_map/reduce_scatter | solution.py:153
Sparse Core Ops, SparseCore 0:
  14.4 70.9 all-gather.2
  170.8 59.2 reduce-scatter.2
  232.5 22.9 reduce-scatter.4

commit v7 on v6

--- a/solution.py
+++ b/solution.py
@@ -92,6 +92,11 @@
     )
     gathered = lax.all_gather(payload, ("dp", "expert"), axis=1, tiled=False)
     return gathered, residual
+
+
+def sibling(x):
+    n_dp = lax.axis_size("dp")
+    return lax.ppermute(x, "dp", perm=[(i, i ^ 1) for i in range(n_dp)])
 
 
 def moe_finish(gathered, meta, residual, topk, w_gate, w_up, w_down):
@@ -145,13 +150,25 @@
     else:
         row_terms = jnp.einsum(
             "tbrxm,tbxmd->btrd", weights, partial, preferred_element_type=jnp.float32
-        ).astype(jnp.bfloat16)
-        row_terms = lax.psum_scatter(
-            row_terms.reshape((n_dp, n_ex) + row_terms.shape[1:]), "dp", scatter_dimension=0, tiled=True
+        )
+        chips = n_dp // 2
+        core = lax.axis_index("dp") % 2
+        same_core = [[i for i in range(n_dp) if i % 2 == c] for c in range(2)]
+        row_terms = row_terms.reshape((chips, 2, n_ex) + row_terms.shape[1:])
+        keep = lax.dynamic_index_in_dim(row_terms, core, 3, keepdims=False)
+        give = lax.dynamic_index_in_dim(row_terms, 1 - core, 3, keepdims=False)
+        chip_sum = (keep + sibling(give)).astype(jnp.bfloat16)
+        chip_sum = lax.psum_scatter(
+            chip_sum, "dp", scatter_dimension=0, tiled=True, axis_index_groups=same_core
         )[0]
-        row_terms = jnp.moveaxis(row_terms, 0, 1)
+        chip_sum = jnp.moveaxis(chip_sum, 1, 0)
+        chip_sum = lax.psum_scatter(chip_sum, "expert", scatter_dimension=0, tiled=True)[0]
+        mine = lax.dynamic_index_in_dim(chip_sum, core, 0, keepdims=False)
+        theirs = sibling(lax.dynamic_index_in_dim(chip_sum, 1 - core, 0, keepdims=False))
+        branch = jnp.where(core == 0, jnp.stack([mine, theirs]), jnp.stack([theirs, mine]))
+        return (residual + branch.astype(jnp.float32)).astype(jnp.bfloat16)
     branch_out = lax.psum_scatter(row_terms, "expert", scatter_dimension=1, tiled=True)
-    return (residual + branch_out[:, 0].astype(jnp.float32)).astype(jnp.bfloat16)
+    return (residual + branch_out[:, 0]).astype(jnp.bfloat16)
 
 
 def body(

time: 269 us -> 291 us (1.082); the launches traced: 264 us -> 290 us
  waiting for transfers between devices: 108 us -> 120 us
  local copies, waits for them, and re-layouts: 27.8 us -> 35.8 us
  other arithmetic: 11.4 us -> 17 us
    unnamed x3 -> x5, waiting for transfers between devices: 0.05 us -> 85.9 us
    reduce_scatter x2 -> x0, waiting for transfers between devices: 84.8 us -> none  [the longest x1 59.4 us: moe_finish(): lax.psum_scatter(row_terms.reshape((n_dp, n_ex) + row_terms.shape[1:]), '...]
    ppermute x0 -> x2, waiting for transfers between devices: none -> 11.1 us  [sibling(): return lax.ppermute(x, 'dp', perm=[(i, i ^ 1) for i in range(n_dp)])]
    convert_element_type x1 -> x2, other arithmetic: 1.64 us -> 7.46 us  [the longest x1 6.72 us: moe_finish(): chip_sum = (keep + sibling(give)).astype(jnp.bfloat16)]
    unnamed x23 -> x26, local copies, waits for them, and re-layouts: 0.83 us -> 4.63 us
    squeeze x0 -> x1, local copies, waits for them, and re-layouts: none -> 3.25 us  [moe_finish(): give = lax.dynamic_index_in_dim(row_terms, 1 - core, 3, keepdims=False)]
  transfers between devices with their start and end apart: 5 -> 7, of which waited for: 5 -> 7; matrix products, arithmetic and copies ran while one was open for 15% -> 14% of each run, Pallas kernels for 0% -> 0%
where the time goes in v7:
time: 291 us; the launch traced here: 290 us
  waiting for transfers between devices  120 us (41%)
  matrix products  93.3 us (32%)
  local copies, waits for them, and re-layouts  35.8 us (12%)
  other arithmetic  17 us (6%)
  between operations  14.9 us (5%)
  starting transfers between devices  9.16 us (3%)
    unnamed x5, waiting for transfers between devices  85.9 us
    dot_general x1, matrix products, moe_finish(): jnp.einsum('tbxmf,xfd->tbxmd', hidden_act, w_down, preferred_element_type...  22.9 us
    dot_general x1, matrix products, moe_finish(): jnp.einsum('tbrxm,tbxmd->btrd', weights, partial, preferred_element_type=...  20.2 us
    dot_general x1, matrix products, moe_finish(): jnp.einsum('tbxmd,xdf->tbxmf', slots, w_gate, preferred_element_type=jnp....  13.9 us
    dot_general x1, matrix products, moe_finish(): jnp.einsum('tbxmd,xdf->tbxmf', slots, w_up, preferred_element_type=jnp.fl...  13.7 us
    all_gather x1, waiting for transfers between devices, moe_layer(): gathered = lax.all_gather(payload, ('dp', 'expert'), axis=1, tiled=False)  12.8 us
    ppermute x2, waiting for transfers between devices, sibling(): return lax.ppermute(x, 'dp', perm=[(i, i ^ 1) for i in range(n_dp)])  11.1 us
    dot_general x1, matrix products, moe_finish(): jnp.einsum('tbrxm,tbrd->tbxmd', sender.astype(jnp.bfloat16), all_rows, pr...  10.5 us
  transfers between devices with their start and end apart: 7, of which 7 were waited for; matrix products, arithmetic and copies ran while one was open for 14% of the time, Pallas kernels for 0%

profile of v7, /device:TPU:0, one launch (start us, length us, event | category | flops | bytes accessed | tf_op | source)
XLA Modules:
  0.0 290.3 jit_solution(8728582484330157124)
XLA Ops:
  14.2 5.2 %all-to-all-start.1 = ((bf16[8,4,16,512]{3,2,1,0:T(8,128)(2,1)}), bf16[8,4,16,512]{3,2,1,0:T(8,128)(2,1)S(1)}, u32[]{:S(2)}, u32[]{:S(2)}) async-start(bf16[8,4,16,512]{3,2,1,0:T(8,128)(2,1)} %param.26), calls=%async_computation.1 | async-start | bytes 1048576 | tf_op jit(solution)/shard_map/all_to_all | solution.py:191
  21.1 1.6 gather_fusion
  22.7 6.5 %all-to-all-done.1 = bf16[8,4,16,512]{3,2,1,0:T(8,128)(2,1)S(1)} async-done(((bf16[8,4,16,512]{3,2,1,0:T(8,128)(2,1)}), bf16[8,4,16,512]{3,2,1,0:T(8,128)(2,1)S(1)}, u32[]{:S(2)}, u32[]{:S(2)}) %all-to-all-start.1) | async-done | bytes 524320 | tf_op jit(solution)/shard_map/all_to_all | solution.py:191
  29.3 3.5 %all-to-all-start = ((bf16[8,4,16,512]{3,2,1,0:T(8,128)(2,1)}), bf16[8,4,16,512]{3,2,1,0:T(8,128)(2,1)S(1)}, u32[]{:S(2)}, u32[]{:S(2)}) async-start(bf16[8,4,16,512]{3,2,1,0:T(8,128)(2,1)} %param.27), calls=%async_computation | async-start | bytes 1048576 | tf_op jit(solution)/shard_map/all_to_all | solution.py:192
  32.9 3.2 %fusion.67 = (f32[2,16,8,8]{3,0,2,1:T(2,128)S(1)}, f32[2,16,8,8,2]{3,4,0,2,1:T(2,128)}) fusion(bf16[2,16,8,8,64]{4,3,2,1,0:T(8,128)(2,1)S(1)} %reshape.271, bf16[2,16,8,64,1]{3,2,1,0,4:T(8,128)(2,1)S(1)} %bitcast.127, pred[2,2]{1,0:T(4,128)(4,1)S(1)} %iota_compare_fusion.3), kind=kOutput, calls=%fused_computation.105 | convolution fusion | flops 534528 | bytes 319492 | tf_op jit(solution)/shard_map/trkgh,urkh->trkgu/dot_general | solution.py:46
  36.1 2.5 gather_fusion.3
  38.6 3.9 %all-to-all-done = bf16[8,4,16,512]{3,2,1,0:T(8,128)(2,1)S(1)} async-done(((bf16[8,4,16,512]{3,2,1,0:T(8,128)(2,1)}), bf16[8,4,16,512]{3,2,1,0:T(8,128)(2,1)S(1)}, u32[]{:S(2)}, u32[]{:S(2)}) %all-to-all-start) | async-done | bytes 524320 | tf_op jit(solution)/shard_map/all_to_all | solution.py:192
  42.4 2.5 gather_fusion.2
  44.9 4.0 %broadcast_select_fusion = (bf16[160,16,512]{2,1,0:T(8,128)(2,1)S(1)}, bf16[160,16,512]{2,1,0:T(8,128)(2,1)}) fusion(bf16[160,16,512]{2,1,0:T(8,128)(2,1)} %gather_fusion.3, pred[160]{0:T(512)(128)(4,1)S(1)} %get-tuple-element.9, bf16[160,16,512]{2,1,0:T(8,128)(2,1)} %gather_fusion.2), kind=kLoop, calls=%fused_computation.25 | loop fusion | flops 2621440 | bytes 10485920 | tf_op jit(solution)/shard_map/jit(_take)/select_n | solution.py:29
  48.9 7.5 %reshape.268 = bf16[16,160,8,64]{3,2,1,0:T(8,128)(2,1)} reshape(bf16[160,16,512]{2,1,0:T(8,128)(2,1)} %get-tuple-element.18) | data formatting | bytes 5242880 | tf_op jit(solution)/shard_map/reshape | solution.py:32
  56.4 4.6 %reshape.270 = bf16[16,160,8,64]{3,2,1,0:T(8,128)(2,1)} reshape(bf16[160,16,512]{2,1,0:T(8,128)(2,1)S(1)} %get-tuple-element.17) | data formatting | bytes 5242880 | tf_op jit(solution)/shard_map/reshape | solution.py:29
  61.0 6.4 %bitcast_reduce_fusion = (f32[2,16,8,8]{3,0,2,1:T(2,128)S(1)}, f32[16,8,160,2,8]{2,4,3,1,0:T(8,128)S(1)}) fusion(pred[16,160]{1,0:T(8,128)(4,1)S(1)} %iota_compare_fusion.1, bf16[2,16,8,8,64]{4,3,2,1,0:T(8,128)(2,1)S(1)} %reshape.271, bf16[16,160,8,64,1]{3,2,1,0,4:T(8,128)(2,1)} %bitcast.123), kind=kOutput, calls=%fused_computation.28 | convolution fusion | flops 42924032 | bytes 4205056 | tf_op jit(solution)/shard_map/trkgh,rlkh->trkgl/dot_general | solution.py:41
  72.6 12.8 %all-gather.3.cloned.1.call-done = bf16[2,512,2944]{2,1,0:T(8,128)(2,1)} async-done(((bf16[2,16,2944]{2,1,0:T(8,128)(2,1)}), bf16[2,512,2944]{2,1,0:T(8,128)(2,1)}) %all-gather.3.cloned.1.call-update) | async-done | bytes 6029328 | tf_op jit(solution)/shard_map/all_gather | solution.py:93
  88.9 10.5 %convolution_convert_fusion = bf16[2,32,16,2,2880]{4,2,3,1,0:T(8,128)(2,1)} fusion(bf16[2,32,16,2944]{3,2,1,0:T(8,128)(2,1)} %bitcast.119, s32[2,32,16,16]{3,2,0,1:T(8,128)S(1)} %copy.153, pred[2,32,16,16]{3,2,0,1:T(8,128)(4,1)S(1)} %copy.152), kind=kOutput, calls=%fused_computation.15 | convolution fusion | flops 194707456 | bytes 17907712 | tf_op jit(solution)/shard_map/tbrxm,tbrd->tbxmd/dot_general | solution.py:118
  99.5 13.7 %fusion.4 = f32[16,2,32,2,256]{4,2,3,1,0:T(8,128)S(1)} fusion(bf16[16,2880,256]{2,1,0:T(8,128)(2,1)} %param.21, bf16[2,32,16,2,2880]{4,2,3,1,0:T(8,128)(2,1)} %convolution_convert_fusion), kind=kOutput, calls=%fused_computation.8 | convolution fusion | flops 3019898880 | bytes 37486592 | tf_op jit(solution)/shard_map/tbxmd,xdf->tbxmf/dot_general | solution.py:125
  113.2 13.9 %fusion.31 = bf16[2,32,16,2,256]{4,1,3,0,2:T(8,128)(2,1)S(1)} fusion(bf16[16,2880,256]{2,1,0:T(8,128)(2,1)} %param.20, bf16[2,32,16,2,2880]{4,2,3,1,0:T(8,128)(2,1)} %convolution_convert_fusion, f32[16,2,32,2,256]{4,2,3,1,0:T(8,128)S(1)} %fusion.4), kind=kOutput, calls=%fused_computation.38 | convolution fusion | flops 3024093184 | bytes 38535168 | tf_op jit(solution)/shard_map/tbxmd,xdf->tbxmf/dot_general | solution.py:124
  127.1 22.9 %convert_bitcast_fusion = bf16[2,32,16,2,2880]{4,1,3,0,2:T(8,128)(2,1)} fusion(bf16[2,32,16,2,256]{4,1,3,0,2:T(8,128)(2,1)S(1)} %fusion.31, bf16[16,256,2880]{1,2,0:T(8,128)(2,1)} %param.22), kind=kOutput, calls=%fused_computation.12 | convolution fusion | flops 3025797120 | bytes 36438016 | tf_op jit(solution)/shard_map/tbxmf,xfd->tbxmd/dot_general | solution.py:129
  150.0 20.2 %fusion.6 = f32[32,2,16,2880,1]{3,2,4,1,0:T(8,128)S(1)} fusion(bf16[2,32,16,2,2880]{4,1,3,0,2:T(8,128)(2,1)} %convert_bitcast_fusion, bf16[2,32,16,16]{3,2,0,1:T(8,128)(2,1)S(1)} %copy.155, s32[2,32,16,16]{3,2,0,1:T(8,128)S(1)} %copy.153, pred[2,32,16,16]{3,2,0,1:T(8,128)(4,1)S(1)} %copy.152), kind=kOutput, calls=%fused_computation.10 | convolution fusion | flops 188841984 | bytes 23707648 | tf_op jit(solution)/shard_map/tbrxm,tbxmd->btrd/dot_general | solution.py:151
  170.2 3.3 %dynamic-slice_bitcast_fusion = f32[4,2,4,16,2880]{4,3,2,1,0:T(8,128)} fusion(f32[4,2,4,2,16,2880]{5,4,3,2,1,0:T(8,128)S(1)} %bitcast.116, s32[]{:T(128)S(6)} %select_n.116), kind=kLoop, calls=%fused_computation.19 | loop fusion | bytes 11796484 | tf_op jit(solution)/shard_map/jit(dynamic_index_in_dim)/squeeze | solution.py:159
  173.5 3.2 %copy-done.3 = f32[32,2,16,2880,1]{3,2,4,1,0:T(8,128)} copy-done((f32[32,2,16,2880,1]{3,2,4,1,0:T(8,128)}, f32[32,2,16,2880,1]{3,2,4,1,0:T(8,128)S(1)}, u32[]{:S(2)}) %copy-start.3) | copy-done | bytes 11796504
  176.9 9.8 %collective-permute-done = f32[4,2,4,16,2880]{4,3,2,1,0:T(8,128)} collective-permute-done((f32[4,2,4,16,2880]{4,3,2,1,0:T(8,128)}, f32[4,2,4,16,2880]{4,3,2,1,0:T(8,128)}, u32[]{:S(2)}, u32[]{:S(2)}) %collective-permute-start) | collective-permute-done | bytes 5898272 | tf_op jit(solution)/shard_map/ppermute | solution.py:99
  186.8 6.7 %fusion.12 = bf16[4,2,4,16,2880]{4,3,2,1,0:T(8,128)(2,1)} fusion(f32[4,2,4,16,2880]{4,3,2,1,0:T(8,128)} %collective-permute-done, f32[4,2,4,2,16,2880]{5,4,3,2,1,0:T(8,128)} %bitcast.117, s32[]{:T(128)S(6)} %select_n.115), kind=kLoop, calls=%fused_computation.17 | loop fusion | flops 2949120 | bytes 14745604 | tf_op jit(solution)/shard_map/convert_element_type | solution.py:160
  193.6 41.9 %reduce-scatter.7.cloned.1.call-done = bf16[1,2,4,16,2880]{4,3,2,1,0:T(8,128)(2,1)} async-done(((bf16[4,2,4,16,2880]{4,3,2,1,0:T(8,128)(2,1)}), bf16[1,2,4,16,2880]{4,3,2,1,0:T(8,128)(2,1)}) %reduce-scatter.7.cloned.1.call-update) | async-done | bytes 737296
  236.8 43.9 %all-reduce.4.cloned.1.call-done = bf16[4,2,16,2880]{3,2,0,1:T(8,128)(2,1)} async-done(((bf16[4,2,16,2880]{3,2,0,1:T(8,128)(2,1)}), bf16[4,2,16,2880]{3,2,0,1:T(8,128)(2,1)}) %all-reduce.4.cloned.1.call-update) | async-done | bytes 737296
  (98 shorter events, 21.2 us)
Async XLA Ops:
  7.2 4.0 %copy-start = (bf16[2880,64]{0,1:T(8,128)(2,1)S(1)}, bf16[2880,64]{0,1:T(8,128)(2,1)}, u32[]{:S(2)}) copy-start(bf16[2880,64]{0,1:T(8,128)(2,1)} %param.18) | copy-start | bytes 1105924
  7.2 78.2 %all-gather.3.cloned.1.call-start = ((), (), s32[]{:S(2)}) async-start(), calls=%async_computation.3 | async-start | bytes 6217728 | tf_op jit(solution)/shard_map/all_gather | solution.py:93
  11.4 8.0 %copy-start.10 = (s32[1,16]{1,0:T(1,128)S(1)}, s32[1,16]{1,0:T(1,128)}, u32[]{:S(2)}) copy-start(s32[1,16]{1,0:T(1,128)} %param.28) | copy-start | bytes 196
  11.4 8.9 %copy-start.6 = (bf16[2,16,4096]{2,1,0:T(8,128)(2,1)S(1)}, bf16[2,16,4096]{2,1,0:T(8,128)(2,1)}, u32[]{:S(2)}) copy-start(bf16[2,16,4096]{2,1,0:T(8,128)(2,1)} %param.23) | copy-start | bytes 786436
  11.4 9.5 %copy-start.8 = (bf16[2,16,512]{2,1,0:T(8,128)(2,1)S(1)}, bf16[2,16,512]{2,1,0:T(8,128)(2,1)}, u32[]{:S(2)}) copy-start(bf16[2,16,512]{2,1,0:T(8,128)(2,1)} %param.24) | copy-start | bytes 98308
  11.4 9.6 %copy-start.9 = (bf16[2,16,512]{2,1,0:T(8,128)(2,1)S(1)}, bf16[2,16,512]{2,1,0:T(8,128)(2,1)}, u32[]{:S(2)}) copy-start(bf16[2,16,512]{2,1,0:T(8,128)(2,1)} %param.25) | copy-start | bytes 98308
  13.0 8.1 %copy-start.2 = (s32[1,32]{1,0:T(1,128)S(1)}, s32[1,32]{1,0:T(1,128)}, u32[]{:S(2)}) copy-start(s32[1,32]{1,0:T(1,128)} %param.29) | copy-start | bytes 388
  14.2 15.0 %all-to-all-start.1 = ((bf16[8,4,16,512]{3,2,1,0:T(8,128)(2,1)}), bf16[8,4,16,512]{3,2,1,0:T(8,128)(2,1)S(1)}, u32[]{:S(2)}, u32[]{:S(2)}) async-start(bf16[8,4,16,512]{3,2,1,0:T(8,128)(2,1)} %param.26), calls=%async_computation.1 | async-start | bytes 1048576 | tf_op jit(solution)/shard_map/all_to_all | solution.py:191
  29.3 13.2 %all-to-all-start = ((bf16[8,4,16,512]{3,2,1,0:T(8,128)(2,1)}), bf16[8,4,16,512]{3,2,1,0:T(8,128)(2,1)S(1)}, u32[]{:S(2)}, u32[]{:S(2)}) async-start(bf16[8,4,16,512]{3,2,1,0:T(8,128)(2,1)} %param.27), calls=%async_computation | async-start | bytes 1048576 | tf_op jit(solution)/shard_map/all_to_all | solution.py:192
  32.8 202.7 %reduce-scatter.7.cloned.1.call-start = ((), (), s32[]{:S(2)}) async-start(), calls=%async_computation.5 | async-start | bytes 3768320
  61.0 6.5 %copy-start.7 = (f32[2,16,8,8,2]{3,4,0,2,1:T(2,128)S(1)}, f32[2,16,8,8,2]{3,4,0,2,1:T(2,128)}, u32[]{:S(2)}) copy-start(f32[2,16,8,8,2]{3,4,0,2,1:T(2,128)} %get-tuple-element.22) | copy-start | bytes 49156
  61.0 8.2 %copy-start.4 = (bf16[16,160,8,64]{3,2,1,0:T(8,128)(2,1)S(1)}, bf16[16,160,8,64]{3,2,1,0:T(8,128)(2,1)}, u32[]{:S(2)}) copy-start(bf16[16,160,8,64]{3,2,1,0:T(8,128)(2,1)} %reshape.268) | copy-start | bytes 7864324
  170.2 6.4 %copy-start.3 = (f32[32,2,16,2880,1]{3,2,4,1,0:T(8,128)}, f32[32,2,16,2880,1]{3,2,4,1,0:T(8,128)S(1)}, u32[]{:S(2)}) copy-start(f32[32,2,16,2880,1]{3,2,4,1,0:T(8,128)S(1)} %fusion.6) | copy-start | bytes 35389444
  176.6 10.1 %collective-permute-start = (f32[4,2,4,16,2880]{4,3,2,1,0:T(8,128)}, f32[4,2,4,16,2880]{4,3,2,1,0:T(8,128)}, u32[]{:S(2)}, u32[]{:S(2)}) collective-permute-start(f32[4,2,4,16,2880]{4,3,2,1,0:T(8,128)} %dynamic-slice_bitcast_fusion), channel_id=1, source_target_pairs={{0,4},{4,0},{8,12},{12,8},{16,20},{20,16},{24,28},{28,24},{1,5},{5... | collective-permute-start | bytes 17694728 | tf_op jit(solution)/shard_map/ppermute | solution.py:99
  176.9 58.6 %copy-start.11 = (u32[32]{0:T(128)S(1)}, u32[32]{0:T(128)}, u32[]{:S(2)}) copy-start(u32[32]{0:T(128)} %constant.145) | copy-start | bytes 388
  176.9 106.1 %copy-start.5 = (bf16[2,16,2880]{2,1,0:T(8,128)(2,1)S(1)}, bf16[2,16,2880]{2,1,0:T(8,128)(2,1)}, u32[]{:S(2)}) copy-start(bf16[2,16,2880]{2,1,0:T(8,128)(2,1)} %param.16) | copy-start | bytes 552964
  186.8 97.0 %copy-start.1 = (bf16[2880,64]{0,1:T(8,128)(2,1)S(1)}, bf16[2880,64]{0,1:T(8,128)(2,1)}, u32[]{:S(2)}) copy-start(bf16[2880,64]{0,1:T(8,128)(2,1)} %param.18) | copy-start | bytes 1105924
  193.5 87.2 %all-reduce.4.cloned.1.call-start = ((), (), s32[]{:S(2)}) async-start(), calls=%async_computation.4 | async-start | bytes 1507328
  281.6 1.4 collective-permute-start.1
Sparse Core Ops, SparseCore 0:
  14.4 70.9 all-gather.2
  193.6 41.8 reduce-scatter.6
  237.8 42.7 all-reduce.3

commit v8 on v6

--- a/solution.py
+++ b/solution.py
@@ -146,10 +146,8 @@
         row_terms = jnp.einsum(
             "tbrxm,tbxmd->btrd", weights, partial, preferred_element_type=jnp.float32
         ).astype(jnp.bfloat16)
-        row_terms = lax.psum_scatter(
-            row_terms.reshape((n_dp, n_ex) + row_terms.shape[1:]), "dp", scatter_dimension=0, tiled=True
-        )[0]
-        row_terms = jnp.moveaxis(row_terms, 0, 1)
+        branch_out = lax.psum_scatter(row_terms, ("dp", "expert"), scatter_dimension=0, tiled=True)
+        return (residual + branch_out[0].astype(jnp.float32)).astype(jnp.bfloat16)
     branch_out = lax.psum_scatter(row_terms, "expert", scatter_dimension=1, tiled=True)
     return (residual + branch_out[:, 0].astype(jnp.float32)).astype(jnp.bfloat16)
 

time: 269 us -> 341 us (1.27)
  waiting for transfers between devices: 108 us -> 180 us
    reduce_scatter x2 -> x1, waiting for transfers between devices: 84.8 us -> 157 us  [moe_finish(): lax.psum_scatter(row_terms, ('dp', 'expert'), scatter_dimension=0, tiled=...]
  transfers between devices with their start and end apart: 5 -> 4, of which waited for: 5 -> 4; matrix products, arithmetic and copies ran while one was open for 15% -> 12% of each run, Pallas kernels for 0% -> 0%
where the time goes in v8:
time: 341 us; the launch traced here: 337 us
  waiting for transfers between devices  180 us (53%)
  matrix products  93.7 us (27%)
  local copies, waits for them, and re-layouts  27.8 us (8%)
  between operations  14.9 us (4%)
  other arithmetic  11.4 us (3%)
  starting transfers between devices  8.76 us (3%)
    reduce_scatter x1, waiting for transfers between devices, moe_finish(): lax.psum_scatter(row_terms, ('dp', 'expert'), scatter_dimension=0, tiled=...  157 us
    dot_general x1, matrix products, moe_finish(): jnp.einsum('tbxmf,xfd->tbxmd', hidden_act, w_down, preferred_element_type...  23.1 us
    dot_general x1, matrix products, moe_finish(): jnp.einsum('tbrxm,tbxmd->btrd', weights, partial, preferred_element_type=...  20.2 us
    dot_general x1, matrix products, moe_finish(): jnp.einsum('tbxmd,xdf->tbxmf', slots, w_gate, preferred_element_type=jnp....  13.9 us
    dot_general x1, matrix products, moe_finish(): jnp.einsum('tbxmd,xdf->tbxmf', slots, w_up, preferred_element_type=jnp.fl...  13.9 us
    all_gather x1, waiting for transfers between devices, moe_layer(): gathered = lax.all_gather(payload, ('dp', 'expert'), axis=1, tiled=False)  12.6 us
    dot_general x1, matrix products, moe_finish(): jnp.einsum('tbrxm,tbrd->tbxmd', sender.astype(jnp.bfloat16), all_rows, pr...  10.5 us
    reshape x1, local copies, waits for them, and re-layouts, attention(): jnp.take(space_keys, slot_ids, axis=0)  7.49 us
  transfers between devices with their start and end apart: 4, of which 4 were waited for; matrix products, arithmetic and copies ran while one was open for 12% of the time, Pallas kernels for 0%

profile of v8, /device:TPU:0, one launch (start us, length us, event | category | flops | bytes accessed | tf_op | source)
XLA Modules:
  0.0 336.6 jit_solution(7745501806003568542)
XLA Ops:
  11.5 1.5 gather_fusion.1
  14.2 5.2 %all-to-all-start = ((bf16[8,4,16,512]{3,2,1,0:T(8,128)(2,1)}), bf16[8,4,16,512]{3,2,1,0:T(8,128)(2,1)S(1)}, u32[]{:S(2)}, u32[]{:S(2)}) async-start(bf16[8,4,16,512]{3,2,1,0:T(8,128)(2,1)} %param.27), calls=%async_computation | async-start | bytes 1048576 | tf_op jit(solution)/shard_map/all_to_all | solution.py:173
  21.1 1.6 gather_fusion
  22.7 6.6 %all-to-all-done = bf16[8,4,16,512]{3,2,1,0:T(8,128)(2,1)S(1)} async-done(((bf16[8,4,16,512]{3,2,1,0:T(8,128)(2,1)}), bf16[8,4,16,512]{3,2,1,0:T(8,128)(2,1)S(1)}, u32[]{:S(2)}, u32[]{:S(2)}) %all-to-all-start) | async-done | bytes 524320 | tf_op jit(solution)/shard_map/all_to_all | solution.py:173
  29.3 3.5 %all-to-all-start.1 = ((bf16[8,4,16,512]{3,2,1,0:T(8,128)(2,1)}), bf16[8,4,16,512]{3,2,1,0:T(8,128)(2,1)S(1)}, u32[]{:S(2)}, u32[]{:S(2)}) async-start(bf16[8,4,16,512]{3,2,1,0:T(8,128)(2,1)} %param.26), calls=%async_computation.1 | async-start | bytes 1048576 | tf_op jit(solution)/shard_map/all_to_all | solution.py:172
  32.9 3.2 fusion.68
  36.1 2.5 gather_fusion.2
  38.6 3.9 %all-to-all-done.1 = bf16[8,4,16,512]{3,2,1,0:T(8,128)(2,1)S(1)} async-done(((bf16[8,4,16,512]{3,2,1,0:T(8,128)(2,1)}), bf16[8,4,16,512]{3,2,1,0:T(8,128)(2,1)S(1)}, u32[]{:S(2)}, u32[]{:S(2)}) %all-to-all-start.1) | async-done | bytes 524320 | tf_op jit(solution)/shard_map/all_to_all | solution.py:172
  42.4 2.5 gather_fusion.3
  44.9 4.1 %broadcast_select_fusion = (bf16[160,16,512]{2,1,0:T(8,128)(2,1)}, bf16[160,16,512]{2,1,0:T(8,128)(2,1)S(1)}) fusion(bf16[160,16,512]{2,1,0:T(8,128)(2,1)} %gather_fusion.3, pred[160]{0:T(512)(128)(4,1)S(1)} %get-tuple-element.9, bf16[160,16,512]{2,1,0:T(8,128)(2,1)} %gather_fusion.2), kind=kLoop, calls=%fused_computation.23 | loop fusion | flops 2621440 | bytes 10485920 | tf_op jit(solution)/shard_map/jit(_take)/select_n | solution.py:29
  49.1 7.5 %reshape.266 = bf16[16,160,8,64]{3,2,1,0:T(8,128)(2,1)} reshape(bf16[160,16,512]{2,1,0:T(8,128)(2,1)} %get-tuple-element.15) | data formatting | bytes 5242880 | tf_op jit(solution)/shard_map/reshape | solution.py:29
  56.5 4.6 %reshape.264 = bf16[16,160,8,64]{3,2,1,0:T(8,128)(2,1)} reshape(bf16[160,16,512]{2,1,0:T(8,128)(2,1)S(1)} %get-tuple-element.16) | data formatting | bytes 5242880 | tf_op jit(solution)/shard_map/reshape | solution.py:32
  61.1 6.5 %bitcast_reduce_fusion = (f32[2,16,8,8]{3,0,2,1:T(2,128)S(1)}, f32[16,8,160,2,8]{2,4,3,1,0:T(8,128)S(1)}) fusion(pred[16,160]{1,0:T(8,128)(4,1)S(1)} %iota_compare_fusion.1, bf16[2,16,8,8,64]{4,3,2,1,0:T(8,128)(2,1)S(1)} %reshape.267, bf16[16,160,8,64,1]{3,2,1,0,4:T(8,128)(2,1)} %bitcast.99), kind=kOutput, calls=%fused_computation.26 | convolution fusion | flops 42924032 | bytes 4205056 | tf_op jit(solution)/shard_map/trkgh,rlkh->trkgl/dot_general | solution.py:41
  69.3 1.5 fusion.27
  71.6 1.2 convert_element_type.80
  72.8 12.6 %all-gather.3.cloned.1.call-done = bf16[2,512,2944]{2,1,0:T(8,128)(2,1)} async-done(((bf16[2,16,2944]{2,1,0:T(8,128)(2,1)}), bf16[2,512,2944]{2,1,0:T(8,128)(2,1)}) %all-gather.3.cloned.1.call-update) | async-done | bytes 6029328 | tf_op jit(solution)/shard_map/all_gather | solution.py:93
  85.4 1.1 slice.25
  88.9 10.5 %convolution_convert_fusion = bf16[2,32,16,2,2880]{4,2,3,1,0:T(8,128)(2,1)} fusion(bf16[2,32,16,2944]{3,2,1,0:T(8,128)(2,1)} %bitcast.93, s32[2,32,16,16]{3,2,0,1:T(8,128)S(1)} %copy.125, pred[2,32,16,16]{3,2,0,1:T(8,128)(4,1)S(1)} %copy.124), kind=kOutput, calls=%fused_computation.16 | convolution fusion | flops 194707456 | bytes 17907712 | tf_op jit(solution)/shard_map/tbrxm,tbrd->tbxmd/dot_general | solution.py:113
  99.4 13.9 %fusion.4 = f32[16,2,32,2,256]{4,2,3,1,0:T(8,128)S(1)} fusion(bf16[16,2880,256]{2,1,0:T(8,128)(2,1)} %param.21, bf16[2,32,16,2,2880]{4,2,3,1,0:T(8,128)(2,1)} %convolution_convert_fusion), kind=kOutput, calls=%fused_computation.8 | convolution fusion | flops 3019898880 | bytes 37486592 | tf_op jit(solution)/shard_map/tbxmd,xdf->tbxmf/dot_general | solution.py:120
  113.4 13.9 %fusion.32 = bf16[2,32,16,2,256]{4,1,3,0,2:T(8,128)(2,1)S(1)} fusion(bf16[16,2880,256]{2,1,0:T(8,128)(2,1)} %param.20, bf16[2,32,16,2,2880]{4,2,3,1,0:T(8,128)(2,1)} %convolution_convert_fusion, f32[16,2,32,2,256]{4,2,3,1,0:T(8,128)S(1)} %fusion.4), kind=kOutput, calls=%fused_computation.36 | convolution fusion | flops 3024093184 | bytes 38535168 | tf_op jit(solution)/shard_map/tbxmd,xdf->tbxmf/dot_general | solution.py:119
  127.3 23.1 %convert_bitcast_fusion = bf16[2,32,16,2,2880]{4,1,3,0,2:T(8,128)(2,1)} fusion(bf16[2,32,16,2,256]{4,1,3,0,2:T(8,128)(2,1)S(1)} %fusion.32, bf16[16,256,2880]{1,2,0:T(8,128)(2,1)} %param.22), kind=kOutput, calls=%fused_computation.13 | convolution fusion | flops 3025797120 | bytes 36438016 | tf_op jit(solution)/shard_map/tbxmf,xfd->tbxmd/dot_general | solution.py:124
  150.4 20.2 %bitcast_convert_fusion = bf16[32,2,16,2880]{3,2,1,0:T(8,128)(2,1)} fusion(bf16[2,32,16,2,2880]{4,1,3,0,2:T(8,128)(2,1)} %convert_bitcast_fusion, bf16[2,32,16,16]{3,2,0,1:T(8,128)(2,1)S(1)} %copy.127, s32[2,32,16,16]{3,2,0,1:T(8,128)S(1)} %copy.125, pred[2,32,16,16]{3,2,0,1:T(8,128)(4,1)S(1)} %copy.124), kind=kOutput, calls=%fused_computation.10 | convolution fusion | flops 191791104 | bytes 17809408 | tf_op jit(solution)/shard_map/tbrxm,tbxmd->btrd/dot_general | solution.py:146
  170.7 157.0 %reduce-scatter.2.cloned.1.call-done = bf16[1,2,16,2880]{3,2,1,0:T(8,128)(2,1)} async-done(((bf16[32,2,16,2880]{3,2,1,0:T(8,128)(2,1)}), bf16[1,2,16,2880]{3,2,1,0:T(8,128)(2,1)}) %reduce-scatter.2.cloned.1.call-update) | async-done | bytes 184336 | tf_op jit(solution)/shard_map/reduce_scatter | solution.py:149
  327.7 1.6 fusion.56
  (86 shorter events, 12.0 us)
Async XLA Ops:
  7.2 4.1 %copy-start = (bf16[2880,64]{0,1:T(8,128)(2,1)S(1)}, bf16[2880,64]{0,1:T(8,128)(2,1)}, u32[]{:S(2)}) copy-start(bf16[2880,64]{0,1:T(8,128)(2,1)} %param.18) | copy-start | bytes 1105924
  7.2 78.2 %all-gather.3.cloned.1.call-start = ((), (), s32[]{:S(2)}) async-start(), calls=%async_computation.4 | async-start | bytes 6217728 | tf_op jit(solution)/shard_map/all_gather | solution.py:93
  11.5 7.9 %copy-start.8 = (s32[1,16]{1,0:T(1,128)S(1)}, s32[1,16]{1,0:T(1,128)}, u32[]{:S(2)}) copy-start(s32[1,16]{1,0:T(1,128)} %param.28) | copy-start | bytes 196
  11.5 8.8 %copy-start.6 = (bf16[2,16,512]{2,1,0:T(8,128)(2,1)S(1)}, bf16[2,16,512]{2,1,0:T(8,128)(2,1)}, u32[]{:S(2)}) copy-start(bf16[2,16,512]{2,1,0:T(8,128)(2,1)} %param.24) | copy-start | bytes 98308
  11.5 8.9 %copy-start.7 = (bf16[2,16,512]{2,1,0:T(8,128)(2,1)S(1)}, bf16[2,16,512]{2,1,0:T(8,128)(2,1)}, u32[]{:S(2)}) copy-start(bf16[2,16,512]{2,1,0:T(8,128)(2,1)} %param.25) | copy-start | bytes 98308
  11.5 9.0 %copy-start.4 = (bf16[2,16,4096]{2,1,0:T(8,128)(2,1)S(1)}, bf16[2,16,4096]{2,1,0:T(8,128)(2,1)}, u32[]{:S(2)}) copy-start(bf16[2,16,4096]{2,1,0:T(8,128)(2,1)} %param.23) | copy-start | bytes 786436
  13.1 8.0 %copy-start.2 = (s32[1,32]{1,0:T(1,128)S(1)}, s32[1,32]{1,0:T(1,128)}, u32[]{:S(2)}) copy-start(s32[1,32]{1,0:T(1,128)} %param.29) | copy-start | bytes 388
  14.2 15.0 %all-to-all-start = ((bf16[8,4,16,512]{3,2,1,0:T(8,128)(2,1)}), bf16[8,4,16,512]{3,2,1,0:T(8,128)(2,1)S(1)}, u32[]{:S(2)}, u32[]{:S(2)}) async-start(bf16[8,4,16,512]{3,2,1,0:T(8,128)(2,1)} %param.27), calls=%async_computation | async-start | bytes 1048576 | tf_op jit(solution)/shard_map/all_to_all | solution.py:173
  29.3 13.2 %all-to-all-start.1 = ((bf16[8,4,16,512]{3,2,1,0:T(8,128)(2,1)}), bf16[8,4,16,512]{3,2,1,0:T(8,128)(2,1)S(1)}, u32[]{:S(2)}, u32[]{:S(2)}) async-start(bf16[8,4,16,512]{3,2,1,0:T(8,128)(2,1)} %param.26), calls=%async_computation.1 | async-start | bytes 1048576 | tf_op jit(solution)/shard_map/all_to_all | solution.py:172
  32.8 294.9 %reduce-scatter.2.cloned.1.call-start = ((), (), s32[]{:S(2)}) async-start(), calls=%async_computation.3 | async-start | bytes 6217728 | tf_op jit(solution)/shard_map/reduce_scatter | solution.py:149
  61.1 8.2 %slice-start = ((s8[5242880]{0:T(1024)(128)(4,1)}), s8[4194304]{0:T(1024)(128)(4,1)S(1)}, s32[]{:S(2)}) async-start(s8[5242880]{0:T(1024)(128)(4,1)} %bitcast.96), calls=%async_computation.5 | async-start | bytes 8388608
  61.1 6.6 %copy-start.5 = (f32[2,16,8,8,2]{3,4,0,2,1:T(2,128)S(1)}, f32[2,16,8,8,2]{3,4,0,2,1:T(2,128)}, u32[]{:S(2)}) copy-start(f32[2,16,8,8,2]{3,4,0,2,1:T(2,128)} %get-tuple-element.20) | copy-start | bytes 49156
  61.1 8.2 %slice-start.1 = ((s8[5242880]{0:T(1024)(128)(4,1)}), s8[1048576]{0:T(1024)(128)(4,1)S(1)}, s32[]{:S(2)}) async-start(s8[5242880]{0:T(1024)(128)(4,1)} %bitcast.96), calls=%async_computation.6 | async-start | bytes 2097152
  170.6 158.7 %copy-start.1 = (bf16[2880,64]{0,1:T(8,128)(2,1)S(1)}, bf16[2880,64]{0,1:T(8,128)(2,1)}, u32[]{:S(2)}) copy-start(bf16[2880,64]{0,1:T(8,128)(2,1)} %param.18) | copy-start | bytes 1105924
  170.6 157.1 %copy-start.3 = (bf16[2,16,2880]{2,1,0:T(8,128)(2,1)S(1)}, bf16[2,16,2880]{2,1,0:T(8,128)(2,1)}, u32[]{:S(2)}) copy-start(bf16[2,16,2880]{2,1,0:T(8,128)(2,1)} %param.16) | copy-start | bytes 552964
Sparse Core Ops, SparseCore 0:
  14.4 70.9 all-gather.2
  170.8 156.8 reduce-scatter.1

commit v9 on v6

--- a/solution.py
+++ b/solution.py
@@ -90,7 +90,10 @@
     payload = jnp.concatenate(
         [normed, gate_vals, routes.astype(jnp.bfloat16), filler], axis=-1
     )
-    gathered = lax.all_gather(payload, ("dp", "expert"), axis=1, tiled=False)
+    gathered = [
+        lax.all_gather(payload[t : t + 1], ("dp", "expert"), axis=1, tiled=False)
+        for t in range(steps)
+    ]
     return gathered, residual
 
 
@@ -181,9 +184,16 @@
     context = attention(
         queries, new_key, new_value, space_keys, space_values, page_counts[0], page_order[0]
     )
-    meta = gathered[..., hidden.shape[-1] :]
-    gathered, meta, context = lax.optimization_barrier((gathered, meta, context))
-    layer_out = moe_finish(gathered, meta, residual, routes.shape[-1], w_gate, w_up, w_down)
+    metas = [g[..., hidden.shape[-1] :] for g in gathered]
+    first, first_meta, context = lax.optimization_barrier((gathered[0], metas[0], context))
+    gathered[0], metas[0] = first, first_meta
+    layer_out = jnp.concatenate(
+        [
+            moe_finish(g, m, residual[t : t + 1], routes.shape[-1], w_gate, w_up, w_down)
+            for t, (g, m) in enumerate(zip(gathered, metas))
+        ],
+        axis=0,
+    )
     return (context, layer_out)
 
 

time: 269 us -> 355 us (1.32)
  waiting for transfers between devices: 108 us -> 162 us
  matrix products: 93.7 us -> 121 us
    all_gather x1 -> x2, waiting for transfers between devices: 12.6 us -> 62.5 us  [moe_layer(): lax.all_gather(payload[t:t + 1], ('dp', 'expert'), axis=1, tiled=False)]
    reduce_scatter x1 -> x2, waiting for transfers between devices: 25.4 us -> 43.7 us  [moe_finish(): lax.psum_scatter(row_terms, 'expert', scatter_dimension=1, tiled=True)]
    reduce_scatter x1 -> x2, waiting for transfers between devices: 59.4 us -> 43.9 us  [moe_finish(): lax.psum_scatter(row_terms.reshape((n_dp, n_ex) + row_terms.shape[1:]), '...]
    dot_general x1 -> x2, matrix products: 13.9 us -> 26.7 us  [moe_finish(): jnp.einsum('tbxmd,xdf->tbxmf', slots, w_gate, preferred_element_type=jnp....]
    dot_general x1 -> x2, matrix products: 13.9 us -> 26.3 us  [moe_finish(): jnp.einsum('tbxmd,xdf->tbxmf', slots, w_up, preferred_element_type=jnp.fl...]
    dot_general x1 -> x2, matrix products: 23.1 us -> 26.9 us  [moe_finish(): jnp.einsum('tbxmf,xfd->tbxmd', hidden_act, w_down, preferred_element_type...]
    dot_general x1 -> x2, matrix products: 10.5 us -> 8.18 us  [moe_finish(): jnp.einsum('tbrxm,tbrd->tbxmd', sender.astype(jnp.bfloat16), all_rows, pr...]
    dot_general x1 -> x2, matrix products: 20.2 us -> 22.1 us  [moe_finish(): jnp.einsum('tbrxm,tbxmd->btrd', weights, partial, preferred_element_type=...]
  transfers between devices with their start and end apart: 5 -> 8, of which waited for: 5 -> 7; matrix products, arithmetic and copies ran while one was open for 15% -> 28% of each run, Pallas kernels for 0% -> 0%
where the time goes in v9:
time: 355 us; the launch traced here: 350 us
  waiting for transfers between devices  162 us (46%)
  matrix products  121 us (34%)
  local copies, waits for them, and re-layouts  28.6 us (8%)
  between operations  14.8 us (4%)
  other arithmetic  14 us (4%)
  starting transfers between devices  8.92 us (3%)
    all_gather x2, waiting for transfers between devices, moe_layer(): lax.all_gather(payload[t:t + 1], ('dp', 'expert'), axis=1, tiled=False)  62.5 us
    reduce_scatter x2, waiting for transfers between devices, moe_finish(): lax.psum_scatter(row_terms.reshape((n_dp, n_ex) + row_terms.shape[1:]), '...  43.9 us
    reduce_scatter x2, waiting for transfers between devices, moe_finish(): lax.psum_scatter(row_terms, 'expert', scatter_dimension=1, tiled=True)  43.7 us
    dot_general x2, matrix products, moe_finish(): jnp.einsum('tbxmf,xfd->tbxmd', hidden_act, w_down, preferred_element_type...  26.9 us
    dot_general x2, matrix products, moe_finish(): jnp.einsum('tbxmd,xdf->tbxmf', slots, w_gate, preferred_element_type=jnp....  26.7 us
    dot_general x2, matrix products, moe_finish(): jnp.einsum('tbxmd,xdf->tbxmf', slots, w_up, preferred_element_type=jnp.fl...  26.3 us
    dot_general x2, matrix products, moe_finish(): jnp.einsum('tbrxm,tbxmd->btrd', weights, partial, preferred_element_type=...  22.1 us
    dot_general x2, matrix products, moe_finish(): jnp.einsum('tbrxm,tbrd->tbxmd', sender.astype(jnp.bfloat16), all_rows, pr...  8.18 us
  transfers between devices with their start and end apart: 8, of which 7 were waited for; matrix products, arithmetic and copies ran while one was open for 28% of the time, Pallas kernels for 0%

profile of v9, /device:TPU:0, one launch (start us, length us, event | category | flops | bytes accessed | tf_op | source)
XLA Modules:
  0.0 350.2 jit_solution(12803779579022015728)
XLA Ops:
  15.0 5.2 %all-to-all-start = ((bf16[8,4,16,512]{3,2,1,0:T(8,128)(2,1)}), bf16[8,4,16,512]{3,2,1,0:T(8,128)(2,1)S(1)}, u32[]{:S(2)}, u32[]{:S(2)}) async-start(bf16[8,4,16,512]{3,2,1,0:T(8,128)(2,1)} %param.27), calls=%async_computation | async-start | bytes 1048576 | tf_op jit(solution)/shard_map/all_to_all | solution.py:178
  23.5 7.1 %all-to-all-done = bf16[8,4,16,512]{3,2,1,0:T(8,128)(2,1)S(1)} async-done(((bf16[8,4,16,512]{3,2,1,0:T(8,128)(2,1)}), bf16[8,4,16,512]{3,2,1,0:T(8,128)(2,1)S(1)}, u32[]{:S(2)}, u32[]{:S(2)}) %all-to-all-start) | async-done | bytes 524320 | tf_op jit(solution)/shard_map/all_to_all | solution.py:178
  30.6 3.5 all-to-all-start.1
  34.3 3.2 fusion.140
  39.9 3.9 %all-to-all-done.1 = bf16[8,4,16,512]{3,2,1,0:T(8,128)(2,1)S(1)} async-done(((bf16[8,4,16,512]{3,2,1,0:T(8,128)(2,1)}), bf16[8,4,16,512]{3,2,1,0:T(8,128)(2,1)S(1)}, u32[]{:S(2)}, u32[]{:S(2)}) %all-to-all-start.1) | async-done | bytes 524320 | tf_op jit(solution)/shard_map/all_to_all | solution.py:177
  46.3 4.2 %broadcast_select_fusion = (bf16[160,16,512]{2,1,0:T(8,128)(2,1)}, bf16[160,16,512]{2,1,0:T(8,128)(2,1)S(1)}) fusion(bf16[160,16,512]{2,1,0:T(8,128)(2,1)} %gather_fusion.3, pred[160]{0:T(512)(128)(4,1)S(1)} %get-tuple-element.13, bf16[160,16,512]{2,1,0:T(8,128)(2,1)} %gather_fusion.2), kind=kLoop, calls=%fused_computation.37 | loop fusion | flops 2621440 | bytes 10485920 | tf_op jit(solution)/shard_map/jit(_take)/select_n | solution.py:29
  50.5 7.5 %reshape.468 = bf16[16,160,8,64]{3,2,1,0:T(8,128)(2,1)} reshape(bf16[160,16,512]{2,1,0:T(8,128)(2,1)} %get-tuple-element.25) | data formatting | bytes 5242880 | tf_op jit(solution)/shard_map/reshape | solution.py:29
  58.0 4.6 %reshape.466 = bf16[16,160,8,64]{3,2,1,0:T(8,128)(2,1)} reshape(bf16[160,16,512]{2,1,0:T(8,128)(2,1)S(1)} %get-tuple-element.26) | data formatting | bytes 5242880 | tf_op jit(solution)/shard_map/reshape | solution.py:32
  62.6 5.6 %bitcast_reduce_fusion = (f32[2,16,8,8]{3,0,2,1:T(2,128)S(1)}, f32[16,8,160,2,8]{2,4,3,1,0:T(8,128)S(1)}) fusion(pred[16,160]{1,0:T(8,128)(4,1)S(1)} %iota_compare_fusion.2, bf16[2,16,8,8,64]{4,3,2,1,0:T(8,128)(2,1)S(1)} %reshape.469, bf16[16,160,8,64,1]{3,2,1,0,4:T(8,128)(2,1)} %bitcast.188), kind=kOutput, calls=%fused_computation.40 | convolution fusion | flops 42924032 | bytes 4205056 | tf_op jit(solution)/shard_map/trkgh,rlkh->trkgl/dot_general | solution.py:41
  73.4 2.7 all-gather.5.cloned.1.call-done
  77.5 59.8 %all-gather.7.cloned.1.call-done = bf16[32,16,2944]{2,1,0:T(8,128)(2,1)} async-done(((bf16[1,16,2944]{2,1,0:T(8,128)(2,1)}), bf16[32,16,2944]{2,1,0:T(8,128)(2,1)}) %all-gather.7.cloned.1.call-update) | async-done | bytes 3014672 | tf_op jit(solution)/shard_map/all_gather | solution.py:94
  141.6 4.1 %convolution_convert_fusion = bf16[32,16,2,2880]{3,1,2,0:T(8,128)(2,1)S(1)} fusion(bf16[1,32,16,2944]{3,2,1,0:T(8,128)(2,1)} %bitcast.190, s32[32,16,16]{2,1,0:T(8,128)S(1)} %copy.163, pred[32,16,16]{2,1,0:T(8,128)(4,1)S(1)} %copy.162), kind=kOutput, calls=%fused_computation.24 | convolution fusion | flops 97353728 | bytes 8953856 | tf_op jit(solution)/shard_map/tbrxm,tbrd->tbxmd/dot_general | solution.py:116
  145.8 12.7 %fusion.4 = f32[16,32,2,256]{3,1,2,0:T(8,128)} fusion(bf16[16,2880,256]{2,1,0:T(8,128)(2,1)} %param.20, bf16[32,16,2,2880]{3,1,2,0:T(8,128)(2,1)S(1)} %convolution_convert_fusion), kind=kOutput, calls=%fused_computation.8 | convolution fusion | flops 1509949440 | bytes 30539776 | tf_op jit(solution)/shard_map/tbxmd,xdf->tbxmf/dot_general | solution.py:122
  158.4 12.9 %fusion.88 = bf16[32,16,2,256]{3,0,2,1:T(8,128)(2,1)} fusion(f32[16,32,2,256]{3,1,2,0:T(8,128)} %fusion.4, bf16[16,2880,256]{2,1,0:T(8,128)(2,1)} %param.21, bf16[32,16,2,2880]{3,1,2,0:T(8,128)(2,1)S(1)} %convolution_convert_fusion), kind=kOutput, calls=%fused_computation.59 | convolution fusion | flops 1512046592 | bytes 31064064 | tf_op jit(solution)/shard_map/tbxmd,xdf->tbxmf/dot_general | solution.py:123
  171.3 13.5 %convert_bitcast_fusion = bf16[32,16,2,2880]{3,0,2,1:T(8,128)(2,1)} fusion(bf16[32,16,2,256]{3,0,2,1:T(8,128)(2,1)} %fusion.88, bf16[16,256,2880]{1,2,0:T(8,128)(2,1)} %param.22), kind=kOutput, calls=%fused_computation.22 | convolution fusion | flops 1512898560 | bytes 30015488 | tf_op jit(solution)/shard_map/tbxmf,xfd->tbxmd/dot_general | solution.py:127
  184.8 11.1 %bitcast_convert_fusion = bf16[32,16,2880]{2,1,0:T(8,128)(2,1)} fusion(bf16[32,16,2,2880]{3,0,2,1:T(8,128)(2,1)} %convert_bitcast_fusion, bf16[32,16,16]{2,1,0:T(8,128)(2,1)S(1)} %copy.165, s32[32,16,16]{2,1,0:T(8,128)S(1)} %copy.163, pred[32,16,16]{2,1,0:T(8,128)(4,1)S(1)} %copy.162), kind=kOutput, calls=%fused_computation.16 | convolution fusion | flops 95895552 | bytes 8904704 | tf_op jit(solution)/shard_map/tbrxm,tbxmd->btrd/dot_general | solution.py:149
  197.0 4.1 %convolution_convert_fusion.1 = bf16[32,16,2,2880]{3,1,2,0:T(8,128)(2,1)S(1)} fusion(bf16[1,32,16,2944]{3,2,1,0:T(8,128)(2,1)} %bitcast.192, s32[32,16,16]{2,1,0:T(8,128)S(1)} %copy.152, pred[32,16,16]{2,1,0:T(8,128)(4,1)S(1)} %copy.151), kind=kOutput, calls=%fused_computation.25 | convolution fusion | flops 97353728 | bytes 8953856 | tf_op jit(solution)/shard_map/tbrxm,tbrd->tbxmd/dot_general | solution.py:116
  201.1 14.0 %fusion.6 = f32[16,32,2,256]{3,1,2,0:T(8,128)} fusion(bf16[16,2880,256]{2,1,0:T(8,128)(2,1)} %param.20, bf16[32,16,2,2880]{3,1,2,0:T(8,128)(2,1)S(1)} %convolution_convert_fusion.1), kind=kOutput, calls=%fused_computation.10 | convolution fusion | flops 1509949440 | bytes 30539776 | tf_op jit(solution)/shard_map/tbxmd,xdf->tbxmf/dot_general | solution.py:122
  215.0 13.5 %fusion.83 = bf16[32,16,2,256]{3,0,2,1:T(8,128)(2,1)} fusion(f32[16,32,2,256]{3,1,2,0:T(8,128)} %fusion.6, bf16[16,2880,256]{2,1,0:T(8,128)(2,1)} %param.21, bf16[32,16,2,2880]{3,1,2,0:T(8,128)(2,1)S(1)} %convolution_convert_fusion.1), kind=kOutput, calls=%fused_computation.58 | convolution fusion | flops 1512046592 | bytes 31064064 | tf_op jit(solution)/shard_map/tbxmd,xdf->tbxmf/dot_general | solution.py:123
  228.5 13.5 %convert_bitcast_fusion.1 = bf16[32,16,2,2880]{3,0,2,1:T(8,128)(2,1)} fusion(bf16[32,16,2,256]{3,0,2,1:T(8,128)(2,1)} %fusion.83, bf16[16,256,2880]{1,2,0:T(8,128)(2,1)} %param.22), kind=kOutput, calls=%fused_computation.23 | convolution fusion | flops 1512898560 | bytes 30015488 | tf_op jit(solution)/shard_map/tbxmf,xfd->tbxmd/dot_general | solution.py:127
  242.1 11.0 %bitcast_convert_fusion.1 = bf16[32,16,2880]{2,1,0:T(8,128)(2,1)} fusion(bf16[32,16,2,2880]{3,0,2,1:T(8,128)(2,1)} %convert_bitcast_fusion.1, bf16[32,16,16]{2,1,0:T(8,128)(2,1)S(1)} %copy-done.8, s32[32,16,16]{2,1,0:T(8,128)S(1)} %copy.152, pred[32,16,16]{2,1,0:T(8,128)(4,1)S(1)} %copy-done.7), kind=kOutput, calls=%fused_computation.17 | convolution fusion | flops 95895552 | bytes 8904704 | tf_op jit(solution)/shard_map/tbrxm,tbxmd->btrd/dot_general | solution.py:149
  253.8 43.9 %reduce-scatter.5.cloned.1.call-done = bf16[1,4,1,16,2880]{4,3,1,2,0:T(8,128)(2,1)} async-done(((bf16[8,4,1,16,2880]{4,3,1,2,0:T(8,128)(2,1)}), bf16[1,4,1,16,2880]{4,3,1,2,0:T(8,128)(2,1)}) %reduce-scatter.5.cloned.1.call-update) | async-done | bytes 368656 | tf_op jit(solution)/shard_map/reduce_scatter | solution.py:152
  297.7 22.6 %reduce-scatter.11.cloned.1.call-done = bf16[1,1,16,2880]{3,2,1,0:T(8,128)(2,1)} async-done(((bf16[1,4,16,2880]{3,2,1,0:T(8,128)(2,1)}), bf16[1,1,16,2880]{3,2,1,0:T(8,128)(2,1)}) %reduce-scatter.11.cloned.1.call-update) | async-done | bytes 92176 | tf_op jit(solution)/shard_map/reduce_scatter | solution.py:156
  320.4 21.1 %reduce-scatter.7.cloned.1.call-done = bf16[1,1,16,2880]{3,2,1,0:T(8,128)(2,1)} async-done(((bf16[1,4,16,2880]{3,2,1,0:T(8,128)(2,1)}), bf16[1,1,16,2880]{3,2,1,0:T(8,128)(2,1)}) %reduce-scatter.7.cloned.1.call-update) | async-done | bytes 92176 | tf_op jit(solution)/shard_map/reduce_scatter | solution.py:156
  (121 shorter events, 30.2 us)
Async XLA Ops:
  7.2 4.0 %copy-start = (bf16[2880,64]{0,1:T(8,128)(2,1)S(1)}, bf16[2880,64]{0,1:T(8,128)(2,1)}, u32[]{:S(2)}) copy-start(bf16[2880,64]{0,1:T(8,128)(2,1)} %param.18) | copy-start | bytes 1105924
  7.2 69.0 %all-gather.5.cloned.1.call-start = ((), (), s32[]{:S(2)}) async-start(), calls=%async_computation.10 | async-start | bytes 3108864 | tf_op jit(solution)/shard_map/all_gather | solution.py:94
  11.4 8.8 %copy-start.14 = (s32[1,16]{1,0:T(1,128)S(1)}, s32[1,16]{1,0:T(1,128)}, u32[]{:S(2)}) copy-start(s32[1,16]{1,0:T(1,128)} %param.28) | copy-start | bytes 196
  11.4 9.7 %copy-start.9 = (bf16[2,16,4096]{2,1,0:T(8,128)(2,1)S(1)}, bf16[2,16,4096]{2,1,0:T(8,128)(2,1)}, u32[]{:S(2)}) copy-start(bf16[2,16,4096]{2,1,0:T(8,128)(2,1)} %param.23) | copy-start | bytes 786436
  11.4 10.2 %copy-start.12 = (bf16[2,16,512]{2,1,0:T(8,128)(2,1)S(1)}, bf16[2,16,512]{2,1,0:T(8,128)(2,1)}, u32[]{:S(2)}) copy-start(bf16[2,16,512]{2,1,0:T(8,128)(2,1)} %param.24) | copy-start | bytes 98308
  11.4 10.3 %copy-start.13 = (bf16[2,16,512]{2,1,0:T(8,128)(2,1)S(1)}, bf16[2,16,512]{2,1,0:T(8,128)(2,1)}, u32[]{:S(2)}) copy-start(bf16[2,16,512]{2,1,0:T(8,128)(2,1)} %param.25) | copy-start | bytes 98308
  13.0 8.9 %copy-start.2 = (s32[1,32]{1,0:T(1,128)S(1)}, s32[1,32]{1,0:T(1,128)}, u32[]{:S(2)}) copy-start(s32[1,32]{1,0:T(1,128)} %param.29) | copy-start | bytes 388
  14.3 123.0 %all-gather.7.cloned.1.call-start = ((), (), s32[]{:S(2)}) async-start(), calls=%async_computation.11 | async-start | bytes 3108864 | tf_op jit(solution)/shard_map/all_gather | solution.py:94
  15.0 15.6 %all-to-all-start = ((bf16[8,4,16,512]{3,2,1,0:T(8,128)(2,1)}), bf16[8,4,16,512]{3,2,1,0:T(8,128)(2,1)S(1)}, u32[]{:S(2)}, u32[]{:S(2)}) async-start(bf16[8,4,16,512]{3,2,1,0:T(8,128)(2,1)} %param.27), calls=%async_computation | async-start | bytes 1048576 | tf_op jit(solution)/shard_map/all_to_all | solution.py:178
  30.6 13.2 %all-to-all-start.1 = ((bf16[8,4,16,512]{3,2,1,0:T(8,128)(2,1)}), bf16[8,4,16,512]{3,2,1,0:T(8,128)(2,1)S(1)}, u32[]{:S(2)}, u32[]{:S(2)}) async-start(bf16[8,4,16,512]{3,2,1,0:T(8,128)(2,1)} %param.26), calls=%async_computation.1 | async-start | bytes 1048576 | tf_op jit(solution)/shard_map/all_to_all | solution.py:177
  34.1 219.0 %reduce-scatter.9.cloned.1.call-start = ((), (), s32[]{:S(2)}) async-start(), calls=%async_computation.8 | async-start | bytes 3391488 | tf_op jit(solution)/shard_map/reduce_scatter | solution.py:152
  62.5 5.7 %copy-start.10 = (f32[2,16,8,8,2]{3,4,0,2,1:T(2,128)S(1)}, f32[2,16,8,8,2]{3,4,0,2,1:T(2,128)}, u32[]{:S(2)}) copy-start(f32[2,16,8,8,2]{3,4,0,2,1:T(2,128)} %get-tuple-element.30) | copy-start | bytes 49156
  62.6 7.4 %copy-start.3 = (bf16[16,160,8,64]{3,2,1,0:T(8,128)(2,1)S(1)}, bf16[16,160,8,64]{3,2,1,0:T(8,128)(2,1)}, u32[]{:S(2)}) copy-start(bf16[16,160,8,64]{3,2,1,0:T(8,128)(2,1)} %reshape.466) | copy-start | bytes 7864324
  184.8 12.0 %copy-start.5 = (s32[32,16,16]{2,0,1:T(8,128)S(1)}, s32[32,16,16]{2,0,1:T(8,128)}, u32[]{:S(2)}) copy-start(s32[32,16,16]{2,0,1:T(8,128)} %reduce-window_subtract_fusion.1) | copy-start | bytes 98308
  184.8 12.2 %copy-start.11 = (pred[32,16,16]{2,0,1:T(8,128)(4,1)S(1)}, pred[32,16,16]{2,0,1:T(8,128)(4,1)}, u32[]{:S(2)}) copy-start(pred[32,16,16]{2,0,1:T(8,128)(4,1)} %convert_compare_fusion.1) | copy-start | bytes 24580
  195.9 101.8 %reduce-scatter.5.cloned.1.call-start = ((), (), s32[]{:S(2)}) async-start(), calls=%async_computation.6 | async-start | bytes 3391488 | tf_op jit(solution)/shard_map/reduce_scatter | solution.py:152
  197.0 18.1 %copy-start.6 = (pred[32,16,16]{2,1,0:T(8,128)(4,1)}, pred[32,16,16]{2,1,0:T(8,128)(4,1)S(1)}, u32[]{:S(2)}) copy-start(pred[32,16,16]{2,1,0:T(8,128)(4,1)S(1)} %copy.151) | copy-start | bytes 24580
  228.5 13.5 %copy-start.7 = (pred[32,16,16]{2,1,0:T(8,128)(4,1)S(1)}, pred[32,16,16]{2,1,0:T(8,128)(4,1)}, u32[]{:S(2)}) copy-start(pred[32,16,16]{2,1,0:T(8,128)(4,1)} %copy-done.6) | copy-start | bytes 24580
  228.5 13.5 %copy-start.8 = (bf16[32,16,16]{2,1,0:T(8,128)(2,1)S(1)}, bf16[32,16,16]{2,1,0:T(8,128)(2,1)}, u32[]{:S(2)}) copy-start(bf16[32,16,16]{2,1,0:T(8,128)(2,1)} %copy.154) | copy-start | bytes 49156
  228.5 114.6 %copy-start.1 = (bf16[2880,64]{0,1:T(8,128)(2,1)S(1)}, bf16[2880,64]{0,1:T(8,128)(2,1)}, u32[]{:S(2)}) copy-start(bf16[2880,64]{0,1:T(8,128)(2,1)} %param.18) | copy-start | bytes 1105924
  242.0 55.7 %copy-start.4 = (bf16[2,16,2880]{2,1,0:T(8,128)(2,1)S(1)}, bf16[2,16,2880]{2,1,0:T(8,128)(2,1)}, u32[]{:S(2)}) copy-start(bf16[2,16,2880]{2,1,0:T(8,128)(2,1)} %param.16) | copy-start | bytes 552964
  253.1 67.3 %reduce-scatter.11.cloned.1.call-start = ((), (), s32[]{:S(2)}) async-start(), calls=%async_computation.9 | async-start | bytes 471040 | tf_op jit(solution)/shard_map/reduce_scatter | solution.py:156
  253.7 87.7 %reduce-scatter.7.cloned.1.call-start = ((), (), s32[]{:S(2)}) async-start(), calls=%async_computation.7 | async-start | bytes 471040 | tf_op jit(solution)/shard_map/reduce_scatter | solution.py:156
Sparse Core Ops, SparseCore 0:
  14.4 61.6 all-gather.4
  79.5 57.6 all-gather.6
  196.0 44.2 reduce-scatter.8
  253.2 44.3 reduce-scatter.4
  299.8 20.5 reduce-scatter.10
  322.6 18.7 reduce-scatter.6

commit v10 on v6

--- a/solution.py
+++ b/solution.py
@@ -149,7 +149,9 @@
         row_terms = lax.psum_scatter(
             row_terms.reshape((n_dp, n_ex) + row_terms.shape[1:]), "dp", scatter_dimension=0, tiled=True
         )[0]
-        row_terms = jnp.moveaxis(row_terms, 0, 1)
+        shares = lax.all_to_all(row_terms, "expert", split_axis=0, concat_axis=0, tiled=True)
+        branch_out = jnp.sum(shares.astype(jnp.float32), axis=0)
+        return (residual + branch_out).astype(jnp.bfloat16)
     branch_out = lax.psum_scatter(row_terms, "expert", scatter_dimension=1, tiled=True)
     return (residual + branch_out[:, 0].astype(jnp.float32)).astype(jnp.bfloat16)
 

time: 269 us -> 267 us (level)
  waiting for transfers between devices: 108 us -> 82.4 us
  blocking collectives: 0 us -> 24 us
    reduce_scatter x1 -> x0, waiting for transfers between devices: 25.4 us -> none  [moe_finish(): lax.psum_scatter(row_terms, 'expert', scatter_dimension=1, tiled=True)]
    all_to_all x0 -> x1, blocking collectives: none -> 24 us  [moe_finish(): lax.all_to_all(row_terms, 'expert', split_axis=0, concat_axis=0, tiled=True)]
  transfers between devices with their start and end apart: 5 -> 4, of which waited for: 5 -> 4; matrix products, arithmetic and copies ran while one was open for 15% -> 15% of each run, Pallas kernels for 0% -> 0%
where the time goes in v10:
time: 267 us; the launch traced here: 262 us
  matrix products  93.7 us (35%)
  waiting for transfers between devices  82.4 us (31%)
  local copies, waits for them, and re-layouts  27.8 us (10%)
  blocking collectives  24 us (9%)
  between operations  14.9 us (6%)
  other arithmetic  10.5 us (4%)
  starting transfers between devices  8.76 us (3%)
    reduce_scatter x1, waiting for transfers between devices, moe_finish(): lax.psum_scatter(row_terms.reshape((n_dp, n_ex) + row_terms.shape[1:]), '...  59.4 us
    all_to_all x1, blocking collectives, moe_finish(): lax.all_to_all(row_terms, 'expert', split_axis=0, concat_axis=0, tiled=True)  24 us
    dot_general x1, matrix products, moe_finish(): jnp.einsum('tbxmf,xfd->tbxmd', hidden_act, w_down, preferred_element_type...  23.1 us
    dot_general x1, matrix products, moe_finish(): jnp.einsum('tbrxm,tbxmd->btrd', weights, partial, preferred_element_type=...  20.2 us
    dot_general x1, matrix products, moe_finish(): jnp.einsum('tbxmd,xdf->tbxmf', slots, w_gate, preferred_element_type=jnp....  13.9 us
    dot_general x1, matrix products, moe_finish(): jnp.einsum('tbxmd,xdf->tbxmf', slots, w_up, preferred_element_type=jnp.fl...  13.9 us
    all_gather x1, waiting for transfers between devices, moe_layer(): gathered = lax.all_gather(payload, ('dp', 'expert'), axis=1, tiled=False)  12.6 us
    dot_general x1, matrix products, moe_finish(): jnp.einsum('tbrxm,tbrd->tbxmd', sender.astype(jnp.bfloat16), all_rows, pr...  10.5 us
  transfers between devices with their start and end apart: 4, of which 4 were waited for; matrix products, arithmetic and copies ran while one was open for 15% of the time, Pallas kernels for 0%

profile of v10, /device:TPU:0, one launch (start us, length us, event | category | flops | bytes accessed | tf_op | source)
XLA Modules:
  0.0 262.2 jit_solution(6205403180816961716)
XLA Ops:
  11.5 1.5 gather_fusion.1
  14.2 5.2 %all-to-all-start = ((bf16[8,4,16,512]{3,2,1,0:T(8,128)(2,1)}), bf16[8,4,16,512]{3,2,1,0:T(8,128)(2,1)S(1)}, u32[]{:S(2)}, u32[]{:S(2)}) async-start(bf16[8,4,16,512]{3,2,1,0:T(8,128)(2,1)} %param.27), calls=%async_computation | async-start | bytes 1048576 | tf_op jit(solution)/shard_map/all_to_all | solution.py:177
  21.1 1.6 gather_fusion
  22.7 6.6 %all-to-all-done = bf16[8,4,16,512]{3,2,1,0:T(8,128)(2,1)S(1)} async-done(((bf16[8,4,16,512]{3,2,1,0:T(8,128)(2,1)}), bf16[8,4,16,512]{3,2,1,0:T(8,128)(2,1)S(1)}, u32[]{:S(2)}, u32[]{:S(2)}) %all-to-all-start) | async-done | bytes 524320 | tf_op jit(solution)/shard_map/all_to_all | solution.py:177
  29.3 3.5 %all-to-all-start.1 = ((bf16[8,4,16,512]{3,2,1,0:T(8,128)(2,1)}), bf16[8,4,16,512]{3,2,1,0:T(8,128)(2,1)S(1)}, u32[]{:S(2)}, u32[]{:S(2)}) async-start(bf16[8,4,16,512]{3,2,1,0:T(8,128)(2,1)} %param.26), calls=%async_computation.1 | async-start | bytes 1048576 | tf_op jit(solution)/shard_map/all_to_all | solution.py:176
  32.9 3.2 %fusion.68 = (f32[2,16,8,8]{3,0,2,1:T(2,128)S(1)}, f32[2,16,8,8,2]{3,4,0,2,1:T(2,128)}) fusion(bf16[2,16,8,8,64]{4,3,2,1,0:T(8,128)(2,1)S(1)} %reshape.268, bf16[2,16,8,64,1]{3,2,1,0,4:T(8,128)(2,1)S(1)} %bitcast.102, pred[2,2]{1,0:T(4,128)(4,1)S(1)} %iota_compare_fusion.3), kind=kOutput, calls=%fused_computation.101 | convolution fusion | flops 534528 | bytes 319492 | tf_op jit(solution)/shard_map/trkgh,urkh->trkgu/dot_general | solution.py:46
  36.1 2.5 gather_fusion.2
  38.6 3.9 %all-to-all-done.1 = bf16[8,4,16,512]{3,2,1,0:T(8,128)(2,1)S(1)} async-done(((bf16[8,4,16,512]{3,2,1,0:T(8,128)(2,1)}), bf16[8,4,16,512]{3,2,1,0:T(8,128)(2,1)S(1)}, u32[]{:S(2)}, u32[]{:S(2)}) %all-to-all-start.1) | async-done | bytes 524320 | tf_op jit(solution)/shard_map/all_to_all | solution.py:176
  42.4 2.5 gather_fusion.3
  44.9 4.1 %broadcast_select_fusion = (bf16[160,16,512]{2,1,0:T(8,128)(2,1)}, bf16[160,16,512]{2,1,0:T(8,128)(2,1)S(1)}) fusion(bf16[160,16,512]{2,1,0:T(8,128)(2,1)} %gather_fusion.3, pred[160]{0:T(512)(128)(4,1)S(1)} %get-tuple-element.9, bf16[160,16,512]{2,1,0:T(8,128)(2,1)} %gather_fusion.2), kind=kLoop, calls=%fused_computation.23 | loop fusion | flops 2621440 | bytes 10485920 | tf_op jit(solution)/shard_map/jit(_take)/select_n | solution.py:29
  49.1 7.5 %reshape.267 = bf16[16,160,8,64]{3,2,1,0:T(8,128)(2,1)} reshape(bf16[160,16,512]{2,1,0:T(8,128)(2,1)} %get-tuple-element.15) | data formatting | bytes 5242880 | tf_op jit(solution)/shard_map/reshape | solution.py:29
  56.5 4.6 %reshape.265 = bf16[16,160,8,64]{3,2,1,0:T(8,128)(2,1)} reshape(bf16[160,16,512]{2,1,0:T(8,128)(2,1)S(1)} %get-tuple-element.16) | data formatting | bytes 5242880 | tf_op jit(solution)/shard_map/reshape | solution.py:32
  61.1 6.5 %bitcast_reduce_fusion = (f32[2,16,8,8]{3,0,2,1:T(2,128)S(1)}, f32[16,8,160,2,8]{2,4,3,1,0:T(8,128)S(1)}) fusion(pred[16,160]{1,0:T(8,128)(4,1)S(1)} %iota_compare_fusion.1, bf16[2,16,8,8,64]{4,3,2,1,0:T(8,128)(2,1)S(1)} %reshape.268, bf16[16,160,8,64,1]{3,2,1,0,4:T(8,128)(2,1)} %bitcast.99), kind=kOutput, calls=%fused_computation.26 | convolution fusion | flops 42924032 | bytes 4205056 | tf_op jit(solution)/shard_map/trkgh,rlkh->trkgl/dot_general | solution.py:41
  69.3 1.5 fusion.27
  71.6 1.2 convert_element_type.77
  72.8 12.6 %all-gather.3.cloned.1.call-done = bf16[2,512,2944]{2,1,0:T(8,128)(2,1)} async-done(((bf16[2,16,2944]{2,1,0:T(8,128)(2,1)}), bf16[2,512,2944]{2,1,0:T(8,128)(2,1)}) %all-gather.3.cloned.1.call-update) | async-done | bytes 6029328 | tf_op jit(solution)/shard_map/all_gather | solution.py:93
  85.4 1.1 slice.25
  88.9 10.5 %convolution_convert_fusion = bf16[2,32,16,2,2880]{4,2,3,1,0:T(8,128)(2,1)} fusion(bf16[2,32,16,2944]{3,2,1,0:T(8,128)(2,1)} %bitcast.93, s32[2,32,16,16]{3,2,0,1:T(8,128)S(1)} %copy.125, pred[2,32,16,16]{3,2,0,1:T(8,128)(4,1)S(1)} %copy.124), kind=kOutput, calls=%fused_computation.16 | convolution fusion | flops 194707456 | bytes 17907712 | tf_op jit(solution)/shard_map/tbrxm,tbrd->tbxmd/dot_general | solution.py:113
  99.4 13.9 %fusion.4 = f32[16,2,32,2,256]{4,2,3,1,0:T(8,128)S(1)} fusion(bf16[16,2880,256]{2,1,0:T(8,128)(2,1)} %param.21, bf16[2,32,16,2,2880]{4,2,3,1,0:T(8,128)(2,1)} %convolution_convert_fusion), kind=kOutput, calls=%fused_computation.8 | convolution fusion | flops 3019898880 | bytes 37486592 | tf_op jit(solution)/shard_map/tbxmd,xdf->tbxmf/dot_general | solution.py:120
  113.4 13.9 %fusion.32 = bf16[2,32,16,2,256]{4,1,3,0,2:T(8,128)(2,1)S(1)} fusion(bf16[16,2880,256]{2,1,0:T(8,128)(2,1)} %param.20, bf16[2,32,16,2,2880]{4,2,3,1,0:T(8,128)(2,1)} %convolution_convert_fusion, f32[16,2,32,2,256]{4,2,3,1,0:T(8,128)S(1)} %fusion.4), kind=kOutput, calls=%fused_computation.37 | convolution fusion | flops 3024093184 | bytes 38535168 | tf_op jit(solution)/shard_map/tbxmd,xdf->tbxmf/dot_general | solution.py:119
  127.3 23.1 %convert_bitcast_fusion = bf16[2,32,16,2,2880]{4,1,3,0,2:T(8,128)(2,1)} fusion(bf16[2,32,16,2,256]{4,1,3,0,2:T(8,128)(2,1)S(1)} %fusion.32, bf16[16,256,2880]{1,2,0:T(8,128)(2,1)} %param.22), kind=kOutput, calls=%fused_computation.13 | convolution fusion | flops 3025797120 | bytes 36438016 | tf_op jit(solution)/shard_map/tbxmf,xfd->tbxmd/dot_general | solution.py:124
  150.4 20.2 %bitcast_convert_fusion = bf16[32,2,16,2880]{3,2,1,0:T(8,128)(2,1)} fusion(bf16[2,32,16,2,2880]{4,1,3,0,2:T(8,128)(2,1)} %convert_bitcast_fusion, bf16[2,32,16,16]{3,2,0,1:T(8,128)(2,1)S(1)} %copy.127, s32[2,32,16,16]{3,2,0,1:T(8,128)S(1)} %copy.125, pred[2,32,16,16]{3,2,0,1:T(8,128)(4,1)S(1)} %copy.124), kind=kOutput, calls=%fused_computation.10 | convolution fusion | flops 191791104 | bytes 17809408 | tf_op jit(solution)/shard_map/tbrxm,tbxmd->btrd/dot_general | solution.py:146
  170.7 59.4 %reduce-scatter.2.cloned.1.call-done = bf16[1,4,2,16,2880]{4,3,2,1,0:T(8,128)(2,1)} async-done(((bf16[8,4,2,16,2880]{4,3,2,1,0:T(8,128)(2,1)}), bf16[1,4,2,16,2880]{4,3,2,1,0:T(8,128)(2,1)}) %reduce-scatter.2.cloned.1.call-update) | async-done | bytes 737296 | tf_op jit(solution)/shard_map/reduce_scatter | solution.py:149
  230.1 24.0 %all_to_all.15 = bf16[4,2,16,2880]{3,2,1,0:T(8,128)(2,1)S(1)} all-to-all(bf16[4,2,16,2880]{3,2,1,0:T(8,128)(2,1)} %bitcast.100), channel_id=1, replica_groups=mesh['dp'=8,'expert'=4] {'expert'}, dimensions={0} | all-to-all | bytes 1474560 | tf_op jit(solution)/shard_map/all_to_all | solution.py:152
  (88 shorter events, 12.8 us)
Async XLA Ops:
  7.2 4.1 %copy-start = (bf16[2880,64]{0,1:T(8,128)(2,1)S(1)}, bf16[2880,64]{0,1:T(8,128)(2,1)}, u32[]{:S(2)}) copy-start(bf16[2880,64]{0,1:T(8,128)(2,1)} %param.18) | copy-start | bytes 1105924
  7.2 78.2 %all-gather.3.cloned.1.call-start = ((), (), s32[]{:S(2)}) async-start(), calls=%async_computation.5 | async-start | bytes 6217728 | tf_op jit(solution)/shard_map/all_gather | solution.py:93
  11.5 7.9 %copy-start.8 = (s32[1,16]{1,0:T(1,128)S(1)}, s32[1,16]{1,0:T(1,128)}, u32[]{:S(2)}) copy-start(s32[1,16]{1,0:T(1,128)} %param.28) | copy-start | bytes 196
  11.5 8.8 %copy-start.6 = (bf16[2,16,512]{2,1,0:T(8,128)(2,1)S(1)}, bf16[2,16,512]{2,1,0:T(8,128)(2,1)}, u32[]{:S(2)}) copy-start(bf16[2,16,512]{2,1,0:T(8,128)(2,1)} %param.24) | copy-start | bytes 98308
  11.5 8.9 %copy-start.7 = (bf16[2,16,512]{2,1,0:T(8,128)(2,1)S(1)}, bf16[2,16,512]{2,1,0:T(8,128)(2,1)}, u32[]{:S(2)}) copy-start(bf16[2,16,512]{2,1,0:T(8,128)(2,1)} %param.25) | copy-start | bytes 98308
  11.5 9.0 %copy-start.4 = (bf16[2,16,4096]{2,1,0:T(8,128)(2,1)S(1)}, bf16[2,16,4096]{2,1,0:T(8,128)(2,1)}, u32[]{:S(2)}) copy-start(bf16[2,16,4096]{2,1,0:T(8,128)(2,1)} %param.23) | copy-start | bytes 786436
  13.1 8.0 %copy-start.2 = (s32[1,32]{1,0:T(1,128)S(1)}, s32[1,32]{1,0:T(1,128)}, u32[]{:S(2)}) copy-start(s32[1,32]{1,0:T(1,128)} %param.29) | copy-start | bytes 388
  14.2 15.0 %all-to-all-start = ((bf16[8,4,16,512]{3,2,1,0:T(8,128)(2,1)}), bf16[8,4,16,512]{3,2,1,0:T(8,128)(2,1)S(1)}, u32[]{:S(2)}, u32[]{:S(2)}) async-start(bf16[8,4,16,512]{3,2,1,0:T(8,128)(2,1)} %param.27), calls=%async_computation | async-start | bytes 1048576 | tf_op jit(solution)/shard_map/all_to_all | solution.py:177
  29.3 13.2 %all-to-all-start.1 = ((bf16[8,4,16,512]{3,2,1,0:T(8,128)(2,1)}), bf16[8,4,16,512]{3,2,1,0:T(8,128)(2,1)S(1)}, u32[]{:S(2)}, u32[]{:S(2)}) async-start(bf16[8,4,16,512]{3,2,1,0:T(8,128)(2,1)} %param.26), calls=%async_computation.1 | async-start | bytes 1048576 | tf_op jit(solution)/shard_map/all_to_all | solution.py:176
  32.8 197.3 %reduce-scatter.2.cloned.1.call-start = ((), (), s32[]{:S(2)}) async-start(), calls=%async_computation.4 | async-start | bytes 6782976 | tf_op jit(solution)/shard_map/reduce_scatter | solution.py:149
  61.1 8.2 %slice-start = ((s8[5242880]{0:T(1024)(128)(4,1)}), s8[4194304]{0:T(1024)(128)(4,1)S(1)}, s32[]{:S(2)}) async-start(s8[5242880]{0:T(1024)(128)(4,1)} %bitcast.96), calls=%async_computation.6 | async-start | bytes 8388608
  61.1 6.6 %copy-start.5 = (f32[2,16,8,8,2]{3,4,0,2,1:T(2,128)S(1)}, f32[2,16,8,8,2]{3,4,0,2,1:T(2,128)}, u32[]{:S(2)}) copy-start(f32[2,16,8,8,2]{3,4,0,2,1:T(2,128)} %get-tuple-element.20) | copy-start | bytes 49156
  61.1 8.2 %slice-start.1 = ((s8[5242880]{0:T(1024)(128)(4,1)}), s8[1048576]{0:T(1024)(128)(4,1)S(1)}, s32[]{:S(2)}) async-start(s8[5242880]{0:T(1024)(128)(4,1)} %bitcast.96), calls=%async_computation.7 | async-start | bytes 2097152
  170.6 83.6 %copy-start.3 = (bf16[2,16,2880]{2,1,0:T(8,128)(2,1)S(1)}, bf16[2,16,2880]{2,1,0:T(8,128)(2,1)}, u32[]{:S(2)}) copy-start(bf16[2,16,2880]{2,1,0:T(8,128)(2,1)} %param.16) | copy-start | bytes 552964
  170.7 84.3 %copy-start.1 = (bf16[2880,64]{0,1:T(8,128)(2,1)S(1)}, bf16[2880,64]{0,1:T(8,128)(2,1)}, u32[]{:S(2)}) copy-start(bf16[2880,64]{0,1:T(8,128)(2,1)} %param.18) | copy-start | bytes 1105924
Sparse Core Ops, SparseCore 0:
  14.4 70.9 all-gather.2
  170.8 59.2 reduce-scatter.1

commit v11 on v10

--- a/solution.py
+++ b/solution.py
@@ -146,9 +146,10 @@
         row_terms = jnp.einsum(
             "tbrxm,tbxmd->btrd", weights, partial, preferred_element_type=jnp.float32
         ).astype(jnp.bfloat16)
-        row_terms = lax.psum_scatter(
-            row_terms.reshape((n_dp, n_ex) + row_terms.shape[1:]), "dp", scatter_dimension=0, tiled=True
-        )[0]
+        row_terms = lax.all_to_all(
+            row_terms.reshape((n_dp, n_ex) + row_terms.shape[1:]), "dp", split_axis=0, concat_axis=0, tiled=True
+        )
+        row_terms = jnp.sum(row_terms.astype(jnp.float32), axis=0).astype(jnp.bfloat16)
         shares = lax.all_to_all(row_terms, "expert", split_axis=0, concat_axis=0, tiled=True)
         branch_out = jnp.sum(shares.astype(jnp.float32), axis=0)
         return (residual + branch_out).astype(jnp.bfloat16)

time: 267 us -> 278 us (1.041)
  blocking collectives: 24 us -> 94.4 us
  waiting for transfers between devices: 82.4 us -> 22.9 us
  other arithmetic: 10.5 us -> 14.3 us
    all_to_all x0 -> x1, blocking collectives: none -> 72.1 us  [moe_finish(): lax.all_to_all(row_terms.reshape((n_dp, n_ex) + row_terms.shape[1:]), 'dp...]
    reduce_scatter x1 -> x0, waiting for transfers between devices: 59.4 us -> none  [moe_finish(): lax.psum_scatter(row_terms.reshape((n_dp, n_ex) + row_terms.shape[1:]), '...]
    reduce_sum x0 -> x1, other arithmetic: none -> 3.73 us  [moe_finish(): jnp.sum(row_terms.astype(jnp.float32), axis=0).astype(jnp.bfloat16)]
  transfers between devices with their start and end apart: 4 -> 3, of which waited for: 4 -> 3; matrix products, arithmetic and copies ran while one was open for 15% -> 14% of each run, Pallas kernels for 0% -> 0%
where the time goes in v11:
time: 278 us; the launch traced here: 274 us
  blocking collectives  94.4 us (34%)
  matrix products  91 us (33%)
  local copies, waits for them, and re-layouts  27.8 us (10%)
  waiting for transfers between devices  22.9 us (8%)
  between operations  14.8 us (5%)
  other arithmetic  14.3 us (5%)
  starting transfers between devices  9.24 us (3%)
    all_to_all x1, blocking collectives, moe_finish(): lax.all_to_all(row_terms.reshape((n_dp, n_ex) + row_terms.shape[1:]), 'dp...  72.1 us
    dot_general x1, matrix products, moe_finish(): jnp.einsum('tbxmf,xfd->tbxmd', hidden_act, w_down, preferred_element_type...  23.1 us
    all_to_all x1, blocking collectives, moe_finish(): lax.all_to_all(row_terms, 'expert', split_axis=0, concat_axis=0, tiled=True)  22.3 us
    dot_general x1, matrix products, moe_finish(): jnp.einsum('tbrxm,tbxmd->btrd', weights, partial, preferred_element_type=...  17.9 us
    dot_general x1, matrix products, moe_finish(): jnp.einsum('tbxmd,xdf->tbxmf', slots, w_gate, preferred_element_type=jnp....  13.9 us
    dot_general x1, matrix products, moe_finish(): jnp.einsum('tbxmd,xdf->tbxmf', slots, w_up, preferred_element_type=jnp.fl...  13.7 us
    all_gather x1, waiting for transfers between devices, moe_layer(): gathered = lax.all_gather(payload, ('dp', 'expert'), axis=1, tiled=False)  12.4 us
    dot_general x1, matrix products, moe_finish(): jnp.einsum('tbrxm,tbrd->tbxmd', sender.astype(jnp.bfloat16), all_rows, pr...  10.5 us
  transfers between devices with their start and end apart: 3, of which 3 were waited for; matrix products, arithmetic and copies ran while one was open for 14% of the time, Pallas kernels for 0%

profile of v11, /device:TPU:0, one launch (start us, length us, event | category | flops | bytes accessed | tf_op | source)
XLA Modules:
  0.0 274.3 jit_solution(17295828154106642725)
XLA Ops:
  11.5 1.5 gather_fusion.1
  14.2 5.2 %all-to-all-start = ((bf16[8,4,16,512]{3,2,1,0:T(8,128)(2,1)}), bf16[8,4,16,512]{3,2,1,0:T(8,128)(2,1)S(1)}, u32[]{:S(2)}, u32[]{:S(2)}) async-start(bf16[8,4,16,512]{3,2,1,0:T(8,128)(2,1)} %param.27), calls=%async_computation | async-start | bytes 1048576 | tf_op jit(solution)/shard_map/all_to_all | solution.py:178
  21.1 1.6 gather_fusion
  22.7 6.6 %all-to-all-done = bf16[8,4,16,512]{3,2,1,0:T(8,128)(2,1)S(1)} async-done(((bf16[8,4,16,512]{3,2,1,0:T(8,128)(2,1)}), bf16[8,4,16,512]{3,2,1,0:T(8,128)(2,1)S(1)}, u32[]{:S(2)}, u32[]{:S(2)}) %all-to-all-start) | async-done | bytes 524320 | tf_op jit(solution)/shard_map/all_to_all | solution.py:178
  29.3 4.0 %all-to-all-start.1 = ((bf16[8,4,16,512]{3,2,1,0:T(8,128)(2,1)}), bf16[8,4,16,512]{3,2,1,0:T(8,128)(2,1)S(1)}, u32[]{:S(2)}, u32[]{:S(2)}) async-start(bf16[8,4,16,512]{3,2,1,0:T(8,128)(2,1)} %param.26), calls=%async_computation.1 | async-start | bytes 1048576 | tf_op jit(solution)/shard_map/all_to_all | solution.py:177
  33.4 3.2 %fusion.68 = (f32[2,16,8,8]{3,0,2,1:T(2,128)S(1)}, f32[2,16,8,8,2]{3,4,0,2,1:T(2,128)}) fusion(bf16[2,16,8,8,64]{4,3,2,1,0:T(8,128)(2,1)S(1)} %reshape.268, bf16[2,16,8,64,1]{3,2,1,0,4:T(8,128)(2,1)S(1)} %bitcast.100, pred[2,2]{1,0:T(4,128)(4,1)S(1)} %iota_compare_fusion.3), kind=kOutput, calls=%fused_computation.101 | convolution fusion | flops 534528 | bytes 319492 | tf_op jit(solution)/shard_map/trkgh,urkh->trkgu/dot_general | solution.py:46
  36.6 2.5 gather_fusion.2
  39.0 3.9 %all-to-all-done.1 = bf16[8,4,16,512]{3,2,1,0:T(8,128)(2,1)S(1)} async-done(((bf16[8,4,16,512]{3,2,1,0:T(8,128)(2,1)}), bf16[8,4,16,512]{3,2,1,0:T(8,128)(2,1)S(1)}, u32[]{:S(2)}, u32[]{:S(2)}) %all-to-all-start.1) | async-done | bytes 524320 | tf_op jit(solution)/shard_map/all_to_all | solution.py:177
  43.0 2.5 gather_fusion.3
  45.4 4.0 %broadcast_select_fusion = (bf16[160,16,512]{2,1,0:T(8,128)(2,1)}, bf16[160,16,512]{2,1,0:T(8,128)(2,1)S(1)}) fusion(bf16[160,16,512]{2,1,0:T(8,128)(2,1)} %gather_fusion.3, pred[160]{0:T(512)(128)(4,1)S(1)} %get-tuple-element.9, bf16[160,16,512]{2,1,0:T(8,128)(2,1)} %gather_fusion.2), kind=kLoop, calls=%fused_computation.23 | loop fusion | flops 2621440 | bytes 10485920 | tf_op jit(solution)/shard_map/jit(_take)/select_n | solution.py:29
  49.4 7.5 %reshape.267 = bf16[16,160,8,64]{3,2,1,0:T(8,128)(2,1)} reshape(bf16[160,16,512]{2,1,0:T(8,128)(2,1)} %get-tuple-element.15) | data formatting | bytes 5242880 | tf_op jit(solution)/shard_map/reshape | solution.py:29
  56.9 4.6 %reshape.265 = bf16[16,160,8,64]{3,2,1,0:T(8,128)(2,1)} reshape(bf16[160,16,512]{2,1,0:T(8,128)(2,1)S(1)} %get-tuple-element.16) | data formatting | bytes 5242880 | tf_op jit(solution)/shard_map/reshape | solution.py:32
  61.5 6.3 %bitcast_reduce_fusion = (f32[2,16,8,8]{3,0,2,1:T(2,128)S(1)}, f32[16,8,160,2,8]{2,4,3,1,0:T(8,128)S(1)}) fusion(pred[16,160]{1,0:T(8,128)(4,1)S(1)} %iota_compare_fusion.1, bf16[2,16,8,8,64]{4,3,2,1,0:T(8,128)(2,1)S(1)} %reshape.268, bf16[16,160,8,64,1]{3,2,1,0,4:T(8,128)(2,1)} %bitcast.98), kind=kOutput, calls=%fused_computation.26 | convolution fusion | flops 42924032 | bytes 4205056 | tf_op jit(solution)/shard_map/trkgh,rlkh->trkgl/dot_general | solution.py:41
  69.5 1.5 fusion.27
  71.8 1.2 convert_element_type.79
  73.0 12.4 %all-gather.3.cloned.1.call-done = bf16[2,512,2944]{2,1,0:T(8,128)(2,1)} async-done(((bf16[2,16,2944]{2,1,0:T(8,128)(2,1)}), bf16[2,512,2944]{2,1,0:T(8,128)(2,1)}) %all-gather.3.cloned.1.call-update) | async-done | bytes 6029328 | tf_op jit(solution)/shard_map/all_gather | solution.py:93
  89.1 10.5 %convolution_convert_fusion = bf16[2,32,16,2,2880]{4,2,3,1,0:T(8,128)(2,1)} fusion(bf16[2,32,16,2944]{3,2,1,0:T(8,128)(2,1)} %bitcast.92, s32[2,32,16,16]{3,2,0,1:T(8,128)S(1)} %copy.125, pred[2,32,16,16]{3,2,0,1:T(8,128)(4,1)S(1)} %copy.124), kind=kOutput, calls=%fused_computation.16 | convolution fusion | flops 194707456 | bytes 17907712 | tf_op jit(solution)/shard_map/tbrxm,tbrd->tbxmd/dot_general | solution.py:113
  99.6 13.7 %fusion.4 = f32[16,2,32,2,256]{4,2,3,1,0:T(8,128)S(1)} fusion(bf16[16,2880,256]{2,1,0:T(8,128)(2,1)} %param.21, bf16[2,32,16,2,2880]{4,2,3,1,0:T(8,128)(2,1)} %convolution_convert_fusion), kind=kOutput, calls=%fused_computation.8 | convolution fusion | flops 3019898880 | bytes 37486592 | tf_op jit(solution)/shard_map/tbxmd,xdf->tbxmf/dot_general | solution.py:120
  113.3 13.9 %fusion.32 = bf16[2,32,16,2,256]{4,1,3,0,2:T(8,128)(2,1)S(1)} fusion(bf16[16,2880,256]{2,1,0:T(8,128)(2,1)} %param.20, bf16[2,32,16,2,2880]{4,2,3,1,0:T(8,128)(2,1)} %convolution_convert_fusion, f32[16,2,32,2,256]{4,2,3,1,0:T(8,128)S(1)} %fusion.4), kind=kOutput, calls=%fused_computation.37 | convolution fusion | flops 3024093184 | bytes 38535168 | tf_op jit(solution)/shard_map/tbxmd,xdf->tbxmf/dot_general | solution.py:119
  127.3 23.1 %convert_bitcast_fusion = bf16[2,32,16,2,2880]{4,1,3,0,2:T(8,128)(2,1)} fusion(bf16[2,32,16,2,256]{4,1,3,0,2:T(8,128)(2,1)S(1)} %fusion.32, bf16[16,256,2880]{1,2,0:T(8,128)(2,1)} %param.22), kind=kOutput, calls=%fused_computation.13 | convolution fusion | flops 3025797120 | bytes 36438016 | tf_op jit(solution)/shard_map/tbxmf,xfd->tbxmd/dot_general | solution.py:124
  150.4 17.9 %bitcast_convert_fusion = bf16[32,2,16,2880]{3,2,1,0:T(8,128)(2,1)S(1)} fusion(bf16[2,32,16,2,2880]{4,1,3,0,2:T(8,128)(2,1)} %convert_bitcast_fusion, bf16[2,32,16,16]{3,2,0,1:T(8,128)(2,1)S(1)} %copy.127, s32[2,32,16,16]{3,2,0,1:T(8,128)S(1)} %copy.125, pred[2,32,16,16]{3,2,0,1:T(8,128)(4,1)S(1)} %copy.124), kind=kOutput, calls=%fused_computation.10 | convolution fusion | flops 191791104 | bytes 17809408 | tf_op jit(solution)/shard_map/tbrxm,tbxmd->btrd/dot_general | solution.py:146
  168.2 72.1 %all_to_all.20 = bf16[8,4,2,16,2880]{4,3,2,1,0:T(8,128)(2,1)} all-to-all(bf16[8,4,2,16,2880]{4,3,2,1,0:T(8,128)(2,1)S(1)} %bitcast.90), channel_id=1, replica_groups=mesh['dp'=8,'expert'=4] {'dp'}, dimensions={0} | all-to-all | bytes 11796480 | tf_op jit(solution)/shard_map/all_to_all | solution.py:149
  240.3 3.7 %reduce_sum.71 = bf16[4,2,16,2880]{3,2,1,0:T(8,128)(2,1)S(1)} reduce(bf16[8,4,2,16,2880]{4,3,2,1,0:T(8,128)(2,1)} %all_to_all.20, bf16[]{:T(256)} %constant.44.clone.1), dimensions={0}, to_apply=%region_10.12 | reduce | flops 2580480 | bytes 6635522 | tf_op jit(solution)/shard_map/reduce_sum | solution.py:152
  244.0 22.3 %all_to_all.21 = bf16[4,2,16,2880]{3,2,1,0:T(8,128)(2,1)S(1)} all-to-all(bf16[4,2,16,2880]{3,2,1,0:T(8,128)(2,1)S(1)} %reduce_sum.71), channel_id=1, replica_groups=mesh['dp'=8,'expert'=4] {'expert'}, dimensions={0} | all-to-all | bytes 1474560 | tf_op jit(solution)/shard_map/all_to_all | solution.py:153
  (87 shorter events, 14.0 us)
Async XLA Ops:
  7.2 4.1 %copy-start = (bf16[2880,64]{0,1:T(8,128)(2,1)S(1)}, bf16[2880,64]{0,1:T(8,128)(2,1)}, u32[]{:S(2)}) copy-start(bf16[2880,64]{0,1:T(8,128)(2,1)} %param.18) | copy-start | bytes 1105924
  7.2 78.2 %all-gather.3.cloned.1.call-start = ((), (), s32[]{:S(2)}) async-start(), calls=%async_computation.4 | async-start | bytes 6217728 | tf_op jit(solution)/shard_map/all_gather | solution.py:93
  11.5 7.9 %copy-start.8 = (s32[1,16]{1,0:T(1,128)S(1)}, s32[1,16]{1,0:T(1,128)}, u32[]{:S(2)}) copy-start(s32[1,16]{1,0:T(1,128)} %param.28) | copy-start | bytes 196
  11.5 8.8 %copy-start.6 = (bf16[2,16,512]{2,1,0:T(8,128)(2,1)S(1)}, bf16[2,16,512]{2,1,0:T(8,128)(2,1)}, u32[]{:S(2)}) copy-start(bf16[2,16,512]{2,1,0:T(8,128)(2,1)} %param.24) | copy-start | bytes 98308
  11.5 8.9 %copy-start.7 = (bf16[2,16,512]{2,1,0:T(8,128)(2,1)S(1)}, bf16[2,16,512]{2,1,0:T(8,128)(2,1)}, u32[]{:S(2)}) copy-start(bf16[2,16,512]{2,1,0:T(8,128)(2,1)} %param.25) | copy-start | bytes 98308
  11.5 9.0 %copy-start.4 = (bf16[2,16,4096]{2,1,0:T(8,128)(2,1)S(1)}, bf16[2,16,4096]{2,1,0:T(8,128)(2,1)}, u32[]{:S(2)}) copy-start(bf16[2,16,4096]{2,1,0:T(8,128)(2,1)} %param.23) | copy-start | bytes 786436
  13.1 8.0 %copy-start.2 = (s32[1,32]{1,0:T(1,128)S(1)}, s32[1,32]{1,0:T(1,128)}, u32[]{:S(2)}) copy-start(s32[1,32]{1,0:T(1,128)} %param.29) | copy-start | bytes 388
  14.2 15.0 %all-to-all-start = ((bf16[8,4,16,512]{3,2,1,0:T(8,128)(2,1)}), bf16[8,4,16,512]{3,2,1,0:T(8,128)(2,1)S(1)}, u32[]{:S(2)}, u32[]{:S(2)}) async-start(bf16[8,4,16,512]{3,2,1,0:T(8,128)(2,1)} %param.27), calls=%async_computation | async-start | bytes 1048576 | tf_op jit(solution)/shard_map/all_to_all | solution.py:178
  29.3 13.7 %all-to-all-start.1 = ((bf16[8,4,16,512]{3,2,1,0:T(8,128)(2,1)}), bf16[8,4,16,512]{3,2,1,0:T(8,128)(2,1)S(1)}, u32[]{:S(2)}, u32[]{:S(2)}) async-start(bf16[8,4,16,512]{3,2,1,0:T(8,128)(2,1)} %param.26), calls=%async_computation.1 | async-start | bytes 1048576 | tf_op jit(solution)/shard_map/all_to_all | solution.py:177
  61.5 8.0 %slice-start = ((s8[5242880]{0:T(1024)(128)(4,1)}), s8[4194304]{0:T(1024)(128)(4,1)S(1)}, s32[]{:S(2)}) async-start(s8[5242880]{0:T(1024)(128)(4,1)} %bitcast.95), calls=%async_computation.5 | async-start | bytes 8388608
  61.5 6.4 %copy-start.5 = (f32[2,16,8,8,2]{3,4,0,2,1:T(2,128)S(1)}, f32[2,16,8,8,2]{3,4,0,2,1:T(2,128)}, u32[]{:S(2)}) copy-start(f32[2,16,8,8,2]{3,4,0,2,1:T(2,128)} %get-tuple-element.20) | copy-start | bytes 49156
  61.5 8.0 %slice-start.1 = ((s8[5242880]{0:T(1024)(128)(4,1)}), s8[1048576]{0:T(1024)(128)(4,1)S(1)}, s32[]{:S(2)}) async-start(s8[5242880]{0:T(1024)(128)(4,1)} %bitcast.95), calls=%async_computation.6 | async-start | bytes 2097152
  240.3 26.9 %copy-start.1 = (bf16[2880,64]{0,1:T(8,128)(2,1)S(1)}, bf16[2880,64]{0,1:T(8,128)(2,1)}, u32[]{:S(2)}) copy-start(bf16[2880,64]{0,1:T(8,128)(2,1)} %param.18) | copy-start | bytes 1105924
  244.0 22.4 %copy-start.3 = (bf16[2,16,2880]{2,1,0:T(8,128)(2,1)S(1)}, bf16[2,16,2880]{2,1,0:T(8,128)(2,1)}, u32[]{:S(2)}) copy-start(bf16[2,16,2880]{2,1,0:T(8,128)(2,1)} %param.16) | copy-start | bytes 552964
Sparse Core Ops, SparseCore 0:
  14.4 70.9 all-gather.2
